TPU v7x, 32 devices: a whole 2x2x4 slice. The times are simulated.
32 devices in a mesh: mass: 8 (over y, x, core), scen: 4 (over z).
Axes of the slice: x: 2, y: 2, z: 4, core: 2. Of those that a mesh axis runs over, the one named last changes fastest.
Arguments:
- density: float32 [4, 524288], P('scen', 'mass'), may hold values from 0.01 to 68
- cotangent: float32 [4, 524288], P('scen', 'mass'), may hold values from -16.5 to 17.5
- rate: float32 [524288], P('mass'), may hold values from 0.2 to 2
Outputs:
- tendency: float32 [4, 524288], P('scen', 'mass')
- adjoint_density: float32 [4, 524288], P('scen', 'mass')
- rate_gradient: float32 [524288], P('mass')
All inputs are finite; a program needn't handle non-finite values.
Results may differ from a plain program's by a relative error of at most 0.00008.
Values sent between devices are 32-bit elements; how exact they have to be, the bound alone decides.
No kernel may reach another device: no remote copies, remote signals or barrier semaphores. Data moves between devices by JAX's collectives and lax.ppermute only.
A program may use at most 64 MiB of HBM per device.

v0:
```python
import math

import jax
import numpy as np
import jax.numpy as jnp
from jax import lax
from jax.sharding import PartitionSpec as P

C1 = 32
C2 = 128


aggregation_coef = 12.0


def from_behind(value, axis, steps):
    count = lax.axis_size(axis)
    first, last = (max(0, -steps), min(count, count - steps))
    return lax.ppermute(value, axis, [(source, source + steps) for source in range(first, last)])


def phases(left, right, total):
    outer = left[:, None] * right[None, :] % total
    angle = outer.astype(jnp.float32) * (2.0 * math.pi / total)
    return (jnp.cos(angle), jnp.sin(angle))


def counting(count):
    return lax.iota(jnp.int32, count)


def complex_dot(form, table, values):
    table_re, table_im = table
    val_re, val_im = values
    high = lax.Precision.HIGHEST
    real_out = jnp.einsum(form, table_re, val_re, precision=high) - jnp.einsum(
        form, table_im, val_im, precision=high
    )
    imag_out = jnp.einsum(form, table_re, val_im, precision=high) + jnp.einsum(
        form, table_im, val_re, precision=high
    )
    return (real_out, imag_out)


def complex_mul(left, right):
    return (left[0] * right[0] - left[1] * right[1], left[0] * right[1] + left[1] * right[0])


def column_forward(values):
    lead = values[0].shape[:-1]
    shaped = (values[0].reshape(lead + (C1, C2)), values[1].reshape(lead + (C1, C2)))
    cos_one, sin_one = phases(counting(C1), counting(C1), C1)
    step_one = complex_dot("pa,...ab->...pb", (cos_one, -sin_one), shaped)
    tw_cos, tw_sin = phases(counting(C1), counting(C2), C1 * C2)
    turned = complex_mul(step_one, (tw_cos, -tw_sin))
    cos_two, sin_two = phases(counting(C2), counting(C2), C2)
    return complex_dot("qb,...pb->...pq", (cos_two, -sin_two), turned)


def column_inverse(values):
    lead = values[0].shape[:-2]
    cos_two, sin_two = phases(counting(C2), counting(C2), C2)
    step_one = complex_dot("qb,...pq->...pb", (cos_two, sin_two), values)
    tw_cos, tw_sin = phases(counting(C1), counting(C2), C1 * C2)
    turned = complex_mul(step_one, (tw_cos, tw_sin))
    cos_one, sin_one = phases(counting(C1), counting(C1), C1)
    result = complex_dot("pa,...pb->...ab", (cos_one, sin_one), turned)
    return (result[0].reshape(lead + (C1 * C2,)), result[1].reshape(lead + (C1 * C2,)))


def exchange(value):
    return lax.all_to_all(value, "mass", 0, 0, tiled=True)


def shards(density, cotangent, rate):
    high = lax.Precision.HIGHEST
    scen_dev, bin_dev = density.shape
    arrays = 2 * scen_dev
    parts = lax.axis_size("mass")
    place = lax.axis_index("mass")
    width = C1 * C2
    rows = bin_dev // width
    half_rows = rows * parts
    full_rows = 2 * half_rows
    cols = width // parts
    block = full_rows // parts
    nbin = half_rows * width
    nfft = 2 * nbin
    beta = aggregation_coef / nbin
    offset = place * bin_dev
    mass = ((offset + counting(bin_dev)).astype(jnp.float32) + 0.5) / nbin
    weighted = mass[None, :] * density
    partial = jnp.concatenate([jnp.sum(weighted, axis=1), jnp.sum(cotangent * weighted, axis=1)])
    tile = jnp.zeros((8, cols), jnp.float32).at[0, :arrays].set(partial)
    stacked = jnp.concatenate([weighted, cotangent], axis=0).reshape(arrays, rows, parts, cols)
    outgoing = stacked.transpose(2, 0, 1, 3).reshape(parts, arrays * rows, cols)
    outgoing = jnp.concatenate([outgoing, jnp.broadcast_to(tile, (parts, 8, cols))], axis=1)
    incoming_rows = exchange(outgoing)
    moments = jnp.sum(incoming_rows[:, arrays * rows, :arrays], axis=0)
    first, cross = moments[:scen_dev], moments[scen_dev:]
    spread = incoming_rows[:, : arrays * rows].reshape(parts, arrays, rows, cols)
    spread = spread.transpose(1, 0, 2, 3).reshape(arrays, half_rows, cols)
    half = block // 2
    pos = counting(block)
    own_rows = jnp.where(pos < half, half * place + pos, (full_rows - half * place - (pos - half)) % full_rows)
    own_rows = jnp.where((place == 0) & (pos == half), full_rows // 2, own_rows)
    table = np.arange(block)[None, :]
    order = np.where(table < half, half * np.arange(parts)[:, None] + table,
                     (full_rows - half * np.arange(parts)[:, None] - (table - half)) % full_rows)
    order[0, half] = full_rows // 2
    order = jnp.asarray(order.reshape(-1), jnp.int32)
    row_cos, row_sin = phases(order, counting(half_rows), full_rows)
    forward_rows = jnp.stack([jnp.stack([row_cos, row_sin], axis=1), jnp.stack([-row_sin, row_cos], axis=1)])
    packed = spread.reshape(2, scen_dev, half_rows, cols)
    freq = jnp.einsum("okir,isrw->oskw", forward_rows, packed, precision=high)
    column_index = place * cols + counting(cols)
    tw_cos, tw_sin = phases(order, column_index, nfft)
    twisted = jnp.stack(complex_mul((freq[0], freq[1]), (tw_cos, -tw_sin)))
    twisted = twisted.reshape(2, scen_dev, parts, block, cols).transpose(2, 0, 1, 3, 4)
    moved = exchange(twisted).transpose(1, 2, 3, 0, 4).reshape(2, scen_dev, block, width)
    spec_re, spec_im = column_forward((moved[0], moved[1]))
    flip_re = jnp.roll(spec_re[:, :, ::-1, ::-1], half, axis=1)
    flip_im = jnp.roll(spec_im[:, :, ::-1, ::-1], half, axis=1)
    self_re = spec_re[:, half, ::-1, ::-1]
    self_im = spec_im[:, half, ::-1, ::-1]
    zero_re = jnp.roll(spec_re[:, 0, ::-1, ::-1], 1, axis=1)
    zero_im = jnp.roll(spec_im[:, 0, ::-1, ::-1], 1, axis=1)
    zero_re = zero_re.at[:, 0, :].set(jnp.roll(zero_re[:, 0, :], 1, axis=1))
    zero_im = zero_im.at[:, 0, :].set(jnp.roll(zero_im[:, 0, :], 1, axis=1))
    lead = place == 0
    mir_re = flip_re.at[:, 0].set(jnp.where(lead, zero_re, flip_re[:, 0]))
    mir_re = mir_re.at[:, half].set(jnp.where(lead, self_re, flip_re[:, half]))
    mir_im = flip_im.at[:, 0].set(jnp.where(lead, zero_im, flip_im[:, 0]))
    mir_im = mir_im.at[:, half].set(jnp.where(lead, self_im, flip_im[:, half]))
    dist_spec = (0.5 * (spec_re + mir_re), 0.5 * (spec_im - mir_im))
    cot_spec = (0.5 * (spec_im + mir_im), 0.5 * (mir_re - spec_re))
    birth_spec = complex_mul(dist_spec, dist_spec)
    adjoint_spec = complex_mul(cot_spec, (dist_spec[0], -dist_spec[1]))
    joined = (birth_spec[0] - adjoint_spec[1], birth_spec[1] + adjoint_spec[0])
    inverted = column_inverse(joined)
    back_cos, back_sin = phases(own_rows, counting(width), nfft)
    untwisted = jnp.stack(complex_mul(inverted, (back_cos, back_sin)))
    untwisted = untwisted.reshape(2, scen_dev, block, parts, cols).transpose(3, 0, 1, 2, 4)
    returned = exchange(untwisted).transpose(1, 2, 0, 3, 4).reshape(2, scen_dev, full_rows, cols)
    inv_cos, inv_sin = phases(counting(half_rows), order, full_rows)
    inverse_rows = jnp.stack([jnp.stack([inv_cos, -inv_sin], axis=1), jnp.stack([inv_sin, inv_cos], axis=1)])
    real_part = jnp.einsum("orik,iskw->osrw", inverse_rows, returned, precision=high)
    real_part = real_part.reshape(arrays, half_rows, cols)
    real_part = real_part.reshape(arrays, parts, rows, cols).transpose(1, 0, 2, 3)
    gathered = exchange(real_part).transpose(1, 2, 0, 3).reshape(arrays, bin_dev) / nfft
    birth = gathered[:scen_dev]
    corr = gathered[scen_dev:]
    flux = rate[None, :] * weighted
    incoming = from_behind(flux[:, -1:], "mass", 1)
    inflow = jnp.concatenate([incoming, flux[:, :-1]], axis=1)
    tendency = 0.5 * beta * birth - beta * first[:, None] * weighted - flux + inflow
    arriving = from_behind(cotangent[:, :1], "mass", -1)
    following = jnp.concatenate([cotangent[:, 1:], arriving], axis=1)
    adjoint = mass[None, :] * (
        beta * corr
        - beta * first[:, None] * cotangent
        - beta * cross[:, None]
        - rate[None, :] * cotangent
        + rate[None, :] * following
    )
    local_grad = jnp.sum(weighted * (following - cotangent), axis=0)
    rate_gradient = lax.psum(local_grad, "scen")
    return (tendency, adjoint, rate_gradient)


def solution(mesh):
    in_specs = (P("scen", "mass"), P("scen", "mass"), P("mass"))
    out_specs = (P("scen", "mass"), P("scen", "mass"), P("mass"))
    return jax.shard_map(shards, mesh=mesh, in_specs=in_specs, out_specs=out_specs, check_vma=False)
```

profile of v0, /device:TPU:0, one launch (start us, length us, event | category | flops | bytes accessed | tf_op | source)
XLA Modules:
  0.0 160.9 jit_solution(11536800356188355654)
XLA Ops:
  7.2 1.2 slice.325
  8.3 1.3 collective-permute-start.1
  9.6 1.6 slice.324
  11.5 2.1 %fusion.31 = (f32[1,65536]{1,0:T(1,128)}, f32[1,65536]{1,0:T(1,128)S(1)}) fusion(f32[1,65536]{1,0:T(1,128)S(1)} %copy-done, f32[1,1]{1,0:T(1,128)} %collective-permute-done.1, f32[1,65535]{1,0:T(1,128)S(1)} %slice.324, f32[1,65536]{1,0:T(1,128)S(1)} %copy-done.6, s32[]{:T(128)S(6)} %mul.713), kind=kLoop, calls=%fused_computation.83 | loop fusion | flops 524288 | bytes 1310724 | tf_op jit(solution)/shard_map/mul | solution.py:166
  13.5 1.2 fusion.186
  15.7 1.4 maximum_bitcast_fusion.6
  18.0 6.5 %all-to-all-start = ((f32[8,40,512]{2,1,0:T(8,128)}), f32[8,40,512]{2,1,0:T(8,128)S(1)}, u32[]{:S(2)}, u32[]{:S(2)}) async-start(f32[8,40,512]{2,1,0:T(8,128)} %pad_maximum_fusion), calls=%async_computation | async-start | bytes 1310720 | tf_op jit(solution)/shard_map/all_to_all | solution.py:72
  25.8 9.8 %all-to-all-done = f32[8,40,512]{2,1,0:T(8,128)S(1)} async-done(((f32[8,40,512]{2,1,0:T(8,128)}), f32[8,40,512]{2,1,0:T(8,128)S(1)}, u32[]{:S(2)}, u32[]{:S(2)}) %all-to-all-start) | async-done | bytes 655392 | tf_op jit(solution)/shard_map/all_to_all | solution.py:72
  36.8 2.4 %multiply_subtract_fusion.3 = (f32[1,1,256,512]{3,2,0,1:T(8,128)S(1)}, f32[1,1,256,512]{3,2,0,1:T(8,128)S(1)}) fusion(f32[2,1,256,512]{3,2,0,1:T(8,128)S(1)} %convolution_bitcast_fusion, s32[512]{0:T(512)S(1)} %iota_add_fusion, s32[256]{0:T(256)S(1)} %copy-done.13), kind=kLoop, calls=%fused_computation.72 | loop fusion | flops 2752512 | bytes 2100224 | tf_op jit(solution)/shard_map/sub | solution.py:46
  40.2 3.7 %all-to-all-start.1 = ((f32[8,2,1,32,512]{4,3,2,1,0:T(8,128)}), f32[8,2,1,32,512]{4,3,2,1,0:T(8,128)S(1)}, u32[]{:S(2)}, u32[]{:S(2)}) async-start(f32[8,2,1,32,512]{4,3,2,1,0:T(8,128)} %maximum_bitcast_fusion), calls=%async_computation.1 | async-start | bytes 2097152 | tf_op jit(solution)/shard_map/all_to_all | solution.py:72
  46.5 12.6 %all-to-all-done.1 = f32[8,2,1,32,512]{4,3,2,1,0:T(8,128)S(1)} async-done(((f32[8,2,1,32,512]{4,3,2,1,0:T(8,128)}), f32[8,2,1,32,512]{4,3,2,1,0:T(8,128)S(1)}, u32[]{:S(2)}, u32[]{:S(2)}) %all-to-all-start.1) | async-done | bytes 1048608 | tf_op jit(solution)/shard_map/all_to_all | solution.py:72
  68.5 1.4 slice.316
  69.9 1.4 rev.5
  71.3 1.3 slice_bitcast_fusion
  73.7 1.4 slice.305
  75.1 1.4 rev.4
  76.5 1.3 slice_bitcast_fusion.1
  83.3 1.3 scatter.25
  97.8 1.5 fusion
  99.3 1.1 reshape.1023
  100.5 2.2 %fusion.1 = f32[1,32,32,128]{3,2,1,0:T(8,128)} fusion(f32[32,128,32]{1,2,0:T(8,128)S(1)} %fusion.35, f32[32,32,128]{2,1,0:T(8,128)S(1)} %convolution_add_fusion.1, f32[32,32,128]{2,1,0:T(8,128)S(1)} %convolution_subtract_fusion.1, f32[32,128]{1,0:T(8,128)} %fusion.106, f32[32,128]{1,0:T(8,128)S(1)} %get-tuple-element.127), kind=kOutput, calls=%fused_computation.4 | convolution fusion | flops 50870272 | bytes 2129920 | tf_op jit(solution)/shard_map/pa,...pb->...ab/dot_general | solution.py:36
  102.7 1.1 reshape.1022
  103.8 3.1 %multiply_subtract_fusion = (f32[1,1,32,8,512]{4,2,1,0,3:T(8,128)S(1)}, f32[1,1,32,8,512]{4,2,1,0,3:T(8,128)S(1)}) fusion(f32[1,1,32,8,512]{4,3,2,1,0:T(8,128)S(1)} %reshape.1023, f32[1,1,32,8,512]{4,3,2,1,0:T(8,128)S(1)} %reshape.1022, s32[8,512]{1,0:T(8,128)S(1)} %copy-done.12, s32[32]{0:T(128)} %and_select_fusion.1), kind=kLoop, calls=%fused_computation.61 | loop fusion | flops 2621440 | bytes 2113664 | tf_op jit(solution)/shard_map/sub | solution.py:46
  108.0 3.7 %all-to-all-start.2 = ((f32[8,2,1,32,512]{4,3,2,1,0:T(8,128)}), f32[8,2,1,32,512]{4,3,2,1,0:T(8,128)S(1)}, u32[]{:S(2)}, u32[]{:S(2)}) async-start(f32[8,2,1,32,512]{4,3,2,1,0:T(8,128)} %maximum_bitcast_fusion.1), calls=%async_computation.2 | async-start | bytes 2097152 | tf_op jit(solution)/shard_map/all_to_all | solution.py:72
  112.4 14.6 %all-to-all-done.2 = f32[8,2,1,32,512]{4,3,2,1,0:T(8,128)S(1)} async-done(((f32[8,2,1,32,512]{4,3,2,1,0:T(8,128)}), f32[8,2,1,32,512]{4,3,2,1,0:T(8,128)S(1)}, u32[]{:S(2)}, u32[]{:S(2)}) %all-to-all-start.2) | async-done | bytes 1048608 | tf_op jit(solution)/shard_map/all_to_all | solution.py:72
  129.1 3.9 %all-to-all-start.3 = ((f32[8,2,16,512]{3,2,1,0:T(8,128)}), f32[8,2,16,512]{3,2,1,0:T(8,128)S(1)}, u32[]{:S(2)}, u32[]{:S(2)}) async-start(f32[8,2,16,512]{3,2,1,0:T(8,128)} %bitcast.191), calls=%async_computation.3 | async-start | bytes 1048576 | tf_op jit(solution)/shard_map/all_to_all | solution.py:72
  135.6 6.8 %all-to-all-done.3 = f32[8,2,16,512]{3,2,1,0:T(8,128)S(1)} async-done(((f32[8,2,16,512]{3,2,1,0:T(8,128)}), f32[8,2,16,512]{3,2,1,0:T(8,128)S(1)}, u32[]{:S(2)}, u32[]{:S(2)}) %all-to-all-start.3) | async-done | bytes 524320 | tf_op jit(solution)/shard_map/all_to_all | solution.py:72
  142.9 1.6 add_multiply_fusion.2
  145.1 1.8 %collective-permute-start = (f32[1,1]{1,0:T(1,128)}, f32[1,1]{1,0:T(1,128)}, u32[]{:S(2)}, u32[]{:S(2)}) collective-permute-start(f32[1,1]{1,0:T(1,128)} %slice.345), channel_id=1, source_target_pairs={{0,4},{4,8},{8,12},{12,16},{16,20},{20,24},{24,28},{1,5},{5,9},{9,... | collective-permute-start | bytes 20 | tf_op jit(solution)/shard_map/ppermute | solution.py:19
  147.4 1.9 %maximum_add_fusion = f32[1,65536]{1,0:T(1,128)} fusion(f32[1,65535]{1,0:T(1,128)S(1)} %bitcast.203, f32[1,1]{1,0:T(1,128)} %collective-permute-done, f32[1,65536]{1,0:T(1,128)S(1)} %get-tuple-element.110, f32[1,65536]{1,0:T(1,128)S(1)} %bitcast.215, f32[1,65536]{1,0:T(1,128)S(1)} %get-tuple-element.90, f32[]{:T(128)} %bitcast.71), kind=kLoop, calls=%fused_computation.80 | loop fusion | flops 327680 | bytes 1310724 | tf_op jit(solution)/shard_map/add | solution.py:156
  149.3 3.1 %all-reduce.3.cloned.1.call-done = f32[65536]{0:T(1024)} async-done(((f32[65536]{0:T(1024)}), f32[65536]{0:T(1024)}) %all-reduce.3.cloned.1.call-update) | async-done | bytes 262160 | tf_op jit(solution)/shard_map/psum | solution.py:167
  152.4 1.7 %copy.93 = f32[65536]{0:T(1024)} copy(f32[65536]{0:T(1024)} %all-reduce.3.cloned.1.call-done) | data formatting | bytes 524288
  (120 shorter events, 43.9 us)
Async XLA Ops:
  8.3 3.1 %collective-permute-start.1 = (f32[1,1]{1,0:T(1,128)}, f32[1,1]{1,0:T(1,128)}, u32[]{:S(2)}, u32[]{:S(2)}) collective-permute-start(f32[1,1]{1,0:T(1,128)} %slice.325), channel_id=1, source_target_pairs={{4,0},{8,4},{12,8},{16,12},{20,16},{24,20},{28,24},{5,1},{9,5},{13... | collective-permute-start | bytes 20 | tf_op jit(solution)/shard_map/ppermute | solution.py:19
  9.6 1.8 %copy-start = (f32[1,65536]{1,0:T(1,128)S(1)}, f32[1,65536]{1,0:T(1,128)}, u32[]{:S(2)}) copy-start(f32[1,65536]{1,0:T(1,128)} %param.19) | copy-start | bytes 786436
  9.6 1.8 %copy-start.6 = (f32[1,65536]{1,0:T(1,128)S(1)}, f32[1,65536]{1,0:T(1,128)}, u32[]{:S(2)}) copy-start(f32[1,65536]{1,0:T(1,128)} %param.18) | copy-start | bytes 786436
  18.0 17.7 %all-to-all-start = ((f32[8,40,512]{2,1,0:T(8,128)}), f32[8,40,512]{2,1,0:T(8,128)S(1)}, u32[]{:S(2)}, u32[]{:S(2)}) async-start(f32[8,40,512]{2,1,0:T(8,128)} %pad_maximum_fusion), calls=%async_computation | async-start | bytes 1310720 | tf_op jit(solution)/shard_map/all_to_all | solution.py:72
  24.5 0.7 copy-start.13
  40.2 18.9 %all-to-all-start.1 = ((f32[8,2,1,32,512]{4,3,2,1,0:T(8,128)}), f32[8,2,1,32,512]{4,3,2,1,0:T(8,128)S(1)}, u32[]{:S(2)}, u32[]{:S(2)}) async-start(f32[8,2,1,32,512]{4,3,2,1,0:T(8,128)} %maximum_bitcast_fusion), calls=%async_computation.1 | async-start | bytes 2097152 | tf_op jit(solution)/shard_map/all_to_all | solution.py:72
  60.4 1.0 copy-start.1
  63.2 0.7 copy-start.5
  72.6 0.5 copy-start.17
  77.7 0.6 copy-start.19
  79.8 2.2 %copy-start.10 = (f32[1,1,32,128]{3,2,1,0:T(8,128)S(1)}, f32[1,1,32,128]{3,2,1,0:T(8,128)}, u32[]{:S(2)}) copy-start(f32[1,1,32,128]{3,2,1,0:T(8,128)} %rev.4) | copy-start | bytes 49156
  80.6 0.7 copy-start.20
  82.0 0.7 copy-start.16
  84.6 1.1 copy-start.8
  85.6 0.7 copy-start.11
  87.2 3.7 %copy-start.2 = (f32[1,16,32,128]{3,2,1,0:T(8,128)S(1)}, f32[1,16,32,128]{3,2,1,0:T(8,128)}, u32[]{:S(2)}) copy-start(f32[1,16,32,128]{3,2,1,0:T(8,128)} %slice.307) | copy-start | bytes 786436
  88.1 0.6 copy-start.18
  89.3 0.7 copy-start.15
  91.0 1.0 copy-start.7
  92.0 0.7 copy-start.9
  95.6 0.8 copy-start.4
  102.7 1.2 copy-start.12
  108.0 3.7 %copy-start.14 = (s32[256]{0:T(256)S(1)}, s32[256]{0:T(256)}, u32[]{:S(2)}) copy-start(s32[256]{0:T(256)} %constant.319.clone) | copy-start | bytes 3076
  108.0 19.0 %all-to-all-start.2 = ((f32[8,2,1,32,512]{4,3,2,1,0:T(8,128)}), f32[8,2,1,32,512]{4,3,2,1,0:T(8,128)S(1)}, u32[]{:S(2)}, u32[]{:S(2)}) async-start(f32[8,2,1,32,512]{4,3,2,1,0:T(8,128)} %maximum_bitcast_fusion.1), calls=%async_computation.2 | async-start | bytes 2097152 | tf_op jit(solution)/shard_map/all_to_all | solution.py:72
  111.7 40.7 %all-reduce.3.cloned.1.call-start = ((), (), s32[]{:S(2)}) async-start(), calls=%async_computation.4 | async-start | bytes 524288 | tf_op jit(solution)/shard_map/psum | solution.py:167
  129.1 3.9 %copy-start.3 = (f32[65536]{0:T(1024)S(1)}, f32[65536]{0:T(1024)}, u32[]{:S(2)}) copy-start(f32[65536]{0:T(1024)} %param.20) | copy-start | bytes 786436
  129.1 13.3 %all-to-all-start.3 = ((f32[8,2,16,512]{3,2,1,0:T(8,128)}), f32[8,2,16,512]{3,2,1,0:T(8,128)S(1)}, u32[]{:S(2)}, u32[]{:S(2)}) async-start(f32[8,2,16,512]{3,2,1,0:T(8,128)} %bitcast.191), calls=%async_computation.3 | async-start | bytes 1048576 | tf_op jit(solution)/shard_map/all_to_all | solution.py:72
  145.1 2.4 %collective-permute-start = (f32[1,1]{1,0:T(1,128)}, f32[1,1]{1,0:T(1,128)}, u32[]{:S(2)}, u32[]{:S(2)}) collective-permute-start(f32[1,1]{1,0:T(1,128)} %slice.345), channel_id=1, source_target_pairs={{0,4},{4,8},{8,12},{12,16},{16,20},{20,24},{24,28},{1,5},{5,9},{9,... | collective-permute-start | bytes 20 | tf_op jit(solution)/shard_map/ppermute | solution.py:19
Sparse Core Ops, SparseCore 0:
  115.4 36.9 all-reduce.2
where the time goes:
time: 162 us; the launch traced here: 161 us
  waiting for transfers between devices  47.4 us (29%)
  local copies, waits for them, and re-layouts  32.7 us (20%)
  other arithmetic  27.6 us (17%)
  starting transfers between devices  20.9 us (13%)
  matrix products  16.5 us (10%)
  between operations  15.8 us (10%)
    all_to_all x4, waiting for transfers between devices, exchange(): return lax.all_to_all(value, 'mass', 0, 0, tiled=True)  43.8 us
    all_to_all x4, starting transfers between devices, exchange(): return lax.all_to_all(value, 'mass', 0, 0, tiled=True)  17.8 us
    unnamed x46, local copies, waits for them, and re-layouts  7.8 us
    sub x2, other arithmetic, complex_mul(): left[0] * right[0] - left[1] * right[1]  5.44 us
    dot_general x4, matrix products, complex_dot(): jnp.einsum(form, table_im, val_im, precision=high)  4.54 us
    dot_general x4, matrix products, complex_dot(): jnp.einsum(form, table_im, val_re, precision=high)  3.82 us
  transfers between devices with their start and end apart: 7, of which 7 were waited for; matrix products, arithmetic and copies ran while one was open for 8% of the time, Pallas kernels for 0%

commit v1 on v0

--- a/solution.py
+++ b/solution.py
@@ -118,22 +118,21 @@
     twisted = jnp.stack(complex_mul((freq[0], freq[1]), (tw_cos, -tw_sin)))
     twisted = twisted.reshape(2, scen_dev, parts, block, cols).transpose(2, 0, 1, 3, 4)
     moved = exchange(twisted).transpose(1, 2, 3, 0, 4).reshape(2, scen_dev, block, width)
-    spec_re, spec_im = column_forward((moved[0], moved[1]))
-    flip_re = jnp.roll(spec_re[:, :, ::-1, ::-1], half, axis=1)
-    flip_im = jnp.roll(spec_im[:, :, ::-1, ::-1], half, axis=1)
-    self_re = spec_re[:, half, ::-1, ::-1]
-    self_im = spec_im[:, half, ::-1, ::-1]
-    zero_re = jnp.roll(spec_re[:, 0, ::-1, ::-1], 1, axis=1)
-    zero_im = jnp.roll(spec_im[:, 0, ::-1, ::-1], 1, axis=1)
-    zero_re = zero_re.at[:, 0, :].set(jnp.roll(zero_re[:, 0, :], 1, axis=1))
-    zero_im = zero_im.at[:, 0, :].set(jnp.roll(zero_im[:, 0, :], 1, axis=1))
     lead = place == 0
-    mir_re = flip_re.at[:, 0].set(jnp.where(lead, zero_re, flip_re[:, 0]))
-    mir_re = mir_re.at[:, half].set(jnp.where(lead, self_re, flip_re[:, half]))
-    mir_im = flip_im.at[:, 0].set(jnp.where(lead, zero_im, flip_im[:, 0]))
-    mir_im = mir_im.at[:, half].set(jnp.where(lead, self_im, flip_im[:, half]))
-    dist_spec = (0.5 * (spec_re + mir_re), 0.5 * (spec_im - mir_im))
-    cot_spec = (0.5 * (spec_im + mir_im), 0.5 * (mir_re - spec_re))
+    keep = (lead & ((pos == 0) | (pos == half)))[:, None]
+    partner_re = jnp.where(keep, moved[0], jnp.roll(moved[0], half, axis=1))
+    partner_im = jnp.where(keep, moved[1], jnp.roll(moved[1], half, axis=1))
+    shift_cos, shift_sin = phases(jnp.ones((1,), jnp.int32), counting(width), width)
+    plain = (lead & (pos == 0))[:, None]
+    shift_cos = jnp.where(plain, 1.0, shift_cos)
+    shift_sin = jnp.where(plain, 0.0, shift_sin)
+    mirror_re = partner_re * shift_cos - partner_im * shift_sin
+    mirror_im = -partner_re * shift_sin - partner_im * shift_cos
+    split_re = jnp.concatenate([0.5 * (moved[0] + mirror_re), 0.5 * (moved[1] - mirror_im)], axis=0)
+    split_im = jnp.concatenate([0.5 * (moved[1] + mirror_im), 0.5 * (mirror_re - moved[0])], axis=0)
+    spec_re, spec_im = column_forward((split_re, split_im))
+    dist_spec = (spec_re[:scen_dev], spec_im[:scen_dev])
+    cot_spec = (spec_re[scen_dev:], spec_im[scen_dev:])
     birth_spec = complex_mul(dist_spec, dist_spec)
     adjoint_spec = complex_mul(cot_spec, (dist_spec[0], -dist_spec[1]))
     joined = (birth_spec[0] - adjoint_spec[1], birth_spec[1] + adjoint_spec[0])

time: 162 us -> 142 us (0.88)
  local copies, waits for them, and re-layouts: 32.7 us -> 14.6 us
  other arithmetic: 27.6 us -> 23.5 us
  matrix products: 16.5 us -> 20 us
    slice x15 -> x3, local copies, waits for them, and re-layouts: 10.2 us -> 0.7 us  [the longest x2 0.4 us: shards(): partner_im = jnp.where(keep, moved[1], jnp.roll(moved[1], half, axis=1))]
    concatenate x4 -> x0, other arithmetic: 3.39 us -> none  [the longest x1 1.08 us: shards(): flip_re = jnp.roll(spec_re[:, :, ::-1, ::-1], half, axis=1)]
    unnamed x46 -> x36, local copies, waits for them, and re-layouts: 7.8 us -> 5 us
    rev x2 -> x0, local copies, waits for them, and re-layouts: 2.77 us -> none  [the longest x1 1.39 us: shards(): zero_re = jnp.roll(spec_re[:, 0, ::-1, ::-1], 1, axis=1)]
  transfers between devices with their start and end apart: 7 -> 7, of which waited for: 7 -> 6; matrix products, arithmetic and copies ran while one was open for 8% -> 11% of each run, Pallas kernels for 0% -> 0%
where the time goes in v1:
time: 142 us; the launch traced here: 141 us
  waiting for transfers between devices  45.8 us (32%)
  other arithmetic  23.5 us (17%)
  starting transfers between devices  21 us (15%)
  matrix products  20 us (14%)
  between operations  15.9 us (11%)
  local copies, waits for them, and re-layouts  14.6 us (10%)
    all_to_all x4, waiting for transfers between devices, exchange(): return lax.all_to_all(value, 'mass', 0, 0, tiled=True)  42.5 us
    all_to_all x4, starting transfers between devices, exchange(): return lax.all_to_all(value, 'mass', 0, 0, tiled=True)  17.8 us
    dot_general x4, matrix products, complex_dot(): jnp.einsum(form, table_im, val_im, precision=high)  5.37 us
    unnamed x36, local copies, waits for them, and re-layouts  5 us
    sub x2, other arithmetic, complex_mul(): left[0] * right[0] - left[1] * right[1]  4.8 us
    dot_general x4, matrix products, complex_dot(): jnp.einsum(form, table_im, val_re, precision=high)  4.65 us
    dot_general x4, matrix products, complex_dot(): jnp.einsum(form, table_re, val_re, precision=high)  4.06 us
    dot_general x4, matrix products, complex_dot(): jnp.einsum(form, table_re, val_im, precision=high)  3.84 us
  transfers between devices with their start and end apart: 7, of which 6 were waited for; matrix products, arithmetic and copies ran while one was open for 11% of the time, Pallas kernels for 0%

profile of v1, /device:TPU:0, one launch (start us, length us, event | category | flops | bytes accessed | tf_op | source)
XLA Modules:
  0.0 140.9 jit_solution(18100774099341090902)
XLA Ops:
  7.2 1.2 slice.115
  8.3 1.3 collective-permute-start.1
  9.6 1.6 %slice.114 = f32[1,65535]{1,0:T(1,128)S(1)} slice(f32[1,65536]{1,0:T(1,128)} %param.7), slice={[0:1], [1:65536]} | slice | bytes 524280 | tf_op jit(solution)/shard_map/slice | solution.py:157
  11.5 2.1 %fusion.29 = (f32[1,65536]{1,0:T(1,128)}, f32[1,65536]{1,0:T(1,128)S(1)}) fusion(f32[1,65536]{1,0:T(1,128)S(1)} %copy-done, f32[1,1]{1,0:T(1,128)} %collective-permute-done.1, f32[1,65535]{1,0:T(1,128)S(1)} %slice.114, f32[1,65536]{1,0:T(1,128)S(1)} %copy-done.4, s32[]{:T(128)S(6)} %mul.831), kind=kLoop, calls=%fused_computation.91 | loop fusion | flops 524288 | bytes 1310724 | tf_op jit(solution)/shard_map/mul | solution.py:165
  13.6 1.2 fusion.193
  15.7 1.4 maximum_bitcast_fusion.6
  18.0 6.5 %all-to-all-start = ((f32[8,40,512]{2,1,0:T(8,128)}), f32[8,40,512]{2,1,0:T(8,128)S(1)}, u32[]{:S(2)}, u32[]{:S(2)}) async-start(f32[8,40,512]{2,1,0:T(8,128)} %pad_maximum_fusion.6), calls=%async_computation | async-start | bytes 1310720 | tf_op jit(solution)/shard_map/all_to_all | solution.py:72
  25.8 9.8 %all-to-all-done = f32[8,40,512]{2,1,0:T(8,128)S(1)} async-done(((f32[8,40,512]{2,1,0:T(8,128)}), f32[8,40,512]{2,1,0:T(8,128)S(1)}, u32[]{:S(2)}, u32[]{:S(2)}) %all-to-all-start) | async-done | bytes 655392 | tf_op jit(solution)/shard_map/all_to_all | solution.py:72
  36.8 2.4 %multiply_subtract_fusion.3 = (f32[1,1,256,512]{3,2,0,1:T(8,128)S(1)}, f32[1,1,256,512]{3,2,0,1:T(8,128)S(1)}) fusion(f32[2,1,256,512]{3,2,0,1:T(8,128)S(1)} %convolution_bitcast_fusion, s32[512]{0:T(512)S(1)} %iota_add_fusion, s32[256]{0:T(256)S(1)} %copy-done.8), kind=kLoop, calls=%fused_computation.74 | loop fusion | flops 2752512 | bytes 2100224 | tf_op jit(solution)/shard_map/sub | solution.py:46
  40.3 3.7 %all-to-all-start.1 = ((f32[8,2,1,32,512]{4,3,2,1,0:T(8,128)}), f32[8,2,1,32,512]{4,3,2,1,0:T(8,128)S(1)}, u32[]{:S(2)}, u32[]{:S(2)}) async-start(f32[8,2,1,32,512]{4,3,2,1,0:T(8,128)} %maximum_bitcast_fusion), calls=%async_computation.1 | async-start | bytes 2097152 | tf_op jit(solution)/shard_map/all_to_all | solution.py:72
  47.9 11.3 %all-to-all-done.1 = f32[8,2,1,32,512]{4,3,2,1,0:T(8,128)S(1)} async-done(((f32[8,2,1,32,512]{4,3,2,1,0:T(8,128)}), f32[8,2,1,32,512]{4,3,2,1,0:T(8,128)S(1)}, u32[]{:S(2)}, u32[]{:S(2)}) %all-to-all-start.1) | async-done | bytes 1048608 | tf_op jit(solution)/shard_map/all_to_all | solution.py:72
  64.9 1.1 fusion.4
  66.0 1.1 fusion.1
  67.2 1.1 fusion
  68.3 1.2 fusion.28
  69.5 1.2 fusion.27
  70.7 1.2 convolution_add_fusion
  72.0 1.2 convolution_subtract_fusion
  78.4 1.5 %fusion.2 = f32[1,32,32,128]{3,2,1,0:T(8,128)} fusion(f32[32,128,32]{1,2,0:T(8,128)S(1)} %fusion.34, f32[32,32,128]{2,1,0:T(8,128)S(1)} %convolution_add_fusion.3, f32[32,32,128]{2,1,0:T(8,128)S(1)} %convolution_subtract_fusion.3, f32[32,128]{1,0:T(8,128)S(1)} %copy-done.2, f32[32,128]{1,0:T(8,128)S(1)} %get-tuple-element.54), kind=kOutput, calls=%fused_computation.8 | convolution fusion | flops 50870272 | bytes 2129920 | tf_op jit(solution)/shard_map/pa,...pb->...ab/dot_general | solution.py:39
  79.9 1.1 reshape.1346
  81.1 2.2 %fusion.3 = f32[1,32,32,128]{3,2,1,0:T(8,128)} fusion(f32[32,128,32]{1,2,0:T(8,128)S(1)} %fusion.33, f32[32,32,128]{2,1,0:T(8,128)S(1)} %convolution_add_fusion.3, f32[32,32,128]{2,1,0:T(8,128)S(1)} %convolution_subtract_fusion.3, f32[32,128]{1,0:T(8,128)} %fusion.119, f32[32,128]{1,0:T(8,128)S(1)} %get-tuple-element.54), kind=kOutput, calls=%fused_computation.10 | convolution fusion | flops 50870272 | bytes 2129920 | tf_op jit(solution)/shard_map/pa,...pb->...ab/dot_general | solution.py:36
  83.3 1.1 reshape.1345
  84.5 2.4 %multiply_subtract_fusion.1 = (f32[1,1,32,8,512]{4,2,1,0,3:T(8,128)S(1)}, f32[1,1,32,8,512]{4,2,1,0,3:T(8,128)S(1)}) fusion(f32[1,1,32,8,512]{4,3,2,1,0:T(8,128)S(1)} %reshape.1346, f32[1,1,32,8,512]{4,3,2,1,0:T(8,128)S(1)} %reshape.1345, s32[8,512]{1,0:T(8,128)S(1)} %copy-done.7, s32[32]{0:T(128)S(1)} %copy-done.12), kind=kLoop, calls=%fused_computation.65 | loop fusion | flops 2621440 | bytes 2113664 | tf_op jit(solution)/shard_map/sub | solution.py:46
  88.0 3.7 %all-to-all-start.2 = ((f32[8,2,1,32,512]{4,3,2,1,0:T(8,128)}), f32[8,2,1,32,512]{4,3,2,1,0:T(8,128)S(1)}, u32[]{:S(2)}, u32[]{:S(2)}) async-start(f32[8,2,1,32,512]{4,3,2,1,0:T(8,128)} %maximum_bitcast_fusion.1), calls=%async_computation.2 | async-start | bytes 2097152 | tf_op jit(solution)/shard_map/all_to_all | solution.py:72
  92.4 14.6 %all-to-all-done.2 = f32[8,2,1,32,512]{4,3,2,1,0:T(8,128)S(1)} async-done(((f32[8,2,1,32,512]{4,3,2,1,0:T(8,128)}), f32[8,2,1,32,512]{4,3,2,1,0:T(8,128)S(1)}, u32[]{:S(2)}, u32[]{:S(2)}) %all-to-all-start.2) | async-done | bytes 1048608 | tf_op jit(solution)/shard_map/all_to_all | solution.py:72
  109.0 3.9 %all-to-all-start.3 = ((f32[8,2,16,512]{3,2,1,0:T(8,128)}), f32[8,2,16,512]{3,2,1,0:T(8,128)S(1)}, u32[]{:S(2)}, u32[]{:S(2)}) async-start(f32[8,2,16,512]{3,2,1,0:T(8,128)} %bitcast.176), calls=%async_computation.3 | async-start | bytes 1048576 | tf_op jit(solution)/shard_map/all_to_all | solution.py:72
  115.6 6.7 %all-to-all-done.3 = f32[8,2,16,512]{3,2,1,0:T(8,128)S(1)} async-done(((f32[8,2,16,512]{3,2,1,0:T(8,128)}), f32[8,2,16,512]{3,2,1,0:T(8,128)S(1)}, u32[]{:S(2)}, u32[]{:S(2)}) %all-to-all-start.3) | async-done | bytes 524320 | tf_op jit(solution)/shard_map/all_to_all | solution.py:72
  122.9 1.6 %add_multiply_fusion.2 = (f32[1,65536]{1,0:T(1,128)}, f32[1,65536]{1,0:T(1,128)S(1)}) fusion(f32[1,65536]{1,0:T(1,128)S(1)} %bitcast.207, f32[1,65536]{1,0:T(1,128)S(1)} %bitcast.206, f32[1,65536]{1,0:T(1,128)S(1)} %copy-done, f32[1,65536]{1,0:T(1,128)S(1)} %bitcast.205, f32[]{:T(128)} %bitcast.60, f32[]{:T(128)} %bitcast.58, s32[]{:T(128)S(6)} %mul.831, ...), kind=kLoop, calls=%fused_computation.94 | loop fusion | flops 786432 | bytes 1835020 | tf_op jit(solution)/shard_map/mul | solution.py:158
  125.1 1.9 %collective-permute-start = (f32[1,1]{1,0:T(1,128)}, f32[1,1]{1,0:T(1,128)}, u32[]{:S(2)}, u32[]{:S(2)}) collective-permute-start(f32[1,1]{1,0:T(1,128)} %slice.131), channel_id=1, source_target_pairs={{0,4},{4,8},{8,12},{12,16},{16,20},{20,24},{24,28},{1,5},{5,9},{9,... | collective-permute-start | bytes 20 | tf_op jit(solution)/shard_map/ppermute | solution.py:19
  127.4 1.9 %maximum_add_fusion = f32[1,65536]{1,0:T(1,128)} fusion(f32[1,65535]{1,0:T(1,128)S(1)} %bitcast.192, f32[1,1]{1,0:T(1,128)} %collective-permute-done, f32[1,65536]{1,0:T(1,128)S(1)} %get-tuple-element.37, f32[1,65536]{1,0:T(1,128)S(1)} %bitcast.204, f32[1,65536]{1,0:T(1,128)S(1)} %get-tuple-element.18, f32[]{:T(128)} %bitcast.58), kind=kLoop, calls=%fused_computation.88 | loop fusion | flops 327680 | bytes 1310724 | tf_op jit(solution)/shard_map/add | solution.py:155
  129.3 3.1 %all-reduce.3.cloned.1.call-done = f32[65536]{0:T(1024)} async-done(((f32[65536]{0:T(1024)}), f32[65536]{0:T(1024)}) %all-reduce.3.cloned.1.call-update) | async-done | bytes 262160 | tf_op jit(solution)/shard_map/psum | solution.py:166
  132.4 1.7 %copy.97 = f32[65536]{0:T(1024)} copy(f32[65536]{0:T(1024)} %all-reduce.3.cloned.1.call-done) | data formatting | bytes 524288
  (88 shorter events, 26.8 us)
Async XLA Ops:
  8.3 3.1 %collective-permute-start.1 = (f32[1,1]{1,0:T(1,128)}, f32[1,1]{1,0:T(1,128)}, u32[]{:S(2)}, u32[]{:S(2)}) collective-permute-start(f32[1,1]{1,0:T(1,128)} %slice.115), channel_id=1, source_target_pairs={{4,0},{8,4},{12,8},{16,12},{20,16},{24,20},{28,24},{5,1},{9,5},{13... | collective-permute-start | bytes 20 | tf_op jit(solution)/shard_map/ppermute | solution.py:19
  9.6 1.8 %copy-start = (f32[1,65536]{1,0:T(1,128)S(1)}, f32[1,65536]{1,0:T(1,128)}, u32[]{:S(2)}) copy-start(f32[1,65536]{1,0:T(1,128)} %param.7) | copy-start | bytes 786436
  9.6 1.8 %copy-start.4 = (f32[1,65536]{1,0:T(1,128)S(1)}, f32[1,65536]{1,0:T(1,128)}, u32[]{:S(2)}) copy-start(f32[1,65536]{1,0:T(1,128)} %param.6) | copy-start | bytes 786436
  18.0 17.7 %all-to-all-start = ((f32[8,40,512]{2,1,0:T(8,128)}), f32[8,40,512]{2,1,0:T(8,128)S(1)}, u32[]{:S(2)}, u32[]{:S(2)}) async-start(f32[8,40,512]{2,1,0:T(8,128)} %pad_maximum_fusion.6), calls=%async_computation | async-start | bytes 1310720 | tf_op jit(solution)/shard_map/all_to_all | solution.py:72
  24.5 0.7 copy-start.8
  40.3 18.9 %all-to-all-start.1 = ((f32[8,2,1,32,512]{4,3,2,1,0:T(8,128)}), f32[8,2,1,32,512]{4,3,2,1,0:T(8,128)S(1)}, u32[]{:S(2)}, u32[]{:S(2)}) async-start(f32[8,2,1,32,512]{4,3,2,1,0:T(8,128)} %maximum_bitcast_fusion), calls=%async_computation.1 | async-start | bytes 2097152 | tf_op jit(solution)/shard_map/all_to_all | solution.py:72
  62.3 0.7 copy-start.5
  62.3 0.7 copy-start.6
  62.3 0.7 copy-start.10
  62.3 0.7 copy-start.11
  67.1 1.1 copy-start.3
  76.2 0.8 copy-start.2
  83.3 1.2 copy-start.7
  83.3 1.2 copy-start.12
  88.0 3.7 %copy-start.9 = (s32[256]{0:T(256)S(1)}, s32[256]{0:T(256)}, u32[]{:S(2)}) copy-start(s32[256]{0:T(256)} %constant.198.clone) | copy-start | bytes 3076
  88.0 19.0 %all-to-all-start.2 = ((f32[8,2,1,32,512]{4,3,2,1,0:T(8,128)}), f32[8,2,1,32,512]{4,3,2,1,0:T(8,128)S(1)}, u32[]{:S(2)}, u32[]{:S(2)}) async-start(f32[8,2,1,32,512]{4,3,2,1,0:T(8,128)} %maximum_bitcast_fusion.1), calls=%async_computation.2 | async-start | bytes 2097152 | tf_op jit(solution)/shard_map/all_to_all | solution.py:72
  91.7 40.7 %all-reduce.3.cloned.1.call-start = ((), (), s32[]{:S(2)}) async-start(), calls=%async_computation.4 | async-start | bytes 524288 | tf_op jit(solution)/shard_map/psum | solution.py:166
  109.0 3.9 %copy-start.1 = (f32[65536]{0:T(1024)S(1)}, f32[65536]{0:T(1024)}, u32[]{:S(2)}) copy-start(f32[65536]{0:T(1024)} %param.8) | copy-start | bytes 786436
  109.0 13.3 %all-to-all-start.3 = ((f32[8,2,16,512]{3,2,1,0:T(8,128)}), f32[8,2,16,512]{3,2,1,0:T(8,128)S(1)}, u32[]{:S(2)}, u32[]{:S(2)}) async-start(f32[8,2,16,512]{3,2,1,0:T(8,128)} %bitcast.176), calls=%async_computation.3 | async-start | bytes 1048576 | tf_op jit(solution)/shard_map/all_to_all | solution.py:72
  125.1 2.3 %collective-permute-start = (f32[1,1]{1,0:T(1,128)}, f32[1,1]{1,0:T(1,128)}, u32[]{:S(2)}, u32[]{:S(2)}) collective-permute-start(f32[1,1]{1,0:T(1,128)} %slice.131), channel_id=1, source_target_pairs={{0,4},{4,8},{8,12},{12,16},{16,20},{20,24},{24,28},{1,5},{5,9},{9,... | collective-permute-start | bytes 20 | tf_op jit(solution)/shard_map/ppermute | solution.py:19
Sparse Core Ops, SparseCore 0:
  95.4 36.9 all-reduce.2

commit v2 on v1

--- a/solution.py
+++ b/solution.py
@@ -163,7 +163,16 @@
         + rate[None, :] * following
     )
     local_grad = jnp.sum(weighted * (following - cotangent), axis=0)
-    rate_gradient = lax.psum(local_grad, "scen")
+    rate_gradient = local_grad
+    groups = lax.axis_size("scen")
+    if groups & (groups - 1) == 0:
+        step = 1
+        while step < groups:
+            pairs = [(source, source ^ step) for source in range(groups)]
+            rate_gradient = rate_gradient + lax.ppermute(rate_gradient, "scen", pairs)
+            step *= 2
+    else:
+        rate_gradient = lax.psum(local_grad, "scen")
     return (tendency, adjoint, rate_gradient)
 
 

time: 142 us -> 125 us (0.88)
  between operations: 15.9 us -> 2.47 us
  waiting for transfers between devices: 45.8 us -> 36.9 us
  starting transfers between devices: 21 us -> 25.2 us
  other arithmetic: 23.5 us -> 25.8 us
  local copies, waits for them, and re-layouts: 14.6 us -> 12.9 us
    all_to_all x4, waiting for transfers between devices: 42.5 us -> 29 us  [exchange(): return lax.all_to_all(value, 'mass', 0, 0, tiled=True)]
    ppermute x0 -> x2, waiting for transfers between devices: none -> 7.58 us  [shards(): rate_gradient = rate_gradient + lax.ppermute(rate_gradient, 'scen', pairs)]
    ppermute x0 -> x2, starting transfers between devices: none -> 4.29 us  [shards(): rate_gradient = rate_gradient + lax.ppermute(rate_gradient, 'scen', pairs)]
    psum x1 -> x0, waiting for transfers between devices: 3.11 us -> none  [shards(): rate_gradient = lax.psum(local_grad, 'scen')]
    add x0 -> x2, other arithmetic: none -> 1.72 us  [shards(): rate_gradient = rate_gradient + lax.ppermute(rate_gradient, 'scen', pairs)]
    unnamed x36 -> x35, local copies, waits for them, and re-layouts: 5 us -> 3.33 us
  transfers between devices with their start and end apart: 7 -> 8, of which waited for: 6 -> 8; matrix products, arithmetic and copies ran while one was open for 11% -> 10% of each run, Pallas kernels for 0% -> 0%
where the time goes in v2:
time: 125 us; the launch traced here: 123 us
  waiting for transfers between devices  36.9 us (30%)
  other arithmetic  25.8 us (21%)
  starting transfers between devices  25.2 us (20%)
  matrix products  20 us (16%)
  local copies, waits for them, and re-layouts  12.9 us (10%)
  between operations  2.47 us (2%)
    all_to_all x4, waiting for transfers between devices, exchange(): return lax.all_to_all(value, 'mass', 0, 0, tiled=True)  29 us
    all_to_all x4, starting transfers between devices, exchange(): return lax.all_to_all(value, 'mass', 0, 0, tiled=True)  17.8 us
    ppermute x2, waiting for transfers between devices, shards(): rate_gradient = rate_gradient + lax.ppermute(rate_gradient, 'scen', pairs)  7.58 us
    sub x2, other arithmetic, complex_mul(): left[0] * right[0] - left[1] * right[1]  5.47 us
    dot_general x4, matrix products, complex_dot(): jnp.einsum(form, table_im, val_im, precision=high)  5.37 us
    dot_general x4, matrix products, complex_dot(): jnp.einsum(form, table_im, val_re, precision=high)  4.64 us
    ppermute x2, starting transfers between devices, shards(): rate_gradient = rate_gradient + lax.ppermute(rate_gradient, 'scen', pairs)  4.29 us
    dot_general x4, matrix products, complex_dot(): jnp.einsum(form, table_re, val_re, precision=high)  4.06 us
  transfers between devices with their start and end apart: 8, of which 8 were waited for; matrix products, arithmetic and copies ran while one was open for 10% of the time, Pallas kernels for 0%

profile of v2, /device:TPU:0, one launch (start us, length us, event | category | flops | bytes accessed | tf_op | source)
XLA Modules:
  0.0 123.4 jit_solution(10996945693753702952)
XLA Ops:
  0.6 1.2 slice.115
  1.8 1.3 %collective-permute-start.1 = (f32[1,1]{1,0:T(1,128)}, f32[1,1]{1,0:T(1,128)}, u32[]{:S(2)}, u32[]{:S(2)}) collective-permute-start(f32[1,1]{1,0:T(1,128)} %slice.115), channel_id=1, source_target_pairs={{4,0},{8,4},{12,8},{16,12},{20,16},{24,20},{28,24},{5,1},{9,5},{13... | collective-permute-start | bytes 20 | tf_op jit(solution)/shard_map/ppermute | solution.py:19
  3.1 1.6 %slice.114 = f32[1,65535]{1,0:T(1,128)S(1)} slice(f32[1,65536]{1,0:T(1,128)} %param.7), slice={[0:1], [1:65536]} | slice | bytes 524280 | tf_op jit(solution)/shard_map/slice | solution.py:157
  4.9 2.1 %fusion.29 = (f32[1,65536]{1,0:T(1,128)}, f32[1,65536]{1,0:T(1,128)S(1)}) fusion(f32[1,65536]{1,0:T(1,128)S(1)} %copy-done, f32[1,1]{1,0:T(1,128)} %collective-permute-done.1, f32[1,65535]{1,0:T(1,128)S(1)} %slice.114, f32[1,65536]{1,0:T(1,128)S(1)} %copy-done.5, s32[]{:T(128)S(6)} %mul.831), kind=kLoop, calls=%fused_computation.91 | loop fusion | flops 524288 | bytes 1310724 | tf_op jit(solution)/shard_map/mul | solution.py:165
  7.0 1.2 fusion.193
  9.2 1.4 %maximum_bitcast_fusion.6 = f32[1,2]{1,0:T(1,128)S(1)} fusion(f32[1]{0:T(128)} %bitcast.6, f32[1]{0:T(128)} %bitcast.5), kind=kLoop, calls=%fused_computation.201 | loop fusion | flops 2 | bytes 16 | tf_op jit(solution)/shard_map/reshape.73
  11.5 6.5 %all-to-all-start = ((f32[8,40,512]{2,1,0:T(8,128)}), f32[8,40,512]{2,1,0:T(8,128)S(1)}, u32[]{:S(2)}, u32[]{:S(2)}) async-start(f32[8,40,512]{2,1,0:T(8,128)} %pad_maximum_fusion.6), calls=%async_computation | async-start | bytes 1310720 | tf_op jit(solution)/shard_map/all_to_all | solution.py:72
  19.3 9.8 %all-to-all-done = f32[8,40,512]{2,1,0:T(8,128)S(1)} async-done(((f32[8,40,512]{2,1,0:T(8,128)}), f32[8,40,512]{2,1,0:T(8,128)S(1)}, u32[]{:S(2)}, u32[]{:S(2)}) %all-to-all-start) | async-done | bytes 655392 | tf_op jit(solution)/shard_map/all_to_all | solution.py:72
  30.3 2.4 %multiply_subtract_fusion.3 = (f32[1,1,256,512]{3,2,0,1:T(8,128)S(1)}, f32[1,1,256,512]{3,2,0,1:T(8,128)S(1)}) fusion(f32[2,1,256,512]{3,2,0,1:T(8,128)S(1)} %convolution_bitcast_fusion, s32[512]{0:T(512)S(1)} %iota_add_fusion, s32[256]{0:T(256)S(1)} %copy-done.9), kind=kLoop, calls=%fused_computation.74 | loop fusion | flops 2752512 | bytes 2100224 | tf_op jit(solution)/shard_map/sub | solution.py:46
  33.7 3.7 %all-to-all-start.1 = ((f32[8,2,1,32,512]{4,3,2,1,0:T(8,128)}), f32[8,2,1,32,512]{4,3,2,1,0:T(8,128)S(1)}, u32[]{:S(2)}, u32[]{:S(2)}) async-start(f32[8,2,1,32,512]{4,3,2,1,0:T(8,128)} %maximum_bitcast_fusion), calls=%async_computation.1 | async-start | bytes 2097152 | tf_op jit(solution)/shard_map/all_to_all | solution.py:72
  41.3 11.3 %all-to-all-done.1 = f32[8,2,1,32,512]{4,3,2,1,0:T(8,128)S(1)} async-done(((f32[8,2,1,32,512]{4,3,2,1,0:T(8,128)}), f32[8,2,1,32,512]{4,3,2,1,0:T(8,128)S(1)}, u32[]{:S(2)}, u32[]{:S(2)}) %all-to-all-start.1) | async-done | bytes 1048608 | tf_op jit(solution)/shard_map/all_to_all | solution.py:72
  61.8 1.2 fusion.28
  63.0 1.2 fusion.27
  64.2 1.2 convolution_add_fusion
  65.5 1.2 %convolution_subtract_fusion = f32[2,32,32,128]{3,2,1,0:T(8,128)S(1)} fusion(f32[2,32,32,128]{3,2,1,0:T(8,128)S(1)} %fusion.27, f32[2,32,32,128]{3,2,1,0:T(8,128)S(1)} %fusion, f32[2,32,32,128]{3,2,1,0:T(8,128)S(1)} %fusion.1, f32[32,128]{1,0:T(8,128)S(1)} %copy-done.4, f32[32,128]{1,0:T(8,128)S(1)} %get-tuple-element.54), kind=kOutput, calls=%fused_computation.1 | convolution fusion | flops 403947520 | bytes 4227072 | tf_op jit(solution)/shard_map/qb,...pb->...pq/dot_general | solution.py:36
  71.9 1.5 %fusion.2 = f32[1,32,32,128]{3,2,1,0:T(8,128)} fusion(f32[32,128,32]{1,2,0:T(8,128)S(1)} %fusion.34, f32[32,32,128]{2,1,0:T(8,128)S(1)} %convolution_add_fusion.3, f32[32,32,128]{2,1,0:T(8,128)S(1)} %convolution_subtract_fusion.3, f32[32,128]{1,0:T(8,128)S(1)} %copy-done.3, f32[32,128]{1,0:T(8,128)S(1)} %get-tuple-element.54), kind=kOutput, calls=%fused_computation.8 | convolution fusion | flops 50870272 | bytes 2129920 | tf_op jit(solution)/shard_map/pa,...pb->...ab/dot_general | solution.py:39
  73.4 1.1 reshape.1346
  74.5 2.2 %fusion.3 = f32[1,32,32,128]{3,2,1,0:T(8,128)} fusion(f32[32,128,32]{1,2,0:T(8,128)S(1)} %fusion.33, f32[32,32,128]{2,1,0:T(8,128)S(1)} %convolution_add_fusion.3, f32[32,32,128]{2,1,0:T(8,128)S(1)} %convolution_subtract_fusion.3, f32[32,128]{1,0:T(8,128)} %fusion.119, f32[32,128]{1,0:T(8,128)S(1)} %get-tuple-element.54), kind=kOutput, calls=%fused_computation.10 | convolution fusion | flops 50870272 | bytes 2129920 | tf_op jit(solution)/shard_map/pa,...pb->...ab/dot_general | solution.py:36
  76.7 1.1 reshape.1345
  77.9 3.1 %multiply_subtract_fusion.1 = (f32[1,1,32,8,512]{4,2,1,0,3:T(8,128)S(1)}, f32[1,1,32,8,512]{4,2,1,0,3:T(8,128)S(1)}) fusion(f32[1,1,32,8,512]{4,3,2,1,0:T(8,128)S(1)} %reshape.1346, f32[1,1,32,8,512]{4,3,2,1,0:T(8,128)S(1)} %reshape.1345, s32[8,512]{1,0:T(8,128)S(1)} %copy-done.8, s32[32]{0:T(128)} %and_select_fusion.1), kind=kLoop, calls=%fused_computation.65 | loop fusion | flops 2621440 | bytes 2113664 | tf_op jit(solution)/shard_map/sub | solution.py:46
  82.1 3.7 %all-to-all-start.2 = ((f32[8,2,1,32,512]{4,3,2,1,0:T(8,128)}), f32[8,2,1,32,512]{4,3,2,1,0:T(8,128)S(1)}, u32[]{:S(2)}, u32[]{:S(2)}) async-start(f32[8,2,1,32,512]{4,3,2,1,0:T(8,128)} %maximum_bitcast_fusion.1), calls=%async_computation.2 | async-start | bytes 2097152 | tf_op jit(solution)/shard_map/all_to_all | solution.py:72
  85.8 1.7 %collective-permute-start.2 = (f32[65536]{0:T(1024)S(1)}, f32[65536]{0:T(1024)S(1)}, u32[]{:S(2)}, u32[]{:S(2)}) collective-permute-start(f32[65536]{0:T(1024)S(1)} %bitcast.201), channel_id=1, source_target_pairs={{0,1},{1,0},{2,3},{3,2},{4,5},{5,4},{6,7},{7,6},{8,9},{9,8},{10,11... | collective-permute-start | bytes 786440 | tf_op jit(solution)/shard_map/ppermute | solution.py:172
  88.1 6.4 %collective-permute-done.2 = f32[65536]{0:T(1024)S(1)} collective-permute-done((f32[65536]{0:T(1024)S(1)}, f32[65536]{0:T(1024)S(1)}, u32[]{:S(2)}, u32[]{:S(2)}) %collective-permute-start.2) | collective-permute-done | bytes 262176 | tf_op jit(solution)/shard_map/ppermute | solution.py:172
  94.5 2.6 %collective-permute-start.3 = (f32[65536]{0:T(1024)S(1)}, f32[65536]{0:T(1024)}, u32[]{:S(2)}, u32[]{:S(2)}) collective-permute-start(f32[65536]{0:T(1024)S(1)} %add.373), channel_id=1, source_target_pairs={{0,2},{1,3},{2,0},{3,1},{4,6},{5,7},{6,4},{7,5},{8,10},{9,11},{10,... | collective-permute-start | bytes 786440 | tf_op jit(solution)/shard_map/ppermute | solution.py:172
  97.2 4.0 %all-to-all-done.2 = f32[8,2,1,32,512]{4,3,2,1,0:T(8,128)S(1)} async-done(((f32[8,2,1,32,512]{4,3,2,1,0:T(8,128)}), f32[8,2,1,32,512]{4,3,2,1,0:T(8,128)S(1)}, u32[]{:S(2)}, u32[]{:S(2)}) %all-to-all-start.2) | async-done | bytes 1048608 | tf_op jit(solution)/shard_map/all_to_all | solution.py:72
  103.1 3.9 %all-to-all-start.3 = ((f32[8,2,16,512]{3,2,1,0:T(8,128)}), f32[8,2,16,512]{3,2,1,0:T(8,128)S(1)}, u32[]{:S(2)}, u32[]{:S(2)}) async-start(f32[8,2,16,512]{3,2,1,0:T(8,128)} %bitcast.176), calls=%async_computation.3 | async-start | bytes 1048576 | tf_op jit(solution)/shard_map/all_to_all | solution.py:72
  107.8 1.2 collective-permute-done.3
  109.0 1.7 %add.374 = f32[65536]{0:T(1024)} add(f32[65536]{0:T(1024)S(1)} %add.373, f32[65536]{0:T(1024)} %collective-permute-done.3) | non-fusion elementwise | flops 65536 | bytes 786432 | tf_op jit(solution)/shard_map/add | solution.py:172
  112.6 3.9 %all-to-all-done.3 = f32[8,2,16,512]{3,2,1,0:T(8,128)S(1)} async-done(((f32[8,2,16,512]{3,2,1,0:T(8,128)}), f32[8,2,16,512]{3,2,1,0:T(8,128)S(1)}, u32[]{:S(2)}, u32[]{:S(2)}) %all-to-all-start.3) | async-done | bytes 524320 | tf_op jit(solution)/shard_map/all_to_all | solution.py:72
  117.0 1.6 %add_multiply_fusion.2 = (f32[1,65536]{1,0:T(1,128)}, f32[1,65536]{1,0:T(1,128)S(1)}) fusion(f32[1,65536]{1,0:T(1,128)S(1)} %bitcast.208, f32[1,65536]{1,0:T(1,128)S(1)} %bitcast.207, f32[1,65536]{1,0:T(1,128)S(1)} %copy-done, f32[1,65536]{1,0:T(1,128)S(1)} %bitcast.206, f32[]{:T(128)} %bitcast.60, f32[]{:T(128)} %bitcast.58, s32[]{:T(128)S(6)} %mul.831, ...), kind=kLoop, calls=%fused_computation.94 | loop fusion | flops 786432 | bytes 1835020 | tf_op jit(solution)/shard_map/mul | solution.py:158
  119.2 1.8 %collective-permute-start = (f32[1,1]{1,0:T(1,128)}, f32[1,1]{1,0:T(1,128)}, u32[]{:S(2)}, u32[]{:S(2)}) collective-permute-start(f32[1,1]{1,0:T(1,128)} %slice.131), channel_id=1, source_target_pairs={{0,4},{4,8},{8,12},{12,16},{16,20},{20,24},{24,28},{1,5},{5,9},{9,... | collective-permute-start | bytes 20 | tf_op jit(solution)/shard_map/ppermute | solution.py:19
  121.5 1.9 %maximum_add_fusion = f32[1,65536]{1,0:T(1,128)} fusion(f32[1,65535]{1,0:T(1,128)S(1)} %bitcast.192, f32[1,1]{1,0:T(1,128)} %collective-permute-done, f32[1,65536]{1,0:T(1,128)S(1)} %get-tuple-element.37, f32[1,65536]{1,0:T(1,128)S(1)} %bitcast.205, f32[1,65536]{1,0:T(1,128)S(1)} %get-tuple-element.18, f32[]{:T(128)} %bitcast.58), kind=kLoop, calls=%fused_computation.88 | loop fusion | flops 327680 | bytes 1310724 | tf_op jit(solution)/shard_map/add | solution.py:155
  (90 shorter events, 30.2 us)
Async XLA Ops:
  1.8 3.1 %collective-permute-start.1 = (f32[1,1]{1,0:T(1,128)}, f32[1,1]{1,0:T(1,128)}, u32[]{:S(2)}, u32[]{:S(2)}) collective-permute-start(f32[1,1]{1,0:T(1,128)} %slice.115), channel_id=1, source_target_pairs={{4,0},{8,4},{12,8},{16,12},{20,16},{24,20},{28,24},{5,1},{9,5},{13... | collective-permute-start | bytes 20 | tf_op jit(solution)/shard_map/ppermute | solution.py:19
  3.1 1.8 %copy-start = (f32[1,65536]{1,0:T(1,128)S(1)}, f32[1,65536]{1,0:T(1,128)}, u32[]{:S(2)}) copy-start(f32[1,65536]{1,0:T(1,128)} %param.7) | copy-start | bytes 786436
  3.1 1.8 %copy-start.5 = (f32[1,65536]{1,0:T(1,128)S(1)}, f32[1,65536]{1,0:T(1,128)}, u32[]{:S(2)}) copy-start(f32[1,65536]{1,0:T(1,128)} %param.6) | copy-start | bytes 786436
  11.5 17.7 %all-to-all-start = ((f32[8,40,512]{2,1,0:T(8,128)}), f32[8,40,512]{2,1,0:T(8,128)S(1)}, u32[]{:S(2)}, u32[]{:S(2)}) async-start(f32[8,40,512]{2,1,0:T(8,128)} %pad_maximum_fusion.6), calls=%async_computation | async-start | bytes 1310720 | tf_op jit(solution)/shard_map/all_to_all | solution.py:72
  18.0 0.7 copy-start.9
  33.7 18.9 %all-to-all-start.1 = ((f32[8,2,1,32,512]{4,3,2,1,0:T(8,128)}), f32[8,2,1,32,512]{4,3,2,1,0:T(8,128)S(1)}, u32[]{:S(2)}, u32[]{:S(2)}) async-start(f32[8,2,1,32,512]{4,3,2,1,0:T(8,128)} %maximum_bitcast_fusion), calls=%async_computation.1 | async-start | bytes 2097152 | tf_op jit(solution)/shard_map/all_to_all | solution.py:72
  55.7 0.7 copy-start.6
  55.7 0.7 copy-start.7
  55.8 0.7 copy-start.11
  55.8 0.7 copy-start.12
  60.6 1.1 copy-start.4
  69.7 0.8 copy-start.3
  76.7 1.2 copy-start.8
  82.1 3.7 %copy-start.1 = (f32[1,65536]{1,0:T(1,128)S(1)}, f32[1,65536]{1,0:T(1,128)}, u32[]{:S(2)}) copy-start(f32[1,65536]{1,0:T(1,128)} %get-tuple-element.17) | copy-start | bytes 786436
  82.1 19.0 %all-to-all-start.2 = ((f32[8,2,1,32,512]{4,3,2,1,0:T(8,128)}), f32[8,2,1,32,512]{4,3,2,1,0:T(8,128)S(1)}, u32[]{:S(2)}, u32[]{:S(2)}) async-start(f32[8,2,1,32,512]{4,3,2,1,0:T(8,128)} %maximum_bitcast_fusion.1), calls=%async_computation.2 | async-start | bytes 2097152 | tf_op jit(solution)/shard_map/all_to_all | solution.py:72
  85.8 1.7 %copy-start.10 = (s32[256]{0:T(256)S(1)}, s32[256]{0:T(256)}, u32[]{:S(2)}) copy-start(s32[256]{0:T(256)} %constant.198.clone) | copy-start | bytes 3076
  85.8 8.7 %collective-permute-start.2 = (f32[65536]{0:T(1024)S(1)}, f32[65536]{0:T(1024)S(1)}, u32[]{:S(2)}, u32[]{:S(2)}) collective-permute-start(f32[65536]{0:T(1024)S(1)} %bitcast.201), channel_id=1, source_target_pairs={{0,1},{1,0},{2,3},{3,2},{4,5},{5,4},{6,7},{7,6},{8,9},{9,8},{10,11... | collective-permute-start | bytes 786440 | tf_op jit(solution)/shard_map/ppermute | solution.py:172
  94.5 14.5 %collective-permute-start.3 = (f32[65536]{0:T(1024)S(1)}, f32[65536]{0:T(1024)}, u32[]{:S(2)}, u32[]{:S(2)}) collective-permute-start(f32[65536]{0:T(1024)S(1)} %add.373), channel_id=1, source_target_pairs={{0,2},{1,3},{2,0},{3,1},{4,6},{5,7},{6,4},{7,5},{8,10},{9,11},{10,... | collective-permute-start | bytes 786440 | tf_op jit(solution)/shard_map/ppermute | solution.py:172
  103.1 3.9 %copy-start.2 = (f32[65536]{0:T(1024)S(1)}, f32[65536]{0:T(1024)}, u32[]{:S(2)}) copy-start(f32[65536]{0:T(1024)} %param.8) | copy-start | bytes 786436
  103.1 13.3 %all-to-all-start.3 = ((f32[8,2,16,512]{3,2,1,0:T(8,128)}), f32[8,2,16,512]{3,2,1,0:T(8,128)S(1)}, u32[]{:S(2)}, u32[]{:S(2)}) async-start(f32[8,2,16,512]{3,2,1,0:T(8,128)} %bitcast.176), calls=%async_computation.3 | async-start | bytes 1048576 | tf_op jit(solution)/shard_map/all_to_all | solution.py:72
  119.2 2.4 %collective-permute-start = (f32[1,1]{1,0:T(1,128)}, f32[1,1]{1,0:T(1,128)}, u32[]{:S(2)}, u32[]{:S(2)}) collective-permute-start(f32[1,1]{1,0:T(1,128)} %slice.131), channel_id=1, source_target_pairs={{0,4},{4,8},{8,12},{12,16},{16,20},{20,24},{24,28},{1,5},{5,9},{9,... | collective-permute-start | bytes 20 | tf_op jit(solution)/shard_map/ppermute | solution.py:19

commit v3 on v2

--- a/solution.py
+++ b/solution.py
@@ -91,13 +91,20 @@
     mass = ((offset + counting(bin_dev)).astype(jnp.float32) + 0.5) / nbin
     weighted = mass[None, :] * density
     partial = jnp.concatenate([jnp.sum(weighted, axis=1), jnp.sum(cotangent * weighted, axis=1)])
-    tile = jnp.zeros((8, cols), jnp.float32).at[0, :arrays].set(partial)
+    flux = rate[None, :] * weighted
+    edges = jnp.concatenate([flux[:, -1], cotangent[:, 0]])
+    tile = jnp.zeros((8, cols), jnp.float32).at[0, :arrays].set(partial).at[1, :arrays].set(edges)
     stacked = jnp.concatenate([weighted, cotangent], axis=0).reshape(arrays, rows, parts, cols)
     outgoing = stacked.transpose(2, 0, 1, 3).reshape(parts, arrays * rows, cols)
     outgoing = jnp.concatenate([outgoing, jnp.broadcast_to(tile, (parts, 8, cols))], axis=1)
     incoming_rows = exchange(outgoing)
     moments = jnp.sum(incoming_rows[:, arrays * rows, :arrays], axis=0)
     first, cross = moments[:scen_dev], moments[scen_dev:]
+    neighbours = incoming_rows[:, arrays * rows + 1, :arrays]
+    behind = lax.dynamic_index_in_dim(neighbours, (place + parts - 1) % parts, keepdims=False)
+    ahead = lax.dynamic_index_in_dim(neighbours, (place + 1) % parts, keepdims=False)
+    incoming = jnp.where(place > 0, behind[:scen_dev], 0.0)[:, None]
+    arriving = jnp.where(place < parts - 1, ahead[scen_dev:], 0.0)[:, None]
     spread = incoming_rows[:, : arrays * rows].reshape(parts, arrays, rows, cols)
     spread = spread.transpose(1, 0, 2, 3).reshape(arrays, half_rows, cols)
     half = block // 2
@@ -149,11 +156,8 @@
     gathered = exchange(real_part).transpose(1, 2, 0, 3).reshape(arrays, bin_dev) / nfft
     birth = gathered[:scen_dev]
     corr = gathered[scen_dev:]
-    flux = rate[None, :] * weighted
-    incoming = from_behind(flux[:, -1:], "mass", 1)
     inflow = jnp.concatenate([incoming, flux[:, :-1]], axis=1)
     tendency = 0.5 * beta * birth - beta * first[:, None] * weighted - flux + inflow
-    arriving = from_behind(cotangent[:, :1], "mass", -1)
     following = jnp.concatenate([cotangent[:, 1:], arriving], axis=1)
     adjoint = mass[None, :] * (
         beta * corr

time: 125 us -> 143 us (1.14)
  the two profiles are of different devices: /device:TPU:0 before, /device:TPU:27 now
where the time goes in v3:
time: 143 us; the launch traced here: 142 us
  waiting for transfers between devices  61.2 us (43%)
  matrix products  21.2 us (15%)
  other arithmetic  20.6 us (14%)
  starting transfers between devices  20 us (14%)
  local copies, waits for them, and re-layouts  16.1 us (11%)
  between operations  3.02 us (2%)
    all_to_all x4, waiting for transfers between devices, exchange(): return lax.all_to_all(value, 'mass', 0, 0, tiled=True)  39.4 us
    ppermute x2, waiting for transfers between devices, shards(): rate_gradient = rate_gradient + lax.ppermute(rate_gradient, 'scen', pairs)  21.8 us
    all_to_all x4, starting transfers between devices, exchange(): return lax.all_to_all(value, 'mass', 0, 0, tiled=True)  19.6 us
    dot_general x4, matrix products, complex_dot(): jnp.einsum(form, table_im, val_re, precision=high)  5.7 us
    sub x2, other arithmetic, complex_mul(): left[0] * right[0] - left[1] * right[1]  4.8 us
    dot_general x4, matrix products, complex_dot(): jnp.einsum(form, table_im, val_im, precision=high)  4.66 us
    dot_general x4, matrix products, complex_dot(): jnp.einsum(form, table_re, val_im, precision=high)  4.65 us
    dot_general x4, matrix products, complex_dot(): jnp.einsum(form, table_re, val_re, precision=high)  4.05 us
  transfers between devices with their start and end apart: 6, of which 6 were waited for; matrix products, arithmetic and copies ran while one was open for 2% of the time, Pallas kernels for 0%

profile of v3, /device:TPU:27, one launch (start us, length us, event | category | flops | bytes accessed | tf_op | source)
XLA Modules:
  0.0 142.2 jit_solution(8355119386897280053)
XLA Ops:
  0.6 1.2 slice.129
  1.8 2.4 %fusion.193 = (f32[]{:T(128)}, f32[]{:T(128)}, f32[1,65536]{1,0:T(1,128)S(1)}) fusion(f32[1,65536]{1,0:T(1,128)} %param.9, f32[1,65536]{1,0:T(1,128)} %param.8, s32[]{:T(128)S(6)} %mul.831), kind=kLoop, calls=%fused_computation.275 | loop fusion | flops 524286 | bytes 786444 | tf_op jit(solution)/shard_map/reduce_sum | solution.py:93
  6.5 1.4 maximum_bitcast_fusion.6
  7.9 1.4 maximum_bitcast_fusion.7
  10.4 4.6 %all-to-all-start = ((f32[8,40,512]{2,1,0:T(8,128)}), f32[8,40,512]{2,1,0:T(8,128)S(1)}, u32[]{:S(2)}, u32[]{:S(2)}) async-start(f32[8,40,512]{2,1,0:T(8,128)} %pad_maximum_fusion.6), calls=%async_computation | async-start | bytes 1310720 | tf_op jit(solution)/shard_map/all_to_all | solution.py:72
  16.3 8.3 %all-to-all-done = f32[8,40,512]{2,1,0:T(8,128)S(1)} async-done(((f32[8,40,512]{2,1,0:T(8,128)}), f32[8,40,512]{2,1,0:T(8,128)S(1)}, u32[]{:S(2)}, u32[]{:S(2)}) %all-to-all-start) | async-done | bytes 655392 | tf_op jit(solution)/shard_map/all_to_all | solution.py:72
  25.8 2.4 %multiply_subtract_fusion.3 = (f32[1,1,256,512]{3,2,0,1:T(8,128)S(1)}, f32[1,1,256,512]{3,2,0,1:T(8,128)S(1)}) fusion(f32[2,1,256,512]{3,2,0,1:T(8,128)S(1)} %convolution_bitcast_fusion, s32[512]{0:T(512)S(1)} %iota_add_fusion, s32[256]{0:T(256)S(1)} %copy-done.3), kind=kLoop, calls=%fused_computation.74 | loop fusion | flops 2752512 | bytes 2100224 | tf_op jit(solution)/shard_map/sub | solution.py:46
  29.2 5.0 %all-to-all-start.1 = ((f32[8,2,1,32,512]{4,3,2,1,0:T(8,128)}), f32[8,2,1,32,512]{4,3,2,1,0:T(8,128)S(1)}, u32[]{:S(2)}, u32[]{:S(2)}) async-start(f32[8,2,1,32,512]{4,3,2,1,0:T(8,128)} %maximum_bitcast_fusion), calls=%async_computation.1 | async-start | bytes 2097152 | tf_op jit(solution)/shard_map/all_to_all | solution.py:72
  34.5 13.5 %all-to-all-done.1 = f32[8,2,1,32,512]{4,3,2,1,0:T(8,128)S(1)} async-done(((f32[8,2,1,32,512]{4,3,2,1,0:T(8,128)}), f32[8,2,1,32,512]{4,3,2,1,0:T(8,128)S(1)}, u32[]{:S(2)}, u32[]{:S(2)}) %all-to-all-start.1) | async-done | bytes 1048608 | tf_op jit(solution)/shard_map/all_to_all | solution.py:72
  50.2 1.4 copy.51
  55.6 1.1 fusion.5
  56.7 1.1 fusion.4
  57.8 1.1 fusion.1
  58.9 1.1 fusion
  60.0 1.2 fusion.27
  61.3 1.2 fusion.28
  62.5 1.2 convolution_subtract_fusion
  63.7 1.2 convolution_add_fusion
  69.4 1.5 %fusion.34 = f32[32,128,32]{1,2,0:T(8,128)} fusion(f32[32,32,128]{2,1,0:T(8,128)S(1)} %convolution_add_fusion.3, f32[32,32,128]{2,1,0:T(8,128)S(1)} %convolution_subtract_fusion.3, f32[32,128]{1,0:T(8,128)S(1)} %fusion.119, f32[32,128]{1,0:T(8,128)S(1)} %get-tuple-element.70), kind=kOutput, calls=%fused_computation.107 | convolution fusion | flops 50739200 | bytes 1605632 | tf_op jit(solution)/shard_map/pa,...pb->...ab/dot_general | solution.py:39
  71.0 1.5 %fusion.3 = f32[1,32,32,128]{3,2,1,0:T(8,128)} fusion(f32[32,128,32]{1,2,0:T(8,128)S(1)} %fusion.33, f32[32,32,128]{2,1,0:T(8,128)S(1)} %convolution_add_fusion.3, f32[32,32,128]{2,1,0:T(8,128)S(1)} %convolution_subtract_fusion.3, f32[32,128]{1,0:T(8,128)S(1)} %fusion.119, f32[32,128]{1,0:T(8,128)S(1)} %get-tuple-element.70), kind=kOutput, calls=%fused_computation.10 | convolution fusion | flops 50870272 | bytes 2129920 | tf_op jit(solution)/shard_map/pa,...pb->...ab/dot_general | solution.py:36
  72.5 1.1 reshape.1384
  73.6 2.5 %fusion.2 = f32[1,32,32,128]{3,2,1,0:T(8,128)} fusion(f32[32,128,32]{1,2,0:T(8,128)} %fusion.34, f32[32,32,128]{2,1,0:T(8,128)S(1)} %convolution_add_fusion.3, f32[32,32,128]{2,1,0:T(8,128)S(1)} %convolution_subtract_fusion.3, f32[32,128]{1,0:T(8,128)S(1)} %fusion.119, f32[32,128]{1,0:T(8,128)S(1)} %get-tuple-element.70), kind=kOutput, calls=%fused_computation.8 | convolution fusion | flops 50870272 | bytes 2129920 | tf_op jit(solution)/shard_map/pa,...pb->...ab/dot_general | solution.py:39
  76.1 1.1 reshape.1385
  77.3 2.4 %multiply_subtract_fusion.1 = (f32[1,1,32,8,512]{4,2,1,0,3:T(8,128)S(1)}, f32[1,1,32,8,512]{4,2,1,0,3:T(8,128)S(1)}) fusion(f32[1,1,32,8,512]{4,3,2,1,0:T(8,128)S(1)} %reshape.1385, f32[1,1,32,8,512]{4,3,2,1,0:T(8,128)S(1)} %reshape.1384, s32[8,512]{1,0:T(8,128)S(1)} %multiply_add_fusion.9, s32[32]{0:T(128)S(1)} %and_select_fusion.1), kind=kLoop, calls=%fused_computation.65 | loop fusion | flops 2621440 | bytes 2113664 | tf_op jit(solution)/shard_map/sub | solution.py:46
  79.7 1.1 maximum_bitcast_fusion.1
  80.8 5.1 %all-to-all-start.2 = ((f32[8,2,1,32,512]{4,3,2,1,0:T(8,128)}), f32[8,2,1,32,512]{4,3,2,1,0:T(8,128)S(1)}, u32[]{:S(2)}, u32[]{:S(2)}) async-start(f32[8,2,1,32,512]{4,3,2,1,0:T(8,128)} %maximum_bitcast_fusion.1), calls=%async_computation.2 | async-start | bytes 2097152 | tf_op jit(solution)/shard_map/all_to_all | solution.py:72
  88.4 11.4 %all-to-all-done.2 = f32[8,2,1,32,512]{4,3,2,1,0:T(8,128)S(1)} async-done(((f32[8,2,1,32,512]{4,3,2,1,0:T(8,128)}), f32[8,2,1,32,512]{4,3,2,1,0:T(8,128)S(1)}, u32[]{:S(2)}, u32[]{:S(2)}) %all-to-all-start.2) | async-done | bytes 1048608 | tf_op jit(solution)/shard_map/all_to_all | solution.py:72
  101.8 5.0 %all-to-all-start.3 = ((f32[8,2,16,512]{3,2,1,0:T(8,128)}), f32[8,2,16,512]{3,2,1,0:T(8,128)S(1)}, u32[]{:S(2)}, u32[]{:S(2)}) async-start(f32[8,2,16,512]{3,2,1,0:T(8,128)} %bitcast.185), calls=%async_computation.3 | async-start | bytes 1048576 | tf_op jit(solution)/shard_map/all_to_all | solution.py:72
  108.8 6.2 %all-to-all-done.3 = f32[8,2,16,512]{3,2,1,0:T(8,128)S(1)} async-done(((f32[8,2,16,512]{3,2,1,0:T(8,128)}), f32[8,2,16,512]{3,2,1,0:T(8,128)S(1)}, u32[]{:S(2)}, u32[]{:S(2)}) %all-to-all-start.3) | async-done | bytes 524320 | tf_op jit(solution)/shard_map/all_to_all | solution.py:72
  116.0 3.3 %fusion.29 = (f32[1,65536]{1,0:T(1,128)S(1)}, f32[1,65536]{1,0:T(1,128)}, f32[1,65536]{1,0:T(1,128)}) fusion(f32[1,65536]{1,0:T(1,128)S(1)} %get-tuple-element.29, f32[1,65536]{1,0:T(1,128)S(1)} %copy-done, f32[1,1]{1,0:T(1,128)} %bitcast.71, f32[1,65535]{1,0:T(1,128)S(1)} %slice.152, f32[1,65536]{1,0:T(1,128)S(1)} %bitcast.217, ...), kind=kLoop, calls=%fused_computation.91 | loop fusion | flops 1245184 | bytes 3145740 | tf_op jit(solution)/shard_map/mul | solution.py:169
  119.4 7.3 %collective-permute-done = f32[65536]{0:T(1024)S(1)} collective-permute-done((f32[65536]{0:T(1024)S(1)}, f32[65536]{0:T(1024)S(1)}, u32[]{:S(2)}, u32[]{:S(2)}) %collective-permute-start) | collective-permute-done | bytes 262176 | tf_op jit(solution)/shard_map/ppermute | solution.py:176
  126.9 14.6 %collective-permute-done.1 = f32[65536]{0:T(1024)S(1)} collective-permute-done((f32[65536]{0:T(1024)S(1)}, f32[65536]{0:T(1024)S(1)}, u32[]{:S(2)}, u32[]{:S(2)}) %collective-permute-start.1) | collective-permute-done | bytes 262176 | tf_op jit(solution)/shard_map/ppermute | solution.py:176
  (71 shorter events, 24.2 us)
Async XLA Ops:
  1.8 2.4 %copy-start = (f32[1,65536]{1,0:T(1,128)S(1)}, f32[1,65536]{1,0:T(1,128)}, u32[]{:S(2)}) copy-start(f32[1,65536]{1,0:T(1,128)} %param.9) | copy-start | bytes 786436
  4.2 1.0 copy-start.1
  10.4 14.2 %all-to-all-start = ((f32[8,40,512]{2,1,0:T(8,128)}), f32[8,40,512]{2,1,0:T(8,128)S(1)}, u32[]{:S(2)}, u32[]{:S(2)}) async-start(f32[8,40,512]{2,1,0:T(8,128)} %pad_maximum_fusion.6), calls=%async_computation | async-start | bytes 1310720 | tf_op jit(solution)/shard_map/all_to_all | solution.py:72
  15.0 0.7 copy-start.3
  29.2 18.8 %all-to-all-start.1 = ((f32[8,2,1,32,512]{4,3,2,1,0:T(8,128)}), f32[8,2,1,32,512]{4,3,2,1,0:T(8,128)S(1)}, u32[]{:S(2)}, u32[]{:S(2)}) async-start(f32[8,2,1,32,512]{4,3,2,1,0:T(8,128)} %maximum_bitcast_fusion), calls=%async_computation.1 | async-start | bytes 2097152 | tf_op jit(solution)/shard_map/all_to_all | solution.py:72
  53.6 1.0 copy-start.2
  80.8 18.9 %all-to-all-start.2 = ((f32[8,2,1,32,512]{4,3,2,1,0:T(8,128)}), f32[8,2,1,32,512]{4,3,2,1,0:T(8,128)S(1)}, u32[]{:S(2)}, u32[]{:S(2)}) async-start(f32[8,2,1,32,512]{4,3,2,1,0:T(8,128)} %maximum_bitcast_fusion.1), calls=%async_computation.2 | async-start | bytes 2097152 | tf_op jit(solution)/shard_map/all_to_all | solution.py:72
  101.8 13.2 %all-to-all-start.3 = ((f32[8,2,16,512]{3,2,1,0:T(8,128)}), f32[8,2,16,512]{3,2,1,0:T(8,128)S(1)}, u32[]{:S(2)}, u32[]{:S(2)}) async-start(f32[8,2,16,512]{3,2,1,0:T(8,128)} %bitcast.185), calls=%async_computation.3 | async-start | bytes 1048576 | tf_op jit(solution)/shard_map/all_to_all | solution.py:72
  119.3 7.4 %collective-permute-start = (f32[65536]{0:T(1024)S(1)}, f32[65536]{0:T(1024)S(1)}, u32[]{:S(2)}, u32[]{:S(2)}) collective-permute-start(f32[65536]{0:T(1024)S(1)} %bitcast.213), channel_id=1, source_target_pairs={{0,1},{1,0},{2,3},{3,2},{4,5},{5,4},{6,7},{7,6},{8,9},{9,8},{10,11... | collective-permute-start | bytes 786440 | tf_op jit(solution)/shard_map/ppermute | solution.py:176
  126.7 14.7 %collective-permute-start.1 = (f32[65536]{0:T(1024)S(1)}, f32[65536]{0:T(1024)S(1)}, u32[]{:S(2)}, u32[]{:S(2)}) collective-permute-start(f32[65536]{0:T(1024)S(1)} %add.401), channel_id=1, source_target_pairs={{0,2},{1,3},{2,0},{3,1},{4,6},{5,7},{6,4},{7,5},{8,10},{9,11},{10,... | collective-permute-start | bytes 786440 | tf_op jit(solution)/shard_map/ppermute | solution.py:176

commit v4 on v3

--- a/solution.py
+++ b/solution.py
@@ -92,19 +92,17 @@
     weighted = mass[None, :] * density
     partial = jnp.concatenate([jnp.sum(weighted, axis=1), jnp.sum(cotangent * weighted, axis=1)])
     flux = rate[None, :] * weighted
-    edges = jnp.concatenate([flux[:, -1], cotangent[:, 0]])
-    tile = jnp.zeros((8, cols), jnp.float32).at[0, :arrays].set(partial).at[1, :arrays].set(edges)
+    tile = jnp.zeros((8, cols), jnp.float32).at[0, :arrays].set(partial).at[1, :scen_dev].set(flux[:, -1])
     stacked = jnp.concatenate([weighted, cotangent], axis=0).reshape(arrays, rows, parts, cols)
     outgoing = stacked.transpose(2, 0, 1, 3).reshape(parts, arrays * rows, cols)
     outgoing = jnp.concatenate([outgoing, jnp.broadcast_to(tile, (parts, 8, cols))], axis=1)
     incoming_rows = exchange(outgoing)
     moments = jnp.sum(incoming_rows[:, arrays * rows, :arrays], axis=0)
     first, cross = moments[:scen_dev], moments[scen_dev:]
-    neighbours = incoming_rows[:, arrays * rows + 1, :arrays]
+    neighbours = incoming_rows[:, arrays * rows + 1, :scen_dev]
     behind = lax.dynamic_index_in_dim(neighbours, (place + parts - 1) % parts, keepdims=False)
-    ahead = lax.dynamic_index_in_dim(neighbours, (place + 1) % parts, keepdims=False)
     incoming = jnp.where(place > 0, behind[:scen_dev], 0.0)[:, None]
-    arriving = jnp.where(place < parts - 1, ahead[scen_dev:], 0.0)[:, None]
+    arriving = from_behind(cotangent[:, :1], "mass", -1)
     spread = incoming_rows[:, : arrays * rows].reshape(parts, arrays, rows, cols)
     spread = spread.transpose(1, 0, 2, 3).reshape(arrays, half_rows, cols)
     half = block // 2

time: 143 us -> 128 us (0.90)
  the two profiles are of different devices: /device:TPU:27 before, /device:TPU:0 now
where the time goes in v4:
time: 128 us
  waiting for transfers between devices  35.9 us (28%)
  other arithmetic  25.1 us (20%)
  starting transfers between devices  23 us (18%)
  matrix products  21.2 us (17%)
  local copies, waits for them, and re-layouts  19.3 us (15%)
  between operations  3.1 us (2%)
    all_to_all x4, waiting for transfers between devices, exchange(): return lax.all_to_all(value, 'mass', 0, 0, tiled=True)  29.7 us
    all_to_all x4, starting transfers between devices, exchange(): return lax.all_to_all(value, 'mass', 0, 0, tiled=True)  17.4 us
    ppermute x2, waiting for transfers between devices, shards(): rate_gradient = rate_gradient + lax.ppermute(rate_gradient, 'scen', pairs)  5.89 us
    dot_general x4, matrix products, complex_dot(): jnp.einsum(form, table_im, val_im, precision=high)  5.72 us
    unnamed x41, local copies, waits for them, and re-layouts  5.63 us
    sub x2, other arithmetic, complex_mul(): left[0] * right[0] - left[1] * right[1]  5.47 us
    dot_general x4, matrix products, complex_dot(): jnp.einsum(form, table_re, val_re, precision=high)  4.86 us
    dot_general x4, matrix products, complex_dot(): jnp.einsum(form, table_im, val_re, precision=high)  4.67 us
  transfers between devices with their start and end apart: 7, of which 7 were waited for; matrix products, arithmetic and copies ran while one was open for 9% of the time, Pallas kernels for 0%

profile of v4, /device:TPU:0, one launch (start us, length us, event | category | flops | bytes accessed | tf_op | source)
XLA Modules:
  0.0 127.6 jit_solution(17834761042464320971)
XLA Ops:
  0.6 1.2 slice.138
  1.8 1.3 %collective-permute-start = (f32[1,1]{1,0:T(1,128)}, f32[1,1]{1,0:T(1,128)}, u32[]{:S(2)}, u32[]{:S(2)}) collective-permute-start(f32[1,1]{1,0:T(1,128)} %slice.138), channel_id=1, source_target_pairs={{4,0},{8,4},{12,8},{16,12},{20,16},{24,20},{28,24},{5,1},{9,5},{13... | collective-permute-start | bytes 20 | tf_op jit(solution)/shard_map/ppermute | solution.py:19
  3.1 1.6 %slice.137 = f32[1,65535]{1,0:T(1,128)S(1)} slice(f32[1,65536]{1,0:T(1,128)} %param.9), slice={[0:1], [1:65536]} | slice | bytes 524280 | tf_op jit(solution)/shard_map/slice | solution.py:159
  5.1 2.1 %fusion.29 = (f32[1,65536]{1,0:T(1,128)}, f32[1,65536]{1,0:T(1,128)S(1)}) fusion(f32[1,65536]{1,0:T(1,128)S(1)} %copy-done, f32[1,1]{1,0:T(1,128)} %collective-permute-done, f32[1,65535]{1,0:T(1,128)S(1)} %slice.137, f32[1,65536]{1,0:T(1,128)S(1)} %copy-done.8, s32[]{:T(128)S(6)} %mul.831), kind=kLoop, calls=%fused_computation.91 | loop fusion | flops 524288 | bytes 1310724 | tf_op jit(solution)/shard_map/mul | solution.py:167
  8.1 1.3 %fusion.193 = (f32[]{:T(128)}, f32[]{:T(128)}, f32[1,65536]{1,0:T(1,128)S(1)}) fusion(f32[1,65536]{1,0:T(1,128)S(1)} %get-tuple-element.30, f32[1,65536]{1,0:T(1,128)S(1)} %copy-done, f32[1,65536]{1,0:T(1,128)S(1)} %bitcast.195), kind=kLoop, calls=%fused_computation.273 | loop fusion | flops 262142 | bytes 1048584 | tf_op jit(solution)/shard_map/reduce_sum | solution.py:93
  10.5 1.4 %maximum_bitcast_fusion.6 = f32[1,2]{1,0:T(1,128)S(1)} fusion(f32[1]{0:T(128)} %bitcast.6, f32[1]{0:T(128)} %bitcast.5), kind=kLoop, calls=%fused_computation.201 | loop fusion | flops 2 | bytes 16 | tf_op jit(solution)/shard_map/reshape.104
  13.6 6.2 %all-to-all-start = ((f32[8,40,512]{2,1,0:T(8,128)}), f32[8,40,512]{2,1,0:T(8,128)S(1)}, u32[]{:S(2)}, u32[]{:S(2)}) async-start(f32[8,40,512]{2,1,0:T(8,128)} %pad_maximum_fusion.6), calls=%async_computation | async-start | bytes 1310720 | tf_op jit(solution)/shard_map/all_to_all | solution.py:72
  21.1 9.8 %all-to-all-done = f32[8,40,512]{2,1,0:T(8,128)S(1)} async-done(((f32[8,40,512]{2,1,0:T(8,128)}), f32[8,40,512]{2,1,0:T(8,128)S(1)}, u32[]{:S(2)}, u32[]{:S(2)}) %all-to-all-start) | async-done | bytes 655392 | tf_op jit(solution)/shard_map/all_to_all | solution.py:72
  32.1 2.4 %multiply_subtract_fusion.3 = (f32[1,1,256,512]{3,2,0,1:T(8,128)S(1)}, f32[1,1,256,512]{3,2,0,1:T(8,128)S(1)}) fusion(f32[2,1,256,512]{3,2,0,1:T(8,128)S(1)} %convolution_bitcast_fusion, s32[512]{0:T(512)S(1)} %iota_add_fusion, s32[256]{0:T(256)S(1)} %copy-done.12), kind=kLoop, calls=%fused_computation.74 | loop fusion | flops 2752512 | bytes 2100224 | tf_op jit(solution)/shard_map/sub | solution.py:46
  35.5 3.7 %all-to-all-start.1 = ((f32[8,2,1,32,512]{4,3,2,1,0:T(8,128)}), f32[8,2,1,32,512]{4,3,2,1,0:T(8,128)S(1)}, u32[]{:S(2)}, u32[]{:S(2)}) async-start(f32[8,2,1,32,512]{4,3,2,1,0:T(8,128)} %maximum_bitcast_fusion), calls=%async_computation.1 | async-start | bytes 2097152 | tf_op jit(solution)/shard_map/all_to_all | solution.py:72
  43.1 11.3 %all-to-all-done.1 = f32[8,2,1,32,512]{4,3,2,1,0:T(8,128)S(1)} async-done(((f32[8,2,1,32,512]{4,3,2,1,0:T(8,128)}), f32[8,2,1,32,512]{4,3,2,1,0:T(8,128)S(1)}, u32[]{:S(2)}, u32[]{:S(2)}) %all-to-all-start.1) | async-done | bytes 1048608 | tf_op jit(solution)/shard_map/all_to_all | solution.py:72
  56.6 1.3 %copy.31 = f32[1,1,32,8,512]{4,3,2,1,0:T(8,128)S(1)} copy(f32[1,1,32,8,512]{4,2,1,0,3:T(8,128)} %get-tuple-element.41) | data formatting | bytes 1048576 | tf_op jit(solution)/shard_map/slice | solution.py:136
  62.6 1.1 fusion.5
  67.1 1.2 fusion.28
  68.3 1.2 fusion.27
  69.6 1.2 convolution_add_fusion
  70.8 1.2 convolution_subtract_fusion
  76.5 1.5 %fusion.33 = f32[32,128,32]{1,2,0:T(8,128)} fusion(f32[32,32,128]{2,1,0:T(8,128)S(1)} %convolution_add_fusion.3, f32[32,32,128]{2,1,0:T(8,128)S(1)} %convolution_subtract_fusion.3, f32[32,128]{1,0:T(8,128)S(1)} %copy-done.6, f32[32,128]{1,0:T(8,128)S(1)} %get-tuple-element.65), kind=kOutput, calls=%fused_computation.106 | convolution fusion | flops 50739200 | bytes 1605632 | tf_op jit(solution)/shard_map/pa,...pb->...ab/dot_general | solution.py:36
  78.0 1.5 %fusion.2 = f32[1,32,32,128]{3,2,1,0:T(8,128)} fusion(f32[32,128,32]{1,2,0:T(8,128)S(1)} %fusion.34, f32[32,32,128]{2,1,0:T(8,128)S(1)} %convolution_add_fusion.3, f32[32,32,128]{2,1,0:T(8,128)S(1)} %convolution_subtract_fusion.3, f32[32,128]{1,0:T(8,128)S(1)} %copy-done.6, f32[32,128]{1,0:T(8,128)S(1)} %get-tuple-element.65), kind=kOutput, calls=%fused_computation.8 | convolution fusion | flops 50870272 | bytes 2129920 | tf_op jit(solution)/shard_map/pa,...pb->...ab/dot_general | solution.py:39
  79.5 1.1 reshape.1377
  80.7 2.6 %fusion.3 = f32[1,32,32,128]{3,2,1,0:T(8,128)} fusion(f32[32,128,32]{1,2,0:T(8,128)} %fusion.33, f32[32,32,128]{2,1,0:T(8,128)S(1)} %convolution_add_fusion.3, f32[32,32,128]{2,1,0:T(8,128)S(1)} %convolution_subtract_fusion.3, f32[32,128]{1,0:T(8,128)} %fusion.119, f32[32,128]{1,0:T(8,128)S(1)} %get-tuple-element.65), kind=kOutput, calls=%fused_computation.10 | convolution fusion | flops 50870272 | bytes 2129920 | tf_op jit(solution)/shard_map/pa,...pb->...ab/dot_general | solution.py:36
  83.2 1.1 reshape.1376
  84.4 3.1 %multiply_subtract_fusion.1 = (f32[1,1,32,8,512]{4,2,1,0,3:T(8,128)S(1)}, f32[1,1,32,8,512]{4,2,1,0,3:T(8,128)S(1)}) fusion(f32[1,1,32,8,512]{4,3,2,1,0:T(8,128)S(1)} %reshape.1377, f32[1,1,32,8,512]{4,3,2,1,0:T(8,128)S(1)} %reshape.1376, s32[8,512]{1,0:T(8,128)S(1)} %copy-done.11, s32[32]{0:T(128)} %and_select_fusion.1), kind=kLoop, calls=%fused_computation.65 | loop fusion | flops 2621440 | bytes 2113664 | tf_op jit(solution)/shard_map/sub | solution.py:46
  88.6 3.7 %all-to-all-start.2 = ((f32[8,2,1,32,512]{4,3,2,1,0:T(8,128)}), f32[8,2,1,32,512]{4,3,2,1,0:T(8,128)S(1)}, u32[]{:S(2)}, u32[]{:S(2)}) async-start(f32[8,2,1,32,512]{4,3,2,1,0:T(8,128)} %maximum_bitcast_fusion.1), calls=%async_computation.2 | async-start | bytes 2097152 | tf_op jit(solution)/shard_map/all_to_all | solution.py:72
  92.3 1.7 %collective-permute-start.1 = (f32[65536]{0:T(1024)S(1)}, f32[65536]{0:T(1024)S(1)}, u32[]{:S(2)}, u32[]{:S(2)}) collective-permute-start(f32[65536]{0:T(1024)S(1)} %bitcast.207), channel_id=1, source_target_pairs={{0,1},{1,0},{2,3},{3,2},{4,5},{5,4},{6,7},{7,6},{8,9},{9,8},{10,11... | collective-permute-start | bytes 786440 | tf_op jit(solution)/shard_map/ppermute | solution.py:174
  95.4 5.6 %collective-permute-done.1 = f32[65536]{0:T(1024)S(1)} collective-permute-done((f32[65536]{0:T(1024)S(1)}, f32[65536]{0:T(1024)S(1)}, u32[]{:S(2)}, u32[]{:S(2)}) %collective-permute-start.1) | collective-permute-done | bytes 262176 | tf_op jit(solution)/shard_map/ppermute | solution.py:174
  101.0 2.7 %collective-permute-start.2 = (f32[65536]{0:T(1024)S(1)}, f32[65536]{0:T(1024)S(1)}, u32[]{:S(2)}, u32[]{:S(2)}) collective-permute-start(f32[65536]{0:T(1024)S(1)} %add.389), channel_id=1, source_target_pairs={{0,2},{1,3},{2,0},{3,1},{4,6},{5,7},{6,4},{7,5},{8,10},{9,11},{10,... | collective-permute-start | bytes 786440 | tf_op jit(solution)/shard_map/ppermute | solution.py:174
  103.7 4.0 %all-to-all-done.2 = f32[8,2,1,32,512]{4,3,2,1,0:T(8,128)S(1)} async-done(((f32[8,2,1,32,512]{4,3,2,1,0:T(8,128)}), f32[8,2,1,32,512]{4,3,2,1,0:T(8,128)S(1)}, u32[]{:S(2)}, u32[]{:S(2)}) %all-to-all-start.2) | async-done | bytes 1048608 | tf_op jit(solution)/shard_map/all_to_all | solution.py:72
  110.6 3.8 %all-to-all-start.3 = ((f32[8,2,16,512]{3,2,1,0:T(8,128)}), f32[8,2,16,512]{3,2,1,0:T(8,128)S(1)}, u32[]{:S(2)}, u32[]{:S(2)}) async-start(f32[8,2,16,512]{3,2,1,0:T(8,128)} %bitcast.180), calls=%async_computation.3 | async-start | bytes 1048576 | tf_op jit(solution)/shard_map/all_to_all | solution.py:72
  119.2 4.6 %all-to-all-done.3 = f32[8,2,16,512]{3,2,1,0:T(8,128)S(1)} async-done(((f32[8,2,16,512]{3,2,1,0:T(8,128)}), f32[8,2,16,512]{3,2,1,0:T(8,128)S(1)}, u32[]{:S(2)}, u32[]{:S(2)}) %all-to-all-start.3) | async-done | bytes 524320 | tf_op jit(solution)/shard_map/all_to_all | solution.py:72
  124.8 1.5 %add_multiply_fusion.2 = f32[1,65536]{1,0:T(1,128)} fusion(f32[1,65536]{1,0:T(1,128)S(1)} %bitcast.213, f32[1,65536]{1,0:T(1,128)S(1)} %bitcast.196, f32[1,65536]{1,0:T(1,128)S(1)} %copy-done, f32[1,65536]{1,0:T(1,128)S(1)} %bitcast.212, f32[]{:T(128)} %bitcast.63, f32[]{:T(128)} %bitcast.59, s32[]{:T(128)S(6)} %mul.831), kind=kLoop, calls=%fused_computation.94 | loop fusion | flops 720896 | bytes 1310732 | tf_op jit(solution)/shard_map/mul | solution.py:160
  126.3 1.3 %maximum_add_fusion = f32[1,65536]{1,0:T(1,128)} fusion(f32[1,65535]{1,0:T(1,128)S(1)} %bitcast.197, f32[1,1]{1,0:T(1,128)} %bitcast.62, f32[1,65536]{1,0:T(1,128)S(1)} %get-tuple-element.48, f32[1,65536]{1,0:T(1,128)S(1)} %bitcast.211, f32[1,65536]{1,0:T(1,128)S(1)} %get-tuple-element.30, f32[]{:T(128)} %bitcast.59), kind=kLoop, calls=%fused_computation.88 | loop fusion | flops 327680 | bytes 1310724 | tf_op jit(solution)/shard_map/add | solution.py:158
  (97 shorter events, 35.1 us)
Async XLA Ops:
  1.8 3.3 %collective-permute-start = (f32[1,1]{1,0:T(1,128)}, f32[1,1]{1,0:T(1,128)}, u32[]{:S(2)}, u32[]{:S(2)}) collective-permute-start(f32[1,1]{1,0:T(1,128)} %slice.138), channel_id=1, source_target_pairs={{4,0},{8,4},{12,8},{16,12},{20,16},{24,20},{28,24},{5,1},{9,5},{13... | collective-permute-start | bytes 20 | tf_op jit(solution)/shard_map/ppermute | solution.py:19
  3.1 2.0 %copy-start = (f32[1,65536]{1,0:T(1,128)S(1)}, f32[1,65536]{1,0:T(1,128)}, u32[]{:S(2)}) copy-start(f32[1,65536]{1,0:T(1,128)} %param.9) | copy-start | bytes 786436
  3.1 2.0 %copy-start.8 = (f32[1,65536]{1,0:T(1,128)S(1)}, f32[1,65536]{1,0:T(1,128)}, u32[]{:S(2)}) copy-start(f32[1,65536]{1,0:T(1,128)} %param.8) | copy-start | bytes 786436
  7.2 0.9 copy-start.1
  13.6 17.4 %all-to-all-start = ((f32[8,40,512]{2,1,0:T(8,128)}), f32[8,40,512]{2,1,0:T(8,128)S(1)}, u32[]{:S(2)}, u32[]{:S(2)}) async-start(f32[8,40,512]{2,1,0:T(8,128)} %pad_maximum_fusion.6), calls=%async_computation | async-start | bytes 1310720 | tf_op jit(solution)/shard_map/all_to_all | solution.py:72
  19.8 0.7 copy-start.12
  35.5 18.9 %all-to-all-start.1 = ((f32[8,2,1,32,512]{4,3,2,1,0:T(8,128)}), f32[8,2,1,32,512]{4,3,2,1,0:T(8,128)S(1)}, u32[]{:S(2)}, u32[]{:S(2)}) async-start(f32[8,2,1,32,512]{4,3,2,1,0:T(8,128)} %maximum_bitcast_fusion), calls=%async_computation.1 | async-start | bytes 2097152 | tf_op jit(solution)/shard_map/all_to_all | solution.py:72
  59.9 1.0 copy-start.2
  61.1 0.7 copy-start.9
  61.1 0.7 copy-start.10
  61.2 0.7 copy-start.14
  61.2 0.7 copy-start.15
  65.9 1.1 copy-start.7
  75.0 0.8 copy-start.6
  83.2 1.2 copy-start.11
  88.6 3.7 %copy-start.3 = (f32[1,65536]{1,0:T(1,128)S(1)}, f32[1,65536]{1,0:T(1,128)}, u32[]{:S(2)}) copy-start(f32[1,65536]{1,0:T(1,128)} %get-tuple-element.29) | copy-start | bytes 786436
  88.6 19.0 %all-to-all-start.2 = ((f32[8,2,1,32,512]{4,3,2,1,0:T(8,128)}), f32[8,2,1,32,512]{4,3,2,1,0:T(8,128)S(1)}, u32[]{:S(2)}, u32[]{:S(2)}) async-start(f32[8,2,1,32,512]{4,3,2,1,0:T(8,128)} %maximum_bitcast_fusion.1), calls=%async_computation.2 | async-start | bytes 2097152 | tf_op jit(solution)/shard_map/all_to_all | solution.py:72
  92.3 1.7 %copy-start.13 = (s32[256]{0:T(256)S(1)}, s32[256]{0:T(256)}, u32[]{:S(2)}) copy-start(s32[256]{0:T(256)} %constant.249.clone) | copy-start | bytes 3076
  92.3 8.6 %collective-permute-start.1 = (f32[65536]{0:T(1024)S(1)}, f32[65536]{0:T(1024)S(1)}, u32[]{:S(2)}, u32[]{:S(2)}) collective-permute-start(f32[65536]{0:T(1024)S(1)} %bitcast.207), channel_id=1, source_target_pairs={{0,1},{1,0},{2,3},{3,2},{4,5},{5,4},{6,7},{7,6},{8,9},{9,8},{10,11... | collective-permute-start | bytes 786440 | tf_op jit(solution)/shard_map/ppermute | solution.py:174
  101.0 14.3 %collective-permute-start.2 = (f32[65536]{0:T(1024)S(1)}, f32[65536]{0:T(1024)S(1)}, u32[]{:S(2)}, u32[]{:S(2)}) collective-permute-start(f32[65536]{0:T(1024)S(1)} %add.389), channel_id=1, source_target_pairs={{0,2},{1,3},{2,0},{3,1},{4,6},{5,7},{6,4},{7,5},{8,10},{9,11},{10,... | collective-permute-start | bytes 786440 | tf_op jit(solution)/shard_map/ppermute | solution.py:174
  107.6 1.0 copy-start.4
  107.6 1.0 copy-start.5
  110.6 13.2 %all-to-all-start.3 = ((f32[8,2,16,512]{3,2,1,0:T(8,128)}), f32[8,2,16,512]{3,2,1,0:T(8,128)S(1)}, u32[]{:S(2)}, u32[]{:S(2)}) async-start(f32[8,2,16,512]{3,2,1,0:T(8,128)} %bitcast.180), calls=%async_computation.3 | async-start | bytes 1048576 | tf_op jit(solution)/shard_map/all_to_all | solution.py:72

commit v5 on v2

--- a/solution.py
+++ b/solution.py
@@ -4,6 +4,8 @@
 import numpy as np
 import jax.numpy as jnp
 from jax import lax
+from jax.experimental import pallas as pl
+from jax.experimental.pallas import tpu as pltpu
 from jax.sharding import PartitionSpec as P
 
 C1 = 32
@@ -66,6 +68,143 @@
     cos_one, sin_one = phases(counting(C1), counting(C1), C1)
     result = complex_dot("pa,...pb->...ab", (cos_one, sin_one), turned)
     return (result[0].reshape(lead + (C1 * C2,)), result[1].reshape(lead + (C1 * C2,)))
+
+
+LANES = 128
+
+
+def butterfly(values, sign):
+    count = len(values)
+    if count == 1:
+        return list(values)
+    even = butterfly(values[0::2], sign)
+    odd = butterfly(values[1::2], sign)
+    out = [None] * count
+    for k in range(count // 2):
+        o_re, o_im = odd[k]
+        if k == 0:
+            t = (o_re, o_im)
+        elif 4 * k == count:
+            t = (-sign * o_im, sign * o_re)
+        else:
+            c = math.cos(2.0 * math.pi * k / count)
+            s = sign * math.sin(2.0 * math.pi * k / count)
+            t = (o_re * c - o_im * s, o_re * s + o_im * c)
+        e_re, e_im = even[k]
+        out[k] = (e_re + t[0], e_im + t[1])
+        out[k + count // 2] = (e_re - t[0], e_im - t[1])
+    return out
+
+
+def column_kernel(x_ref, phi_ref, tw1_ref, tw2_ref, back_ref, flag_ref, dft_ref, o_ref):
+    parts, _, scen_dev, block, cols = x_ref.shape
+    tiles = cols // LANES
+    half = block // 2
+    high = lax.Precision.HIGHEST
+    keep = flag_ref[0] > 0.5
+    plain = flag_ref[1] > 0.5
+    dft_cos = dft_ref[0]
+    dft_sin = dft_ref[1]
+
+    def cmul(a, b):
+        return (a[0] * b[0] - a[1] * b[1], a[0] * b[1] + a[1] * b[0])
+
+    def transform(grid, sign):
+        stage = [butterfly([grid[src][t] for src in range(parts)], sign) for t in range(tiles)]
+        turned = []
+        for k1 in range(parts):
+            row = []
+            for t in range(tiles):
+                w = (tw1_ref[0, k1 * tiles + t], sign * tw1_ref[1, k1 * tiles + t])
+                row.append(cmul(stage[t][k1], w))
+            mixed = butterfly(row, sign)
+            turned.append([cmul(mixed[m1], (tw2_ref[0, m1], sign * tw2_ref[1, m1])) for m1 in range(tiles)])
+        flat_re = jnp.concatenate([turned[k][m][0] for k in range(parts) for m in range(tiles)], axis=0)
+        flat_im = jnp.concatenate([turned[k][m][1] for k in range(parts) for m in range(tiles)], axis=0)
+        dot = lambda a, b: jnp.dot(a, b, precision=high, preferred_element_type=jnp.float32)
+        out_re = dot(flat_re, dft_cos) - sign * dot(flat_im, dft_sin)
+        out_im = dot(flat_im, dft_cos) + sign * dot(flat_re, dft_sin)
+        return out_re, out_im
+
+    def inverse(flat, sign):
+        dot = lambda a, b: jnp.dot(a, b, precision=high, preferred_element_type=jnp.float32)
+        f_re, f_im = flat
+        b_re = dot(f_re, dft_cos) - sign * dot(f_im, dft_sin)
+        b_im = dot(f_im, dft_cos) + sign * dot(f_re, dft_sin)
+        piece = lambda a, k, m: a[(k * tiles + m) * block:(k * tiles + m + 1) * block]
+        stage = []
+        for k1 in range(parts):
+            row = [cmul((piece(b_re, k1, m), piece(b_im, k1, m)), (tw2_ref[0, m], sign * tw2_ref[1, m]))
+                   for m in range(tiles)]
+            mixed = butterfly(row, sign)
+            stage.append([cmul(mixed[t], (tw1_ref[0, k1 * tiles + t], sign * tw1_ref[1, k1 * tiles + t]))
+                          for t in range(tiles)])
+        grid = [butterfly([stage[k1][t] for k1 in range(parts)], sign) for t in range(tiles)]
+        return grid
+
+    for sc in range(scen_dev):
+        w_grid, c_grid = [], []
+        for src in range(parts):
+            w_row, c_row = [], []
+            for t in range(tiles):
+                lanes = slice(t * LANES, (t + 1) * LANES)
+                t_re = x_ref[src, 0, sc, :, lanes]
+                t_im = x_ref[src, 1, sc, :, lanes]
+                swap_re = jnp.concatenate([t_re[half:], t_re[:half]], axis=0)
+                swap_im = jnp.concatenate([t_im[half:], t_im[:half]], axis=0)
+                p_re = jnp.where(keep, t_re, swap_re)
+                p_im = jnp.where(keep, t_im, swap_im)
+                f_re = jnp.where(plain, 1.0, phi_ref[0, src * tiles + t])
+                f_im = jnp.where(plain, 0.0, -phi_ref[1, src * tiles + t])
+                u_re = p_re * f_re + p_im * f_im
+                u_im = p_re * f_im - p_im * f_re
+                w_row.append((0.5 * (t_re + u_re), 0.5 * (t_im + u_im)))
+                c_row.append((0.5 * (t_im - u_im), 0.5 * (u_re - t_re)))
+            w_grid.append(w_row)
+            c_grid.append(c_row)
+        dist = transform(w_grid, -1.0)
+        cot = transform(c_grid, -1.0)
+        birth = cmul(dist, dist)
+        adjoint = cmul(cot, (dist[0], -dist[1]))
+        joined = (birth[0] - adjoint[1], birth[1] + adjoint[0])
+        grid = inverse(joined, 1.0)
+        for src in range(parts):
+            for t in range(tiles):
+                lanes = slice(t * LANES, (t + 1) * LANES)
+                value = cmul(grid[t][src], (back_ref[0, src * tiles + t], back_ref[1, src * tiles + t]))
+                o_ref[src, 0, sc, :, lanes] = value[0]
+                o_ref[src, 1, sc, :, lanes] = value[1]
+
+
+def column_stage(received, own_rows, place, nfft):
+    parts, _, scen_dev, block, cols = received.shape
+    tiles = cols // LANES
+    width = parts * cols
+    half = block // 2
+    pos = counting(block)
+    lane = counting(LANES)
+    chunk = counting(parts * tiles)
+    base = (chunk * LANES)[:, None] + lane[None, :]
+    phi = jnp.stack(phases(jnp.ones((1,), jnp.int32), base.reshape(-1), width)).reshape(2, parts * tiles, 1, LANES)
+    k1 = chunk // tiles
+    within = (chunk % tiles) * LANES
+    tw1 = jnp.stack(phases(jnp.ones((1,), jnp.int32), ((within[:, None] + lane[None, :]) * k1[:, None]).reshape(-1), width))
+    tw1 = tw1.reshape(2, parts * tiles, 1, LANES)
+    tw2 = jnp.stack(phases(counting(tiles), lane, cols)).reshape(2, tiles, 1, LANES)
+    back = jnp.stack(phases(own_rows, counting(width), nfft))
+    back = back.reshape(2, block, parts * tiles, LANES).transpose(0, 2, 1, 3)
+    lead = place == 0
+    keep = jnp.broadcast_to((lead & ((pos == 0) | (pos == half)))[:, None], (block, LANES))
+    plain = jnp.broadcast_to((lead & (pos == 0))[:, None], (block, LANES))
+    flags = jnp.stack([keep, plain]).astype(jnp.float32)
+    dft = jnp.stack(phases(lane, lane, LANES))
+    vmem = pl.BlockSpec(memory_space=pltpu.VMEM)
+    return pl.pallas_call(
+        column_kernel,
+        out_shape=jax.ShapeDtypeStruct(received.shape, jnp.float32),
+        in_specs=[vmem] * 7,
+        out_specs=vmem,
+    )(received, phi, tw1, tw2, back, flags, dft)
 
 
 def exchange(value):
@@ -117,29 +256,7 @@
     tw_cos, tw_sin = phases(order, column_index, nfft)
     twisted = jnp.stack(complex_mul((freq[0], freq[1]), (tw_cos, -tw_sin)))
     twisted = twisted.reshape(2, scen_dev, parts, block, cols).transpose(2, 0, 1, 3, 4)
-    moved = exchange(twisted).transpose(1, 2, 3, 0, 4).reshape(2, scen_dev, block, width)
-    lead = place == 0
-    keep = (lead & ((pos == 0) | (pos == half)))[:, None]
-    partner_re = jnp.where(keep, moved[0], jnp.roll(moved[0], half, axis=1))
-    partner_im = jnp.where(keep, moved[1], jnp.roll(moved[1], half, axis=1))
-    shift_cos, shift_sin = phases(jnp.ones((1,), jnp.int32), counting(width), width)
-    plain = (lead & (pos == 0))[:, None]
-    shift_cos = jnp.where(plain, 1.0, shift_cos)
-    shift_sin = jnp.where(plain, 0.0, shift_sin)
-    mirror_re = partner_re * shift_cos - partner_im * shift_sin
-    mirror_im = -partner_re * shift_sin - partner_im * shift_cos
-    split_re = jnp.concatenate([0.5 * (moved[0] + mirror_re), 0.5 * (moved[1] - mirror_im)], axis=0)
-    split_im = jnp.concatenate([0.5 * (moved[1] + mirror_im), 0.5 * (mirror_re - moved[0])], axis=0)
-    spec_re, spec_im = column_forward((split_re, split_im))
-    dist_spec = (spec_re[:scen_dev], spec_im[:scen_dev])
-    cot_spec = (spec_re[scen_dev:], spec_im[scen_dev:])
-    birth_spec = complex_mul(dist_spec, dist_spec)
-    adjoint_spec = complex_mul(cot_spec, (dist_spec[0], -dist_spec[1]))
-    joined = (birth_spec[0] - adjoint_spec[1], birth_spec[1] + adjoint_spec[0])
-    inverted = column_inverse(joined)
-    back_cos, back_sin = phases(own_rows, counting(width), nfft)
-    untwisted = jnp.stack(complex_mul(inverted, (back_cos, back_sin)))
-    untwisted = untwisted.reshape(2, scen_dev, block, parts, cols).transpose(3, 0, 1, 2, 4)
+    untwisted = column_stage(exchange(twisted), own_rows, place, nfft)
     returned = exchange(untwisted).transpose(1, 2, 0, 3, 4).reshape(2, scen_dev, full_rows, cols)
     inv_cos, inv_sin = phases(counting(half_rows), order, full_rows)
     inverse_rows = jnp.stack([jnp.stack([inv_cos, -inv_sin], axis=1), jnp.stack([inv_sin, inv_cos], axis=1)])

time: 125 us -> 109 us (0.87)
  matrix products: 20 us -> 2.12 us
  Pallas kernels: 0 us -> 11 us
  local copies, waits for them, and re-layouts: 12.9 us -> 7.42 us
  other arithmetic: 25.8 us -> 22.9 us
    dot_general x16 -> x0, matrix products: 17.9 us -> none  [the longest x4 5.37 us: complex_dot(): jnp.einsum(form, table_im, val_im, precision=high)]
    pallas_call x0 -> x1, Pallas kernels: none -> 11 us  [column_stage(): pl.pallas_call(column_kernel, out_shape=jax.ShapeDtypeStruct(received.sha...]
    sub x2 -> x1, other arithmetic: 5.47 us -> 2.36 us  [complex_mul(): left[0] * right[0] - left[1] * right[1]]
    another operation x1 -> x5, other arithmetic: 1.37 us -> 3.92 us
    cos x1 -> x3, other arithmetic: 0.69 us -> 3.04 us  [phases(): return (jnp.cos(angle), jnp.sin(angle))]
    reshape x2 -> x0, local copies, waits for them, and re-layouts: 2.28 us -> none  [the longest x1 1.14 us: column_inverse(): result[0].reshape(lead + (C1 * C2,))]
    unnamed x35 -> x13, local copies, waits for them, and re-layouts: 3.33 us -> 1.72 us
  transfers between devices with their start and end apart: 8 -> 8, of which waited for: 8 -> 6; matrix products, arithmetic and copies ran while one was open for 10% -> 14% of each run, Pallas kernels for 0% -> 0%
where the time goes in v5:
time: 109 us; the launch traced here: 107 us
  waiting for transfers between devices  36.7 us (34%)
  starting transfers between devices  25 us (23%)
  other arithmetic  22.9 us (21%)
  Pallas kernels  11 us (10%)
  local copies, waits for them, and re-layouts  7.42 us (7%)
  between operations  2.22 us (2%)
  matrix products  2.12 us (2%)
    all_to_all x4, waiting for transfers between devices, exchange(): return lax.all_to_all(value, 'mass', 0, 0, tiled=True)  29.5 us
    all_to_all x4, starting transfers between devices, exchange(): return lax.all_to_all(value, 'mass', 0, 0, tiled=True)  17.6 us
    pallas_call x1, Pallas kernels, column_stage(): pl.pallas_call(column_kernel, out_shape=jax.ShapeDtypeStruct(received.sha...  11 us
    ppermute x2, waiting for transfers between devices, shards(): rate_gradient = rate_gradient + lax.ppermute(rate_gradient, 'scen', pairs)  7.18 us
    ppermute x2, starting transfers between devices, shards(): rate_gradient = rate_gradient + lax.ppermute(rate_gradient, 'scen', pairs)  4.3 us
    ppermute x2, starting transfers between devices, from_behind(): lax.ppermute(value, axis, [(source, source + steps) for source in range(f...  3.15 us
    cos x3, other arithmetic, phases(): return (jnp.cos(angle), jnp.sin(angle))  3.04 us
    sub x1, other arithmetic, complex_mul(): left[0] * right[0] - left[1] * right[1]  2.36 us
  transfers between devices with their start and end apart: 8, of which 6 were waited for; matrix products, arithmetic and copies ran while one was open for 14% of the time, Pallas kernels for 0%

profile of v5, /device:TPU:0, one launch (start us, length us, event | category | flops | bytes accessed | tf_op | source)
XLA Modules:
  0.0 107.4 jit_solution(13153736884558603434)
XLA Ops:
  0.6 1.2 %slice.65 = f32[1,1]{1,0:T(1,128)} slice(f32[1,65536]{1,0:T(1,128)} %param.7), slice={[0:1], [0:1]} | slice | bytes 8 | tf_op jit(solution)/shard_map/slice | solution.py:273
  1.8 1.3 %collective-permute-start.1 = (f32[1,1]{1,0:T(1,128)}, f32[1,1]{1,0:T(1,128)}, u32[]{:S(2)}, u32[]{:S(2)}) collective-permute-start(f32[1,1]{1,0:T(1,128)} %slice.65), channel_id=1, source_target_pairs={{4,0},{8,4},{12,8},{16,12},{20,16},{24,20},{28,24},{5,1},{9,5},{13... | collective-permute-start | bytes 20 | tf_op jit(solution)/shard_map/ppermute | solution.py:21
  3.2 1.6 %slice.64 = f32[1,65535]{1,0:T(1,128)S(1)} slice(f32[1,65536]{1,0:T(1,128)} %param.7), slice={[0:1], [1:65536]} | slice | bytes 524280 | tf_op jit(solution)/shard_map/slice | solution.py:274
  7.3 1.4 %fusion.13 = (f32[1,65536]{1,0:T(1,128)S(1)}, f32[1,65536]{1,0:T(1,128)S(1)}) fusion(f32[1,65536]{1,0:T(1,128)S(1)} %copy-done, f32[1,1]{1,0:T(1,128)} %collective-permute-done.1, f32[1,65535]{1,0:T(1,128)S(1)} %slice.64, f32[1,65536]{1,0:T(1,128)S(1)} %copy-done.3, s32[]{:T(128)S(6)} %mul.481), kind=kLoop, calls=%fused_computation.43 | loop fusion | flops 524288 | bytes 1310724 | tf_op jit(solution)/shard_map/mul | solution.py:282
  8.7 1.2 %fusion.60 = (f32[]{:T(128)}, f32[]{:T(128)}) fusion(f32[1,65536]{1,0:T(1,128)S(1)} %get-tuple-element.18, f32[1,65536]{1,0:T(1,128)S(1)} %copy-done), kind=kLoop, calls=%fused_computation.139 | loop fusion | flops 196606 | bytes 524296 | tf_op jit(solution)/shard_map/reduce_sum | solution.py:232
  10.8 1.4 %maximum_bitcast_fusion.6 = f32[1,2]{1,0:T(1,128)S(1)} fusion(f32[1]{0:T(128)} %bitcast.6, f32[1]{0:T(128)} %bitcast.5), kind=kLoop, calls=%fused_computation.134 | loop fusion | flops 2 | bytes 16 | tf_op jit(solution)/shard_map/reshape.48
  12.2 0.9 pad_maximum_fusion
  13.1 6.4 %all-to-all-start = ((f32[8,40,512]{2,1,0:T(8,128)}), f32[8,40,512]{2,1,0:T(8,128)S(1)}, u32[]{:S(2)}, u32[]{:S(2)}) async-start(f32[8,40,512]{2,1,0:T(8,128)} %pad_maximum_fusion), calls=%async_computation | async-start | bytes 1310720 | tf_op jit(solution)/shard_map/all_to_all | solution.py:211
  20.1 10.6 %all-to-all-done = f32[8,40,512]{2,1,0:T(8,128)S(1)} async-done(((f32[8,40,512]{2,1,0:T(8,128)}), f32[8,40,512]{2,1,0:T(8,128)S(1)}, u32[]{:S(2)}, u32[]{:S(2)}) %all-to-all-start) | async-done | bytes 655392 | tf_op jit(solution)/shard_map/all_to_all | solution.py:211
  30.8 1.0 convolution_bitcast_fusion
  31.8 2.4 %multiply_subtract_fusion = (f32[1,1,256,512]{3,2,0,1:T(8,128)S(1)}, f32[1,1,256,512]{3,2,0,1:T(8,128)S(1)}) fusion(f32[2,1,256,512]{3,2,0,1:T(8,128)S(1)} %convolution_bitcast_fusion, s32[512]{0:T(512)S(1)} %iota_add_fusion, s32[256]{0:T(256)S(1)} %copy-done.4), kind=kLoop, calls=%fused_computation.32 | loop fusion | flops 2752512 | bytes 2100224 | tf_op jit(solution)/shard_map/sub | solution.py:48
  34.2 1.1 maximum_bitcast_fusion
  35.3 3.7 %all-to-all-start.1 = ((f32[8,2,1,32,512]{4,3,2,1,0:T(8,128)}), f32[8,2,1,32,512]{4,3,2,1,0:T(8,128)S(1)}, u32[]{:S(2)}, u32[]{:S(2)}) async-start(f32[8,2,1,32,512]{4,3,2,1,0:T(8,128)} %maximum_bitcast_fusion), calls=%async_computation.1 | async-start | bytes 2097152 | tf_op jit(solution)/shard_map/all_to_all | solution.py:211
  41.4 2.1 %fusion.15 = (f32[1,32,32,128]{3,1,2,0:T(8,128)S(1)}, f32[1,32,32,128]{3,1,2,0:T(8,128)S(1)}) fusion(s32[32,128]{1,0:T(8,128)S(1)} %multiply_add_fusion.1, s32[32]{0:T(128)S(1)} %and_select_fusion.1), kind=kLoop, calls=%fused_computation.48 | loop fusion | flops 1835008 | bytes 1065088 | tf_op jit(solution)/shard_map/cos | solution.py:27
  43.5 1.1 %maximum_bitcast_fusion.1.back_ref = f32[2,32,32,128]{3,2,1,0:T(8,128)} fusion(f32[1,32,32,128]{3,1,2,0:T(8,128)S(1)} %get-tuple-element.30, f32[1,32,32,128]{3,1,2,0:T(8,128)S(1)} %get-tuple-element.29), kind=kLoop, calls=%fused_computation.2 | loop fusion | flops 262144 | bytes 2097152 | tf_op jit(solution)/shard_map/transpose | solution.py:195
  44.6 9.6 %all-to-all-done.1.x_ref = f32[8,2,1,32,512]{4,3,2,1,0:T(8,128)S(1)} async-done(((f32[8,2,1,32,512]{4,3,2,1,0:T(8,128)}), f32[8,2,1,32,512]{4,3,2,1,0:T(8,128)S(1)}, u32[]{:S(2)}, u32[]{:S(2)}) %all-to-all-start.1) | async-done | bytes 1048608 | tf_op jit(solution)/shard_map/all_to_all | solution.py:211
  54.2 1.0 copy-done.1
  55.1 11.0 %shard_map.67 = f32[8,2,1,32,512]{4,3,2,1,0:T(8,128)} custom-call(f32[8,2,1,32,512]{4,3,2,1,0:T(8,128)} %copy-done.1, f32[2,32,1,128]{3,2,1,0:T(1,128)} %pad_maximum_fusion.3.phi_ref, f32[2,32,1,128]{3,2,1,0:T(1,128)} %pad_maximum_fusion.4.tw1_ref, f32[2,4,1,128]{3,2,1,0:T(1,128)} %bitcast.100, f32[2,32,32,128]{3,2,1,0:T(8,128)} %maximum_bitcast_fusion.1.back_ref, ...), custom_call_target="tpu_custom_call" | custom-call | tf_op jit(solution)/shard_map/pallas_call | solution.py:202
  66.1 3.8 %all-to-all-start.2 = ((f32[8,2,1,32,512]{4,3,2,1,0:T(8,128)}), f32[8,2,1,32,512]{4,3,2,1,0:T(8,128)S(1)}, u32[]{:S(2)}, u32[]{:S(2)}) async-start(f32[8,2,1,32,512]{4,3,2,1,0:T(8,128)} %shard_map.67), calls=%async_computation.2 | async-start | bytes 2097152 | tf_op jit(solution)/shard_map/all_to_all | solution.py:211
  69.9 1.6 %collective-permute-start.2 = (f32[65536]{0:T(1024)S(1)}, f32[65536]{0:T(1024)S(1)}, u32[]{:S(2)}, u32[]{:S(2)}) collective-permute-start(f32[65536]{0:T(1024)S(1)} %bitcast.90), channel_id=1, source_target_pairs={{0,1},{1,0},{2,3},{3,2},{4,5},{5,4},{6,7},{7,6},{8,9},{9,8},{10,11... | collective-permute-start | bytes 786440 | tf_op jit(solution)/shard_map/ppermute | solution.py:289
  72.1 6.2 %collective-permute-done.2 = f32[65536]{0:T(1024)S(1)} collective-permute-done((f32[65536]{0:T(1024)S(1)}, f32[65536]{0:T(1024)S(1)}, u32[]{:S(2)}, u32[]{:S(2)}) %collective-permute-start.2) | collective-permute-done | bytes 262176 | tf_op jit(solution)/shard_map/ppermute | solution.py:289
  78.3 2.7 %collective-permute-start.3 = (f32[65536]{0:T(1024)S(1)}, f32[65536]{0:T(1024)S(1)}, u32[]{:S(2)}, u32[]{:S(2)}) collective-permute-start(f32[65536]{0:T(1024)S(1)} %add.364), channel_id=1, source_target_pairs={{0,2},{1,3},{2,0},{3,1},{4,6},{5,7},{6,4},{7,5},{8,10},{9,11},{10,... | collective-permute-start | bytes 786440 | tf_op jit(solution)/shard_map/ppermute | solution.py:289
  81.0 4.0 %all-to-all-done.2 = f32[8,2,1,32,512]{4,3,2,1,0:T(8,128)S(1)} async-done(((f32[8,2,1,32,512]{4,3,2,1,0:T(8,128)}), f32[8,2,1,32,512]{4,3,2,1,0:T(8,128)S(1)}, u32[]{:S(2)}, u32[]{:S(2)}) %all-to-all-start.2) | async-done | bytes 1048608 | tf_op jit(solution)/shard_map/all_to_all | solution.py:211
  85.1 1.1 %fusion.9 = f32[512,2,128,1]{0,2,3,1:T(8,128)S(1)} fusion(f32[2,256,512,1]{2,1,0,3:T(8,128)S(1)} %bitcast.79, f32[1,128,2,256]{3,1,2,0:T(8,128)S(1)} %get-tuple-element.26, f32[1,128,2,256]{3,1,2,0:T(8,128)S(1)} %get-tuple-element.25), kind=kOutput, calls=%fused_computation.25 | convolution fusion | flops 805437440 | bytes 2097152 | tf_op jit(solution)/shard_map/orik,iskw->osrw/dot_general | solution.py:263
  86.2 0.9 copy.42
  87.1 3.6 %all-to-all-start.3 = ((f32[8,2,16,512]{3,2,1,0:T(8,128)}), f32[8,2,16,512]{3,2,1,0:T(8,128)S(1)}, u32[]{:S(2)}, u32[]{:S(2)}) async-start(f32[8,2,16,512]{3,2,1,0:T(8,128)} %bitcast.74), calls=%async_computation.3 | async-start | bytes 1048576 | tf_op jit(solution)/shard_map/all_to_all | solution.py:211
  91.4 1.0 collective-permute-done.3
  92.4 0.7 add.365
  95.1 5.3 %all-to-all-done.3 = f32[8,2,16,512]{3,2,1,0:T(8,128)S(1)} async-done(((f32[8,2,16,512]{3,2,1,0:T(8,128)}), f32[8,2,16,512]{3,2,1,0:T(8,128)S(1)}, u32[]{:S(2)}, u32[]{:S(2)}) %all-to-all-start.3) | async-done | bytes 524320 | tf_op jit(solution)/shard_map/all_to_all | solution.py:211
  100.9 1.6 %add_multiply_fusion = (f32[1,65536]{1,0:T(1,128)}, f32[1,65536]{1,0:T(1,128)S(1)}) fusion(f32[1,65536]{1,0:T(1,128)S(1)} %bitcast.97, f32[1,65536]{1,0:T(1,128)S(1)} %bitcast.96, f32[1,65536]{1,0:T(1,128)S(1)} %copy-done, f32[1,65536]{1,0:T(1,128)S(1)} %bitcast.95, f32[]{:T(128)} %bitcast.38, f32[]{:T(128)} %bitcast.36, s32[]{:T(128)S(6)} %mul.481, ...), kind=kLoop, calls=%fused_computation.46 | loop fusion | flops 786432 | bytes 1835020 | tf_op jit(solution)/shard_map/mul | solution.py:275
  103.1 1.9 %collective-permute-start = (f32[1,1]{1,0:T(1,128)}, f32[1,1]{1,0:T(1,128)}, u32[]{:S(2)}, u32[]{:S(2)}) collective-permute-start(f32[1,1]{1,0:T(1,128)} %slice.71), channel_id=1, source_target_pairs={{0,4},{4,8},{8,12},{12,16},{16,20},{20,24},{24,28},{1,5},{5,9},{9,... | collective-permute-start | bytes 20 | tf_op jit(solution)/shard_map/ppermute | solution.py:21
  105.4 2.0 %maximum_add_fusion = f32[1,65536]{1,0:T(1,128)} fusion(f32[1,65535]{1,0:T(1,128)S(1)} %bitcast.81, f32[1,1]{1,0:T(1,128)} %collective-permute-done, f32[1,65536]{1,0:T(1,128)S(1)} %get-tuple-element.24, f32[1,65536]{1,0:T(1,128)S(1)} %bitcast.94, f32[1,65536]{1,0:T(1,128)S(1)} %get-tuple-element.18, f32[]{:T(128)} %bitcast.36), kind=kLoop, calls=%fused_computation.40 | loop fusion | flops 327680 | bytes 1310724 | tf_op jit(solution)/shard_map/add | solution.py:272
  (53 shorter events, 10.0 us)
Async XLA Ops:
  1.8 5.5 %collective-permute-start.1 = (f32[1,1]{1,0:T(1,128)}, f32[1,1]{1,0:T(1,128)}, u32[]{:S(2)}, u32[]{:S(2)}) collective-permute-start(f32[1,1]{1,0:T(1,128)} %slice.65), channel_id=1, source_target_pairs={{4,0},{8,4},{12,8},{16,12},{20,16},{24,20},{28,24},{5,1},{9,5},{13... | collective-permute-start | bytes 20 | tf_op jit(solution)/shard_map/ppermute | solution.py:21
  4.8 0.7 copy-start.4
  4.9 2.4 %copy-start = (f32[1,65536]{1,0:T(1,128)S(1)}, f32[1,65536]{1,0:T(1,128)}, u32[]{:S(2)}) copy-start(f32[1,65536]{1,0:T(1,128)} %param.7) | copy-start | bytes 786436
  4.9 2.4 %copy-start.3 = (f32[1,65536]{1,0:T(1,128)S(1)}, f32[1,65536]{1,0:T(1,128)}, u32[]{:S(2)}) copy-start(f32[1,65536]{1,0:T(1,128)} %param.6) | copy-start | bytes 786436
  13.1 17.6 %all-to-all-start = ((f32[8,40,512]{2,1,0:T(8,128)}), f32[8,40,512]{2,1,0:T(8,128)S(1)}, u32[]{:S(2)}, u32[]{:S(2)}) async-start(f32[8,40,512]{2,1,0:T(8,128)} %pad_maximum_fusion), calls=%async_computation | async-start | bytes 1310720 | tf_op jit(solution)/shard_map/all_to_all | solution.py:211
  35.3 18.9 %all-to-all-start.1 = ((f32[8,2,1,32,512]{4,3,2,1,0:T(8,128)}), f32[8,2,1,32,512]{4,3,2,1,0:T(8,128)S(1)}, u32[]{:S(2)}, u32[]{:S(2)}) async-start(f32[8,2,1,32,512]{4,3,2,1,0:T(8,128)} %maximum_bitcast_fusion), calls=%async_computation.1 | async-start | bytes 2097152 | tf_op jit(solution)/shard_map/all_to_all | solution.py:211
  54.2 1.0 copy-start.1
  66.1 18.9 %all-to-all-start.2 = ((f32[8,2,1,32,512]{4,3,2,1,0:T(8,128)}), f32[8,2,1,32,512]{4,3,2,1,0:T(8,128)S(1)}, u32[]{:S(2)}, u32[]{:S(2)}) async-start(f32[8,2,1,32,512]{4,3,2,1,0:T(8,128)} %shard_map.67), calls=%async_computation.2 | async-start | bytes 2097152 | tf_op jit(solution)/shard_map/all_to_all | solution.py:211
  69.9 8.4 %collective-permute-start.2 = (f32[65536]{0:T(1024)S(1)}, f32[65536]{0:T(1024)S(1)}, u32[]{:S(2)}, u32[]{:S(2)}) collective-permute-start(f32[65536]{0:T(1024)S(1)} %bitcast.90), channel_id=1, source_target_pairs={{0,1},{1,0},{2,3},{3,2},{4,5},{5,4},{6,7},{7,6},{8,9},{9,8},{10,11... | collective-permute-start | bytes 786440 | tf_op jit(solution)/shard_map/ppermute | solution.py:289
  78.3 14.1 %collective-permute-start.3 = (f32[65536]{0:T(1024)S(1)}, f32[65536]{0:T(1024)S(1)}, u32[]{:S(2)}, u32[]{:S(2)}) collective-permute-start(f32[65536]{0:T(1024)S(1)} %add.364), channel_id=1, source_target_pairs={{0,2},{1,3},{2,0},{3,1},{4,6},{5,7},{6,4},{7,5},{8,10},{9,11},{10,... | collective-permute-start | bytes 786440 | tf_op jit(solution)/shard_map/ppermute | solution.py:289
  87.1 3.6 %copy-start.2 = (f32[65536]{0:T(1024)S(1)}, f32[65536]{0:T(1024)}, u32[]{:S(2)}) copy-start(f32[65536]{0:T(1024)} %param.8) | copy-start | bytes 786436
  87.1 13.3 %all-to-all-start.3 = ((f32[8,2,16,512]{3,2,1,0:T(8,128)}), f32[8,2,16,512]{3,2,1,0:T(8,128)S(1)}, u32[]{:S(2)}, u32[]{:S(2)}) async-start(f32[8,2,16,512]{3,2,1,0:T(8,128)} %bitcast.74), calls=%async_computation.3 | async-start | bytes 1048576 | tf_op jit(solution)/shard_map/all_to_all | solution.py:211
  103.1 2.3 %collective-permute-start = (f32[1,1]{1,0:T(1,128)}, f32[1,1]{1,0:T(1,128)}, u32[]{:S(2)}, u32[]{:S(2)}) collective-permute-start(f32[1,1]{1,0:T(1,128)} %slice.71), channel_id=1, source_target_pairs={{0,4},{4,8},{8,12},{12,16},{16,20},{20,24},{24,28},{1,5},{5,9},{9,... | collective-permute-start | bytes 20 | tf_op jit(solution)/shard_map/ppermute | solution.py:21

commit v6 on v5

--- a/solution.py
+++ b/solution.py
@@ -230,13 +230,17 @@
     mass = ((offset + counting(bin_dev)).astype(jnp.float32) + 0.5) / nbin
     weighted = mass[None, :] * density
     partial = jnp.concatenate([jnp.sum(weighted, axis=1), jnp.sum(cotangent * weighted, axis=1)])
-    tile = jnp.zeros((8, cols), jnp.float32).at[0, :arrays].set(partial)
+    flux = rate[None, :] * weighted
+    tile = jnp.zeros((8, cols), jnp.float32).at[0, :arrays].set(partial).at[1, :scen_dev].set(flux[:, -1])
     stacked = jnp.concatenate([weighted, cotangent], axis=0).reshape(arrays, rows, parts, cols)
     outgoing = stacked.transpose(2, 0, 1, 3).reshape(parts, arrays * rows, cols)
     outgoing = jnp.concatenate([outgoing, jnp.broadcast_to(tile, (parts, 8, cols))], axis=1)
     incoming_rows = exchange(outgoing)
     moments = jnp.sum(incoming_rows[:, arrays * rows, :arrays], axis=0)
     first, cross = moments[:scen_dev], moments[scen_dev:]
+    neighbours = incoming_rows[:, arrays * rows + 1, :scen_dev]
+    behind = lax.dynamic_index_in_dim(neighbours, (place + parts - 1) % parts, keepdims=False)
+    incoming = jnp.where(place > 0, behind, 0.0)[:, None]
     spread = incoming_rows[:, : arrays * rows].reshape(parts, arrays, rows, cols)
     spread = spread.transpose(1, 0, 2, 3).reshape(arrays, half_rows, cols)
     half = block // 2
@@ -253,7 +257,7 @@
     packed = spread.reshape(2, scen_dev, half_rows, cols)
     freq = jnp.einsum("okir,isrw->oskw", forward_rows, packed, precision=high)
     column_index = place * cols + counting(cols)
-    tw_cos, tw_sin = phases(order, column_index, nfft)
+    tw_cos, tw_sin = lax.optimization_barrier(phases(order, column_index, nfft))
     twisted = jnp.stack(complex_mul((freq[0], freq[1]), (tw_cos, -tw_sin)))
     twisted = twisted.reshape(2, scen_dev, parts, block, cols).transpose(2, 0, 1, 3, 4)
     untwisted = column_stage(exchange(twisted), own_rows, place, nfft)
@@ -266,8 +270,6 @@
     gathered = exchange(real_part).transpose(1, 2, 0, 3).reshape(arrays, bin_dev) / nfft
     birth = gathered[:scen_dev]
     corr = gathered[scen_dev:]
-    flux = rate[None, :] * weighted
-    incoming = from_behind(flux[:, -1:], "mass", 1)
     inflow = jnp.concatenate([incoming, flux[:, :-1]], axis=1)
     tendency = 0.5 * beta * birth - beta * first[:, None] * weighted - flux + inflow
     arriving = from_behind(cotangent[:, :1], "mass", -1)

time: 109 us -> 111 us (1.018)
  local copies, waits for them, and re-layouts: 7.42 us -> 11.7 us
  waiting for transfers between devices: 36.7 us -> 32.7 us
  other arithmetic: 22.9 us -> 26.4 us
  starting transfers between devices: 25 us -> 23.1 us
    unnamed x13 -> x27, local copies, waits for them, and re-layouts: 1.72 us -> 4.63 us
    all_to_all x4, waiting for transfers between devices: 29.5 us -> 27 us  [exchange(): return lax.all_to_all(value, 'mass', 0, 0, tiled=True)]
    sin x3 -> x4, other arithmetic: 0.92 us -> 3.03 us  [phases(): return (jnp.cos(angle), jnp.sin(angle))]
    sub x1, other arithmetic: 2.36 us -> 0.27 us  [complex_mul(): left[0] * right[0] - left[1] * right[1]]
    ppermute x2 -> x1, starting transfers between devices: 3.15 us -> 1.28 us  [from_behind(): lax.ppermute(value, axis, [(source, source + steps) for source in range(f...]
    ppermute x2, waiting for transfers between devices: 7.18 us -> 5.65 us  [shards(): rate_gradient = rate_gradient + lax.ppermute(rate_gradient, 'scen', pairs)]
  transfers between devices with their start and end apart: 8 -> 7, of which waited for: 6 -> 6; matrix products, arithmetic and copies ran while one was open for 14% -> 20% of each run, Pallas kernels for 0% -> 0%
where the time goes in v6:
time: 111 us; the launch traced here: 110 us
  waiting for transfers between devices  32.7 us (29%)
  other arithmetic  26.4 us (24%)
  starting transfers between devices  23.1 us (21%)
  local copies, waits for them, and re-layouts  11.7 us (11%)
  Pallas kernels  10.9 us (10%)
  between operations  2.83 us (3%)
  matrix products  2.12 us (2%)
    all_to_all x4, waiting for transfers between devices, exchange(): return lax.all_to_all(value, 'mass', 0, 0, tiled=True)  27 us
    all_to_all x4, starting transfers between devices, exchange(): return lax.all_to_all(value, 'mass', 0, 0, tiled=True)  17.5 us
    pallas_call x1, Pallas kernels, column_stage(): pl.pallas_call(column_kernel, out_shape=jax.ShapeDtypeStruct(received.sha...  10.9 us
    ppermute x2, waiting for transfers between devices, shards(): rate_gradient = rate_gradient + lax.ppermute(rate_gradient, 'scen', pairs)  5.65 us
    unnamed x27, local copies, waits for them, and re-layouts  4.63 us
    ppermute x2, starting transfers between devices, shards(): rate_gradient = rate_gradient + lax.ppermute(rate_gradient, 'scen', pairs)  4.3 us
    cos x3, other arithmetic, phases(): return (jnp.cos(angle), jnp.sin(angle))  3.04 us
    sin x4, other arithmetic, phases(): return (jnp.cos(angle), jnp.sin(angle))  3.03 us
  transfers between devices with their start and end apart: 7, of which 6 were waited for; matrix products, arithmetic and copies ran while one was open for 20% of the time, Pallas kernels for 0%

profile of v6, /device:TPU:0, one launch (start us, length us, event | category | flops | bytes accessed | tf_op | source)
XLA Modules:
  0.0 109.8 jit_solution(4330569787489192961)
XLA Ops:
  0.6 1.2 %slice.88 = f32[1,1]{1,0:T(1,128)} slice(f32[1,65536]{1,0:T(1,128)} %param.9), slice={[0:1], [0:1]} | slice | bytes 8 | tf_op jit(solution)/shard_map/slice | solution.py:275
  1.8 1.3 %collective-permute-start = (f32[1,1]{1,0:T(1,128)}, f32[1,1]{1,0:T(1,128)}, u32[]{:S(2)}, u32[]{:S(2)}) collective-permute-start(f32[1,1]{1,0:T(1,128)} %slice.88), channel_id=1, source_target_pairs={{4,0},{8,4},{12,8},{16,12},{20,16},{24,20},{28,24},{5,1},{9,5},{13... | collective-permute-start | bytes 20 | tf_op jit(solution)/shard_map/ppermute | solution.py:21
  3.1 1.6 %slice.87 = f32[1,65535]{1,0:T(1,128)S(1)} slice(f32[1,65536]{1,0:T(1,128)} %param.9), slice={[0:1], [1:65536]} | slice | bytes 524280 | tf_op jit(solution)/shard_map/slice | solution.py:276
  5.9 2.1 %fusion.17 = (f32[256,512]{1,0:T(8,128)S(1)}, f32[256,512]{1,0:T(8,128)S(1)}) fusion(s32[512]{0:T(512)S(1)} %iota_add_fusion, s32[256]{0:T(256)S(1)} %copy-done.8), kind=kLoop, calls=%fused_computation.50 | loop fusion | flops 1835008 | bytes 1051648 | tf_op jit(solution)/shard_map/sin | solution.py:27
  11.2 1.4 %fusion.14 = (f32[1,65536]{1,0:T(1,128)S(1)}, f32[1,65536]{1,0:T(1,128)S(1)}) fusion(f32[1,65536]{1,0:T(1,128)S(1)} %copy-done, f32[1,1]{1,0:T(1,128)} %collective-permute-done, f32[1,65535]{1,0:T(1,128)S(1)} %slice.87, f32[1,65536]{1,0:T(1,128)S(1)} %copy-done.6, s32[]{:T(128)S(6)} %mul.447), kind=kLoop, calls=%fused_computation.44 | loop fusion | flops 524288 | bytes 1310724 | tf_op jit(solution)/shard_map/mul | solution.py:284
  13.6 1.3 %fusion.62 = (f32[]{:T(128)}, f32[]{:T(128)}, f32[1,65536]{1,0:T(1,128)S(1)}) fusion(f32[1,65536]{1,0:T(1,128)S(1)} %get-tuple-element.34, f32[1,65536]{1,0:T(1,128)S(1)} %copy-done, f32[1,65536]{1,0:T(1,128)S(1)} %bitcast.99), kind=kLoop, calls=%fused_computation.142 | loop fusion | flops 262142 | bytes 1048584 | tf_op jit(solution)/shard_map/reduce_sum | solution.py:232
  16.0 1.4 %maximum_bitcast_fusion.6 = f32[1,2]{1,0:T(1,128)S(1)} fusion(f32[1]{0:T(128)} %bitcast.6, f32[1]{0:T(128)} %bitcast.5), kind=kLoop, calls=%fused_computation.136 | loop fusion | flops 2 | bytes 16 | tf_op jit(solution)/shard_map/reshape.79
  18.1 0.9 pad_maximum_fusion
  19.0 6.4 %all-to-all-start = ((f32[8,40,512]{2,1,0:T(8,128)}), f32[8,40,512]{2,1,0:T(8,128)S(1)}, u32[]{:S(2)}, u32[]{:S(2)}) async-start(f32[8,40,512]{2,1,0:T(8,128)} %pad_maximum_fusion), calls=%async_computation | async-start | bytes 1310720 | tf_op jit(solution)/shard_map/all_to_all | solution.py:211
  27.4 9.1 %all-to-all-done = f32[8,40,512]{2,1,0:T(8,128)S(1)} async-done(((f32[8,40,512]{2,1,0:T(8,128)}), f32[8,40,512]{2,1,0:T(8,128)S(1)}, u32[]{:S(2)}, u32[]{:S(2)}) %all-to-all-start) | async-done | bytes 655392 | tf_op jit(solution)/shard_map/all_to_all | solution.py:211
  36.7 0.9 copy-done.5
  37.6 1.0 fusion.6
  38.9 1.1 maximum_bitcast_fusion
  39.9 3.9 %all-to-all-start.1 = ((f32[8,2,1,32,512]{4,3,2,1,0:T(8,128)}), f32[8,2,1,32,512]{4,3,2,1,0:T(8,128)S(1)}, u32[]{:S(2)}, u32[]{:S(2)}) async-start(f32[8,2,1,32,512]{4,3,2,1,0:T(8,128)} %maximum_bitcast_fusion), calls=%async_computation.1 | async-start | bytes 2097152 | tf_op jit(solution)/shard_map/all_to_all | solution.py:211
  45.9 2.1 %fusion.16 = (f32[1,32,32,128]{3,1,2,0:T(8,128)S(1)}, f32[1,32,32,128]{3,1,2,0:T(8,128)S(1)}) fusion(s32[32,128]{1,0:T(8,128)S(1)} %multiply_add_fusion.1, s32[32]{0:T(128)S(1)} %copy-done.10), kind=kLoop, calls=%fused_computation.49 | loop fusion | flops 1835008 | bytes 1065088 | tf_op jit(solution)/shard_map/cos | solution.py:27
  48.0 1.1 maximum_bitcast_fusion.1.back_ref
  49.1 9.9 %all-to-all-done.1.x_ref = f32[8,2,1,32,512]{4,3,2,1,0:T(8,128)S(1)} async-done(((f32[8,2,1,32,512]{4,3,2,1,0:T(8,128)}), f32[8,2,1,32,512]{4,3,2,1,0:T(8,128)S(1)}, u32[]{:S(2)}, u32[]{:S(2)}) %all-to-all-start.1) | async-done | bytes 1048608 | tf_op jit(solution)/shard_map/all_to_all | solution.py:211
  59.0 1.0 copy-done.1
  60.0 10.9 %shard_map.67 = f32[8,2,1,32,512]{4,3,2,1,0:T(8,128)} custom-call(f32[8,2,1,32,512]{4,3,2,1,0:T(8,128)} %copy-done.1, f32[2,32,1,128]{3,2,1,0:T(1,128)} %pad_maximum_fusion.3.phi_ref, f32[2,32,1,128]{3,2,1,0:T(1,128)} %pad_maximum_fusion.4.tw1_ref, f32[2,4,1,128]{3,2,1,0:T(1,128)} %bitcast.120, f32[2,32,32,128]{3,2,1,0:T(8,128)} %maximum_bitcast_fusion.1.back_ref, ...), custom_call_target="tpu_custom_call" | custom-call | tf_op jit(solution)/shard_map/pallas_call | solution.py:202
  70.9 3.8 %all-to-all-start.2 = ((f32[8,2,1,32,512]{4,3,2,1,0:T(8,128)}), f32[8,2,1,32,512]{4,3,2,1,0:T(8,128)S(1)}, u32[]{:S(2)}, u32[]{:S(2)}) async-start(f32[8,2,1,32,512]{4,3,2,1,0:T(8,128)} %shard_map.67), calls=%async_computation.2 | async-start | bytes 2097152 | tf_op jit(solution)/shard_map/all_to_all | solution.py:211
  74.7 1.6 %collective-permute-start.1 = (f32[65536]{0:T(1024)S(1)}, f32[65536]{0:T(1024)S(1)}, u32[]{:S(2)}, u32[]{:S(2)}) collective-permute-start(f32[65536]{0:T(1024)S(1)} %bitcast.111), channel_id=1, source_target_pairs={{0,1},{1,0},{2,3},{3,2},{4,5},{5,4},{6,7},{7,6},{8,9},{9,8},{10,11... | collective-permute-start | bytes 786440 | tf_op jit(solution)/shard_map/ppermute | solution.py:291
  77.8 5.3 %collective-permute-done.1 = f32[65536]{0:T(1024)S(1)} collective-permute-done((f32[65536]{0:T(1024)S(1)}, f32[65536]{0:T(1024)S(1)}, u32[]{:S(2)}, u32[]{:S(2)}) %collective-permute-start.1) | collective-permute-done | bytes 262176 | tf_op jit(solution)/shard_map/ppermute | solution.py:291
  83.1 2.7 %collective-permute-start.2 = (f32[65536]{0:T(1024)S(1)}, f32[65536]{0:T(1024)}, u32[]{:S(2)}, u32[]{:S(2)}) collective-permute-start(f32[65536]{0:T(1024)S(1)} %add.365), channel_id=1, source_target_pairs={{0,2},{1,3},{2,0},{3,1},{4,6},{5,7},{6,4},{7,5},{8,10},{9,11},{10,... | collective-permute-start | bytes 786440 | tf_op jit(solution)/shard_map/ppermute | solution.py:291
  85.8 4.0 %all-to-all-done.2 = f32[8,2,1,32,512]{4,3,2,1,0:T(8,128)S(1)} async-done(((f32[8,2,1,32,512]{4,3,2,1,0:T(8,128)}), f32[8,2,1,32,512]{4,3,2,1,0:T(8,128)S(1)}, u32[]{:S(2)}, u32[]{:S(2)}) %all-to-all-start.2) | async-done | bytes 1048608 | tf_op jit(solution)/shard_map/all_to_all | solution.py:211
  89.9 0.8 copy-done.3
  90.9 1.1 fusion.10
  91.9 0.9 copy.42
  92.8 3.5 %all-to-all-start.3 = ((f32[8,2,16,512]{3,2,1,0:T(8,128)}), f32[8,2,16,512]{3,2,1,0:T(8,128)S(1)}, u32[]{:S(2)}, u32[]{:S(2)}) async-start(f32[8,2,16,512]{3,2,1,0:T(8,128)} %bitcast.91), calls=%async_computation.3 | async-start | bytes 1048576 | tf_op jit(solution)/shard_map/all_to_all | solution.py:211
  97.3 1.7 %add.366 = f32[65536]{0:T(1024)} add(f32[65536]{0:T(1024)S(1)} %add.365, f32[65536]{0:T(1024)} %collective-permute-done.2) | non-fusion elementwise | flops 65536 | bytes 786432 | tf_op jit(solution)/shard_map/add | solution.py:291
  102.0 4.0 %all-to-all-done.3 = f32[8,2,16,512]{3,2,1,0:T(8,128)S(1)} async-done(((f32[8,2,16,512]{3,2,1,0:T(8,128)}), f32[8,2,16,512]{3,2,1,0:T(8,128)S(1)}, u32[]{:S(2)}, u32[]{:S(2)}) %all-to-all-start.3) | async-done | bytes 524320 | tf_op jit(solution)/shard_map/all_to_all | solution.py:211
  107.0 1.5 %add_multiply_fusion = f32[1,65536]{1,0:T(1,128)} fusion(f32[1,65536]{1,0:T(1,128)S(1)} %bitcast.117, f32[1,65536]{1,0:T(1,128)S(1)} %bitcast.100, f32[1,65536]{1,0:T(1,128)S(1)} %copy-done, f32[1,65536]{1,0:T(1,128)S(1)} %bitcast.116, f32[]{:T(128)} %bitcast.44, f32[]{:T(128)} %bitcast.40, s32[]{:T(128)S(6)} %mul.447), kind=kLoop, calls=%fused_computation.47 | loop fusion | flops 720896 | bytes 1310732 | tf_op jit(solution)/shard_map/mul | solution.py:277
  108.5 1.3 %maximum_add_fusion = f32[1,65536]{1,0:T(1,128)} fusion(f32[1,65535]{1,0:T(1,128)S(1)} %bitcast.101, f32[1,1]{1,0:T(1,128)} %bitcast.43, f32[1,65536]{1,0:T(1,128)S(1)} %get-tuple-element.39, f32[1,65536]{1,0:T(1,128)S(1)} %bitcast.115, f32[1,65536]{1,0:T(1,128)S(1)} %get-tuple-element.34, f32[]{:T(128)} %bitcast.40), kind=kLoop, calls=%fused_computation.41 | loop fusion | flops 327680 | bytes 1310724 | tf_op jit(solution)/shard_map/add | solution.py:274
  (69 shorter events, 16.3 us)
Async XLA Ops:
  1.8 9.4 %collective-permute-start = (f32[1,1]{1,0:T(1,128)}, f32[1,1]{1,0:T(1,128)}, u32[]{:S(2)}, u32[]{:S(2)}) collective-permute-start(f32[1,1]{1,0:T(1,128)} %slice.88), channel_id=1, source_target_pairs={{4,0},{8,4},{12,8},{16,12},{20,16},{24,20},{28,24},{5,1},{9,5},{13... | collective-permute-start | bytes 20 | tf_op jit(solution)/shard_map/ppermute | solution.py:21
  5.3 0.7 copy-start.8
  5.9 5.3 %copy-start = (f32[1,65536]{1,0:T(1,128)S(1)}, f32[1,65536]{1,0:T(1,128)}, u32[]{:S(2)}) copy-start(f32[1,65536]{1,0:T(1,128)} %param.9) | copy-start | bytes 786436
  5.9 5.3 %copy-start.6 = (f32[1,65536]{1,0:T(1,128)S(1)}, f32[1,65536]{1,0:T(1,128)}, u32[]{:S(2)}) copy-start(f32[1,65536]{1,0:T(1,128)} %param.8) | copy-start | bytes 786436
  12.6 1.0 copy-start.2
  19.0 17.6 %all-to-all-start = ((f32[8,40,512]{2,1,0:T(8,128)}), f32[8,40,512]{2,1,0:T(8,128)S(1)}, u32[]{:S(2)}, u32[]{:S(2)}) async-start(f32[8,40,512]{2,1,0:T(8,128)} %pad_maximum_fusion), calls=%async_computation | async-start | bytes 1310720 | tf_op jit(solution)/shard_map/all_to_all | solution.py:211
  26.0 0.8 copy-start.11
  36.6 1.0 copy-start.5
  39.9 3.9 %copy-start.7 = (f32[1,32,1,128]{3,1,2,0:T(8,128)S(1)}, f32[1,32,1,128]{3,1,2,0:T(8,128)}, u32[]{:S(2)}) copy-start(f32[1,32,1,128]{3,1,2,0:T(8,128)} %fusion.47) | copy-start | bytes 49156
  39.9 19.0 %all-to-all-start.1 = ((f32[8,2,1,32,512]{4,3,2,1,0:T(8,128)}), f32[8,2,1,32,512]{4,3,2,1,0:T(8,128)S(1)}, u32[]{:S(2)}, u32[]{:S(2)}) async-start(f32[8,2,1,32,512]{4,3,2,1,0:T(8,128)} %maximum_bitcast_fusion), calls=%async_computation.1 | async-start | bytes 2097152 | tf_op jit(solution)/shard_map/all_to_all | solution.py:211
  45.2 0.7 copy-start.10
  59.0 1.0 copy-start.1
  70.9 18.9 %all-to-all-start.2 = ((f32[8,2,1,32,512]{4,3,2,1,0:T(8,128)}), f32[8,2,1,32,512]{4,3,2,1,0:T(8,128)S(1)}, u32[]{:S(2)}, u32[]{:S(2)}) async-start(f32[8,2,1,32,512]{4,3,2,1,0:T(8,128)} %shard_map.67), calls=%async_computation.2 | async-start | bytes 2097152 | tf_op jit(solution)/shard_map/all_to_all | solution.py:211
  74.7 1.7 %copy-start.9 = (s32[256]{0:T(256)S(1)}, s32[256]{0:T(256)}, u32[]{:S(2)}) copy-start(s32[256]{0:T(256)} %constant.253.clone) | copy-start | bytes 3076
  74.7 8.4 %collective-permute-start.1 = (f32[65536]{0:T(1024)S(1)}, f32[65536]{0:T(1024)S(1)}, u32[]{:S(2)}, u32[]{:S(2)}) collective-permute-start(f32[65536]{0:T(1024)S(1)} %bitcast.111), channel_id=1, source_target_pairs={{0,1},{1,0},{2,3},{3,2},{4,5},{5,4},{6,7},{7,6},{8,9},{9,8},{10,11... | collective-permute-start | bytes 786440 | tf_op jit(solution)/shard_map/ppermute | solution.py:291
  83.1 14.1 %collective-permute-start.2 = (f32[65536]{0:T(1024)S(1)}, f32[65536]{0:T(1024)}, u32[]{:S(2)}, u32[]{:S(2)}) collective-permute-start(f32[65536]{0:T(1024)S(1)} %add.365), channel_id=1, source_target_pairs={{0,2},{1,3},{2,0},{3,1},{4,6},{5,7},{6,4},{7,5},{8,10},{9,11},{10,... | collective-permute-start | bytes 786440 | tf_op jit(solution)/shard_map/ppermute | solution.py:291
  89.8 1.0 copy-start.3
  89.8 1.0 copy-start.4
  92.8 13.2 %all-to-all-start.3 = ((f32[8,2,16,512]{3,2,1,0:T(8,128)}), f32[8,2,16,512]{3,2,1,0:T(8,128)S(1)}, u32[]{:S(2)}, u32[]{:S(2)}) async-start(f32[8,2,16,512]{3,2,1,0:T(8,128)} %bitcast.91), calls=%async_computation.3 | async-start | bytes 1048576 | tf_op jit(solution)/shard_map/all_to_all | solution.py:211

commit v7 on v6

--- a/solution.py
+++ b/solution.py
@@ -182,22 +182,26 @@
     width = parts * cols
     half = block // 2
     pos = counting(block)
-    lane = counting(LANES)
-    chunk = counting(parts * tiles)
-    base = (chunk * LANES)[:, None] + lane[None, :]
-    phi = jnp.stack(phases(jnp.ones((1,), jnp.int32), base.reshape(-1), width)).reshape(2, parts * tiles, 1, LANES)
-    k1 = chunk // tiles
-    within = (chunk % tiles) * LANES
-    tw1 = jnp.stack(phases(jnp.ones((1,), jnp.int32), ((within[:, None] + lane[None, :]) * k1[:, None]).reshape(-1), width))
+
+    def table(angle):
+        return jnp.asarray(np.stack([np.cos(angle), np.sin(angle)]), jnp.float32)
+
+    lane = np.arange(LANES)
+    chunk = np.arange(parts * tiles)
+    spots = chunk[:, None] * LANES + lane[None, :]
+    phi = table(2.0 * np.pi * spots / width).reshape(2, parts * tiles, 1, LANES)
+    tw1 = table(2.0 * np.pi * (((chunk % tiles) * LANES)[:, None] + lane[None, :]) * (chunk // tiles)[:, None] / width)
     tw1 = tw1.reshape(2, parts * tiles, 1, LANES)
-    tw2 = jnp.stack(phases(counting(tiles), lane, cols)).reshape(2, tiles, 1, LANES)
-    back = jnp.stack(phases(own_rows, counting(width), nfft))
-    back = back.reshape(2, block, parts * tiles, LANES).transpose(0, 2, 1, 3)
+    tw2 = table(2.0 * np.pi * np.arange(tiles)[:, None] * lane[None, :] / cols).reshape(2, tiles, 1, LANES)
+    dft = table(2.0 * np.pi * ((lane[:, None] * lane[None, :]) % LANES) / LANES)
+    coarse = phases(own_rows, counting(parts * tiles) * LANES, nfft)
+    fine = phases(own_rows, counting(LANES), nfft)
+    back = complex_mul((coarse[0].T[:, :, None], coarse[1].T[:, :, None]), (fine[0][None], fine[1][None]))
+    back = jnp.stack(back)
     lead = place == 0
     keep = jnp.broadcast_to((lead & ((pos == 0) | (pos == half)))[:, None], (block, LANES))
     plain = jnp.broadcast_to((lead & (pos == 0))[:, None], (block, LANES))
     flags = jnp.stack([keep, plain]).astype(jnp.float32)
-    dft = jnp.stack(phases(lane, lane, LANES))
     vmem = pl.BlockSpec(memory_space=pltpu.VMEM)
     return pl.pallas_call(
         column_kernel,
@@ -251,18 +255,25 @@
     order = np.where(table < half, half * np.arange(parts)[:, None] + table,
                      (full_rows - half * np.arange(parts)[:, None] - (table - half)) % full_rows)
     order[0, half] = full_rows // 2
-    order = jnp.asarray(order.reshape(-1), jnp.int32)
-    row_cos, row_sin = phases(order, counting(half_rows), full_rows)
+    order_np = order.reshape(-1)
+    order = jnp.asarray(order_np, jnp.int32)
+    row_angle = 2.0 * np.pi * ((order_np[:, None] * np.arange(half_rows)[None, :]) % full_rows) / full_rows
+    row_cos, row_sin = jnp.asarray(np.cos(row_angle), jnp.float32), jnp.asarray(np.sin(row_angle), jnp.float32)
     forward_rows = jnp.stack([jnp.stack([row_cos, row_sin], axis=1), jnp.stack([-row_sin, row_cos], axis=1)])
     packed = spread.reshape(2, scen_dev, half_rows, cols)
     freq = jnp.einsum("okir,isrw->oskw", forward_rows, packed, precision=high)
-    column_index = place * cols + counting(cols)
-    tw_cos, tw_sin = lax.optimization_barrier(phases(order, column_index, nfft))
+    tiles = cols // LANES
+    coarse_cos, coarse_sin = phases(order, place * cols + counting(tiles) * LANES, nfft)
+    fine_angle = 2.0 * np.pi * ((order_np[:, None] * np.arange(LANES)[None, :]) % nfft) / nfft
+    fine_cos = jnp.asarray(np.cos(fine_angle), jnp.float32)[:, None, :]
+    fine_sin = jnp.asarray(np.sin(fine_angle), jnp.float32)[:, None, :]
+    tw_cos, tw_sin = complex_mul((coarse_cos[:, :, None], coarse_sin[:, :, None]), (fine_cos, fine_sin))
+    tw_cos, tw_sin = tw_cos.reshape(full_rows, cols), tw_sin.reshape(full_rows, cols)
     twisted = jnp.stack(complex_mul((freq[0], freq[1]), (tw_cos, -tw_sin)))
     twisted = twisted.reshape(2, scen_dev, parts, block, cols).transpose(2, 0, 1, 3, 4)
     untwisted = column_stage(exchange(twisted), own_rows, place, nfft)
     returned = exchange(untwisted).transpose(1, 2, 0, 3, 4).reshape(2, scen_dev, full_rows, cols)
-    inv_cos, inv_sin = phases(counting(half_rows), order, full_rows)
+    inv_cos, inv_sin = row_cos.T, row_sin.T
     inverse_rows = jnp.stack([jnp.stack([inv_cos, -inv_sin], axis=1), jnp.stack([inv_sin, inv_cos], axis=1)])
     real_part = jnp.einsum("orik,iskw->osrw", inverse_rows, returned, precision=high)
     real_part = real_part.reshape(arrays, half_rows, cols)

time: 111 us -> 106 us (0.955)
  other arithmetic: 26.4 us -> 16.9 us
  waiting for transfers between devices: 32.7 us -> 36.7 us
    another operation x7 -> x2, other arithmetic: 5.5 us -> 2.4 us
    sin x4 -> x0, other arithmetic: 3.03 us -> none  [phases(): return (jnp.cos(angle), jnp.sin(angle))]
    ppermute x2, waiting for transfers between devices: 5.65 us -> 8.52 us  [shards(): rate_gradient = rate_gradient + lax.ppermute(rate_gradient, 'scen', pairs)]
    cos x3, other arithmetic: 3.04 us -> 0.43 us  [phases(): return (jnp.cos(angle), jnp.sin(angle))]
    all_to_all x4, waiting for transfers between devices: 27 us -> 28.2 us  [exchange(): return lax.all_to_all(value, 'mass', 0, 0, tiled=True)]
    unnamed x27 -> x23, local copies, waits for them, and re-layouts: 4.63 us -> 4.53 us
  transfers between devices with their start and end apart: 7 -> 7, of which waited for: 6 -> 6; matrix products, arithmetic and copies ran while one was open for 20% -> 11% of each run, Pallas kernels for 0% -> 0%
where the time goes in v7:
time: 106 us; the launch traced here: 105 us
  waiting for transfers between devices  36.7 us (35%)
  starting transfers between devices  23.2 us (22%)
  other arithmetic  16.9 us (16%)
  local copies, waits for them, and re-layouts  12.2 us (12%)
  Pallas kernels  11 us (10%)
  between operations  2.96 us (3%)
  matrix products  2.13 us (2%)
    all_to_all x4, waiting for transfers between devices, exchange(): return lax.all_to_all(value, 'mass', 0, 0, tiled=True)  28.2 us
    all_to_all x4, starting transfers between devices, exchange(): return lax.all_to_all(value, 'mass', 0, 0, tiled=True)  17.6 us
    pallas_call x1, Pallas kernels, column_stage(): pl.pallas_call(column_kernel, out_shape=jax.ShapeDtypeStruct(received.sha...  11 us
    ppermute x2, waiting for transfers between devices, shards(): rate_gradient = rate_gradient + lax.ppermute(rate_gradient, 'scen', pairs)  8.52 us
    unnamed x23, local copies, waits for them, and re-layouts  4.53 us
    ppermute x2, starting transfers between devices, shards(): rate_gradient = rate_gradient + lax.ppermute(rate_gradient, 'scen', pairs)  4.3 us
    add x2, other arithmetic, shards(): rate_gradient = rate_gradient + lax.ppermute(rate_gradient, 'scen', pairs)  2.66 us
  transfers between devices with their start and end apart: 7, of which 6 were waited for; matrix products, arithmetic and copies ran while one was open for 11% of the time, Pallas kernels for 0%

profile of v7, /device:TPU:0, one launch (start us, length us, event | category | flops | bytes accessed | tf_op | source)
XLA Modules:
  0.0 105.1 jit_solution(4403768664083876910)
XLA Ops:
  0.6 1.2 %slice.88 = f32[1,1]{1,0:T(1,128)} slice(f32[1,65536]{1,0:T(1,128)} %param.17), slice={[0:1], [0:1]} | slice | bytes 8 | tf_op jit(solution)/shard_map/slice | solution.py:286
  1.8 1.3 %collective-permute-start = (f32[1,1]{1,0:T(1,128)}, f32[1,1]{1,0:T(1,128)}, u32[]{:S(2)}, u32[]{:S(2)}) collective-permute-start(f32[1,1]{1,0:T(1,128)} %slice.88), channel_id=1, source_target_pairs={{4,0},{8,4},{12,8},{16,12},{20,16},{24,20},{28,24},{5,1},{9,5},{13... | collective-permute-start | bytes 20 | tf_op jit(solution)/shard_map/ppermute | solution.py:21
  3.1 1.6 %slice.87 = f32[1,65535]{1,0:T(1,128)S(1)} slice(f32[1,65536]{1,0:T(1,128)} %param.17), slice={[0:1], [1:65536]} | slice | bytes 524280 | tf_op jit(solution)/shard_map/slice | solution.py:287
  5.7 2.0 %fusion = (f32[1,65536]{1,0:T(1,128)}, f32[1,65536]{1,0:T(1,128)S(1)}) fusion(f32[1,65536]{1,0:T(1,128)S(1)} %copy-done, f32[1,1]{1,0:T(1,128)} %collective-permute-done, f32[1,65535]{1,0:T(1,128)S(1)} %slice.87, f32[1,65536]{1,0:T(1,128)S(1)} %copy-done.6, s32[]{:T(128)S(6)} %mul.385), kind=kLoop, calls=%fused_computation.19 | loop fusion | flops 524288 | bytes 1310724 | tf_op jit(solution)/shard_map/mul | solution.py:295
  8.6 1.3 %fusion.21 = (f32[]{:T(128)}, f32[]{:T(128)}, f32[1,65536]{1,0:T(1,128)S(1)}) fusion(f32[1,65536]{1,0:T(1,128)S(1)} %get-tuple-element.30, f32[1,65536]{1,0:T(1,128)S(1)} %copy-done, f32[1,65536]{1,0:T(1,128)S(1)} %bitcast.73), kind=kLoop, calls=%fused_computation.71 | loop fusion | flops 262142 | bytes 1048584 | tf_op jit(solution)/shard_map/reduce_sum | solution.py:236
  11.0 1.4 %maximum_bitcast_fusion.1 = f32[1,2]{1,0:T(1,128)S(1)} fusion(f32[1]{0:T(128)} %bitcast.4, f32[1]{0:T(128)} %bitcast.3), kind=kLoop, calls=%fused_computation.67 | loop fusion | flops 2 | bytes 16 | tf_op jit(solution)/shard_map/reshape.79
  13.1 0.9 pad_maximum_fusion.1
  14.0 6.5 %all-to-all-start = ((f32[8,40,512]{2,1,0:T(8,128)}), f32[8,40,512]{2,1,0:T(8,128)S(1)}, u32[]{:S(2)}, u32[]{:S(2)}) async-start(f32[8,40,512]{2,1,0:T(8,128)} %pad_maximum_fusion.1), calls=%async_computation | async-start | bytes 1310720 | tf_op jit(solution)/shard_map/all_to_all | solution.py:215
  22.5 9.2 %all-to-all-done = f32[8,40,512]{2,1,0:T(8,128)S(1)} async-done(((f32[8,40,512]{2,1,0:T(8,128)}), f32[8,40,512]{2,1,0:T(8,128)S(1)}, u32[]{:S(2)}, u32[]{:S(2)}) %all-to-all-start) | async-done | bytes 655392 | tf_op jit(solution)/shard_map/all_to_all | solution.py:215
  31.8 1.0 copy-done.5
  32.8 1.1 %convolution_bitcast_fusion = f32[2,1,256,512]{3,2,0,1:T(8,128)S(1)} fusion(f32[2,128,512,1]{2,1,0,3:T(8,128)S(1)} %bitcast.81, f32[2,256,2,128]{3,1,2,0:T(8,128)S(1)} %copy-done.5), kind=kOutput, calls=%fused_computation | convolution fusion | flops 805306368 | bytes 2097152 | tf_op jit(solution)/shard_map/okir,isrw->oskw/dot_general | solution.py:264
  34.1 1.1 %maximum_bitcast_fusion = f32[8,2,1,32,512]{4,3,2,1,0:T(8,128)} fusion(f32[1,1,8,32,512]{4,3,1,0,2:T(8,128)S(1)} %bitcast.84, f32[1,1,8,32,512]{4,3,1,0,2:T(8,128)S(1)} %bitcast.83), kind=kLoop, calls=%fused_computation.1 | loop fusion | flops 262144 | bytes 2097152 | tf_op jit(solution)/shard_map/transpose | solution.py:273
  35.2 3.7 %all-to-all-start.1 = ((f32[8,2,1,32,512]{4,3,2,1,0:T(8,128)}), f32[8,2,1,32,512]{4,3,2,1,0:T(8,128)S(1)}, u32[]{:S(2)}, u32[]{:S(2)}) async-start(f32[8,2,1,32,512]{4,3,2,1,0:T(8,128)} %maximum_bitcast_fusion), calls=%async_computation.1 | async-start | bytes 2097152 | tf_op jit(solution)/shard_map/all_to_all | solution.py:215
  39.6 1.0 pad_maximum_fusion.back_ref
  40.7 13.4 %all-to-all-done.1.x_ref = f32[8,2,1,32,512]{4,3,2,1,0:T(8,128)S(1)} async-done(((f32[8,2,1,32,512]{4,3,2,1,0:T(8,128)}), f32[8,2,1,32,512]{4,3,2,1,0:T(8,128)S(1)}, u32[]{:S(2)}, u32[]{:S(2)}) %all-to-all-start.1) | async-done | bytes 1048608 | tf_op jit(solution)/shard_map/all_to_all | solution.py:215
  54.1 1.0 copy-done.1
  55.1 11.0 %shard_map.139 = f32[8,2,1,32,512]{4,3,2,1,0:T(8,128)} custom-call(f32[8,2,1,32,512]{4,3,2,1,0:T(8,128)} %copy-done.1, f32[2,32,1,128]{3,2,1,0:T(1,128)} %constant.205.phi_ref, f32[2,32,1,128]{3,2,1,0:T(1,128)} %constant.206.tw1_ref, f32[2,4,1,128]{3,2,1,0:T(1,128)} %constant.207.tw2_ref, f32[2,32,32,128]{3,2,1,0:T(8,128)} %pad_maximum_fusion.back_ref, ...), custom_call_target="tpu_custom_call" | custom-call | tf_op jit(solution)/shard_map/pallas_call | solution.py:206
  66.1 3.7 %all-to-all-start.2 = ((f32[8,2,1,32,512]{4,3,2,1,0:T(8,128)}), f32[8,2,1,32,512]{4,3,2,1,0:T(8,128)S(1)}, u32[]{:S(2)}, u32[]{:S(2)}) async-start(f32[8,2,1,32,512]{4,3,2,1,0:T(8,128)} %shard_map.139), calls=%async_computation.2 | async-start | bytes 2097152 | tf_op jit(solution)/shard_map/all_to_all | solution.py:215
  69.8 1.6 %collective-permute-start.1 = (f32[65536]{0:T(1024)S(1)}, f32[65536]{0:T(1024)}, u32[]{:S(2)}, u32[]{:S(2)}) collective-permute-start(f32[65536]{0:T(1024)S(1)} %bitcast.85), channel_id=1, source_target_pairs={{0,1},{1,0},{2,3},{3,2},{4,5},{5,4},{6,7},{7,6},{8,9},{9,8},{10,11... | collective-permute-start | bytes 786440 | tf_op jit(solution)/shard_map/ppermute | solution.py:302
  71.4 7.1 %collective-permute-done.1 = f32[65536]{0:T(1024)} collective-permute-done((f32[65536]{0:T(1024)S(1)}, f32[65536]{0:T(1024)}, u32[]{:S(2)}, u32[]{:S(2)}) %collective-permute-start.1) | collective-permute-done | bytes 262176 | tf_op jit(solution)/shard_map/ppermute | solution.py:302
  78.5 1.0 add.182
  79.5 2.7 %collective-permute-start.2 = (f32[65536]{0:T(1024)S(1)}, f32[65536]{0:T(1024)}, u32[]{:S(2)}, u32[]{:S(2)}) collective-permute-start(f32[65536]{0:T(1024)S(1)} %add.182), channel_id=1, source_target_pairs={{0,2},{1,3},{2,0},{3,1},{4,6},{5,7},{6,4},{7,5},{8,10},{9,11},{10,... | collective-permute-start | bytes 786440 | tf_op jit(solution)/shard_map/ppermute | solution.py:302
  82.1 3.0 %all-to-all-done.2 = f32[8,2,1,32,512]{4,3,2,1,0:T(8,128)S(1)} async-done(((f32[8,2,1,32,512]{4,3,2,1,0:T(8,128)}), f32[8,2,1,32,512]{4,3,2,1,0:T(8,128)S(1)}, u32[]{:S(2)}, u32[]{:S(2)}) %all-to-all-start.2) | async-done | bytes 1048608 | tf_op jit(solution)/shard_map/all_to_all | solution.py:215
  85.2 0.9 copy-done.4
  86.2 1.1 %fusion.24 = f32[512,2,128,1]{0,2,3,1:T(8,128)S(1)} fusion(f32[2,256,512,1]{2,1,0,3:T(8,128)S(1)} %bitcast.72, f32[2,128,2,256]{3,1,2,0:T(8,128)S(1)} %copy-done.4), kind=kOutput, calls=%fused_computation.73 | convolution fusion | flops 805306368 | bytes 2097152 | tf_op jit(solution)/shard_map/orik,iskw->osrw/dot_general | solution.py:278
  87.2 0.9 copy.46
  88.1 3.7 %all-to-all-start.3 = ((f32[8,2,16,512]{3,2,1,0:T(8,128)}), f32[8,2,16,512]{3,2,1,0:T(8,128)S(1)}, u32[]{:S(2)}, u32[]{:S(2)}) async-start(f32[8,2,16,512]{3,2,1,0:T(8,128)} %bitcast.67), calls=%async_computation.3 | async-start | bytes 1048576 | tf_op jit(solution)/shard_map/all_to_all | solution.py:215
  92.5 1.4 %collective-permute-done.2 = f32[65536]{0:T(1024)} collective-permute-done((f32[65536]{0:T(1024)S(1)}, f32[65536]{0:T(1024)}, u32[]{:S(2)}, u32[]{:S(2)}) %collective-permute-start.2) | collective-permute-done | bytes 262176 | tf_op jit(solution)/shard_map/ppermute | solution.py:302
  93.9 1.7 %add.183 = f32[65536]{0:T(1024)} add(f32[65536]{0:T(1024)S(1)} %add.182, f32[65536]{0:T(1024)} %collective-permute-done.2) | non-fusion elementwise | flops 65536 | bytes 786432 | tf_op jit(solution)/shard_map/add | solution.py:302
  98.7 2.6 %all-to-all-done.3 = f32[8,2,16,512]{3,2,1,0:T(8,128)S(1)} async-done(((f32[8,2,16,512]{3,2,1,0:T(8,128)}), f32[8,2,16,512]{3,2,1,0:T(8,128)S(1)}, u32[]{:S(2)}, u32[]{:S(2)}) %all-to-all-start.3) | async-done | bytes 524320 | tf_op jit(solution)/shard_map/all_to_all | solution.py:215
  102.3 1.5 %add_multiply_fusion = f32[1,65536]{1,0:T(1,128)} fusion(f32[1,65536]{1,0:T(1,128)S(1)} %bitcast.91, f32[1,65536]{1,0:T(1,128)S(1)} %bitcast.74, f32[1,65536]{1,0:T(1,128)S(1)} %copy-done, f32[1,65536]{1,0:T(1,128)S(1)} %bitcast.90, f32[]{:T(128)} %bitcast.33, f32[]{:T(128)} %bitcast.29, s32[]{:T(128)S(6)} %mul.385), kind=kLoop, calls=%fused_computation.22 | loop fusion | flops 720896 | bytes 1310732 | tf_op jit(solution)/shard_map/mul | solution.py:288
  103.8 1.3 %maximum_add_fusion = f32[1,65536]{1,0:T(1,128)} fusion(f32[1,65535]{1,0:T(1,128)S(1)} %bitcast.75, f32[1,1]{1,0:T(1,128)} %bitcast.32, f32[1,65536]{1,0:T(1,128)S(1)} %get-tuple-element.37, f32[1,65536]{1,0:T(1,128)S(1)} %bitcast.89, f32[1,65536]{1,0:T(1,128)S(1)} %get-tuple-element.30, f32[]{:T(128)} %bitcast.29), kind=kLoop, calls=%fused_computation.16 | loop fusion | flops 327680 | bytes 1310724 | tf_op jit(solution)/shard_map/add | solution.py:285
  (56 shorter events, 9.3 us)
Async XLA Ops:
  1.8 3.4 %collective-permute-start = (f32[1,1]{1,0:T(1,128)}, f32[1,1]{1,0:T(1,128)}, u32[]{:S(2)}, u32[]{:S(2)}) collective-permute-start(f32[1,1]{1,0:T(1,128)} %slice.88), channel_id=1, source_target_pairs={{4,0},{8,4},{12,8},{16,12},{20,16},{24,20},{28,24},{5,1},{9,5},{13... | collective-permute-start | bytes 20 | tf_op jit(solution)/shard_map/ppermute | solution.py:21
  3.1 1.7 %copy-start.9 = (s32[256]{0:T(256)S(1)}, s32[256]{0:T(256)}, u32[]{:S(2)}) copy-start(s32[256]{0:T(256)} %constant.183.clone) | copy-start | bytes 3076
  3.1 2.1 %copy-start.6 = (f32[1,65536]{1,0:T(1,128)S(1)}, f32[1,65536]{1,0:T(1,128)}, u32[]{:S(2)}) copy-start(f32[1,65536]{1,0:T(1,128)} %param.16) | copy-start | bytes 786436
  4.7 1.0 copy-start
  7.7 0.9 copy-start.2
  14.0 6.5 %copy-start.7 = (f32[256,128]{1,0:T(8,128)S(1)}, f32[256,128]{1,0:T(8,128)}, u32[]{:S(2)}) copy-start(f32[256,128]{1,0:T(8,128)} %constant.187.clone) | copy-start | bytes 393220
  14.0 6.5 %copy-start.8 = (f32[256,128]{1,0:T(8,128)S(1)}, f32[256,128]{1,0:T(8,128)}, u32[]{:S(2)}) copy-start(f32[256,128]{1,0:T(8,128)} %constant.186.clone) | copy-start | bytes 393220
  14.0 17.6 %all-to-all-start = ((f32[8,40,512]{2,1,0:T(8,128)}), f32[8,40,512]{2,1,0:T(8,128)S(1)}, u32[]{:S(2)}, u32[]{:S(2)}) async-start(f32[8,40,512]{2,1,0:T(8,128)} %pad_maximum_fusion.1), calls=%async_computation | async-start | bytes 1310720 | tf_op jit(solution)/shard_map/all_to_all | solution.py:215
  31.7 1.0 copy-start.5
  35.2 18.9 %all-to-all-start.1 = ((f32[8,2,1,32,512]{4,3,2,1,0:T(8,128)}), f32[8,2,1,32,512]{4,3,2,1,0:T(8,128)S(1)}, u32[]{:S(2)}, u32[]{:S(2)}) async-start(f32[8,2,1,32,512]{4,3,2,1,0:T(8,128)} %maximum_bitcast_fusion), calls=%async_computation.1 | async-start | bytes 2097152 | tf_op jit(solution)/shard_map/all_to_all | solution.py:215
  54.1 1.0 copy-start.1
  66.1 3.7 %copy-start.3 = (f32[1,65536]{1,0:T(1,128)S(1)}, f32[1,65536]{1,0:T(1,128)}, u32[]{:S(2)}) copy-start(f32[1,65536]{1,0:T(1,128)} %get-tuple-element.29) | copy-start | bytes 786436
  66.1 19.0 %all-to-all-start.2 = ((f32[8,2,1,32,512]{4,3,2,1,0:T(8,128)}), f32[8,2,1,32,512]{4,3,2,1,0:T(8,128)S(1)}, u32[]{:S(2)}, u32[]{:S(2)}) async-start(f32[8,2,1,32,512]{4,3,2,1,0:T(8,128)} %shard_map.139), calls=%async_computation.2 | async-start | bytes 2097152 | tf_op jit(solution)/shard_map/all_to_all | solution.py:215
  69.8 8.7 %collective-permute-start.1 = (f32[65536]{0:T(1024)S(1)}, f32[65536]{0:T(1024)}, u32[]{:S(2)}, u32[]{:S(2)}) collective-permute-start(f32[65536]{0:T(1024)S(1)} %bitcast.85), channel_id=1, source_target_pairs={{0,1},{1,0},{2,3},{3,2},{4,5},{5,4},{6,7},{7,6},{8,9},{9,8},{10,11... | collective-permute-start | bytes 786440 | tf_op jit(solution)/shard_map/ppermute | solution.py:302
  79.5 14.4 %collective-permute-start.2 = (f32[65536]{0:T(1024)S(1)}, f32[65536]{0:T(1024)}, u32[]{:S(2)}, u32[]{:S(2)}) collective-permute-start(f32[65536]{0:T(1024)S(1)} %add.182), channel_id=1, source_target_pairs={{0,2},{1,3},{2,0},{3,1},{4,6},{5,7},{6,4},{7,5},{8,10},{9,11},{10,... | collective-permute-start | bytes 786440 | tf_op jit(solution)/shard_map/ppermute | solution.py:302
  85.1 1.0 copy-start.4
  88.1 13.2 %all-to-all-start.3 = ((f32[8,2,16,512]{3,2,1,0:T(8,128)}), f32[8,2,16,512]{3,2,1,0:T(8,128)S(1)}, u32[]{:S(2)}, u32[]{:S(2)}) async-start(f32[8,2,16,512]{3,2,1,0:T(8,128)} %bitcast.67), calls=%async_computation.3 | async-start | bytes 1048576 | tf_op jit(solution)/shard_map/all_to_all | solution.py:215

commit v8 on v7

--- a/solution.py
+++ b/solution.py
@@ -1,3 +1,4 @@
+import functools
 import math
 
 import jax
@@ -211,6 +212,61 @@
     )(received, phi, tw1, tw2, back, flags, dft)
 
 
+def prologue_kernel(nbin, base_ref, d_ref, c_ref, r_ref, o_ref):
+    parts, _, cols = o_ref.shape
+    scen_dev = d_ref.shape[0]
+    lines = d_ref.shape[1]
+    tiles = cols // LANES
+    rows = (o_ref.shape[1] - 8) // (2 * scen_dev)
+    per_row = lines // rows
+    arrays = 2 * scen_dev
+    base = base_ref[0]
+    line = lax.broadcasted_iota(jnp.int32, (lines, LANES), 0)
+    lane = lax.broadcasted_iota(jnp.int32, (lines, LANES), 1)
+    mass = ((base + line * LANES + lane).astype(jnp.float32) + 0.5) / nbin
+    sums = []
+    flux_last = []
+    for sc in range(scen_dev):
+        weighted = mass * d_ref[sc]
+        sums.append((jnp.sum(weighted), sc))
+        sums.append((jnp.sum(c_ref[sc] * weighted), scen_dev + sc))
+        flux_last.append(r_ref[lines - 1:lines, LANES - 1:LANES] * weighted[lines - 1:lines, LANES - 1:LANES])
+    t_row = lax.broadcasted_iota(jnp.int32, (8, cols), 0)
+    t_lane = lax.broadcasted_iota(jnp.int32, (8, cols), 1)
+    tile = jnp.zeros((8, cols), jnp.float32)
+    for value, slot in sums:
+        tile = jnp.where((t_row == 0) & (t_lane == slot), value, tile)
+    for sc in range(scen_dev):
+        tile = jnp.where((t_row == 1) & (t_lane == sc), flux_last[sc], tile)
+    s_line = lax.broadcasted_iota(jnp.int32, (rows, LANES), 0)
+    s_lane = lax.broadcasted_iota(jnp.int32, (rows, LANES), 1)
+    for j in range(parts):
+        for t in range(tiles):
+            first_line = j * tiles + t
+            picked = s_line * per_row + first_line
+            part_mass = ((base + picked * LANES + s_lane).astype(jnp.float32) + 0.5) / nbin
+            for sc in range(scen_dev):
+                dens = d_ref[sc, pl.ds(first_line, rows, stride=per_row), :]
+                cot = c_ref[sc, pl.ds(first_line, rows, stride=per_row), :]
+                o_ref[j, sc * rows:(sc + 1) * rows, t * LANES:(t + 1) * LANES] = part_mass * dens
+                o_ref[j, (scen_dev + sc) * rows:(scen_dev + sc + 1) * rows, t * LANES:(t + 1) * LANES] = cot
+        o_ref[j, arrays * rows:arrays * rows + 8, :] = tile
+
+
+def prologue(density, cotangent, rate, offset, nbin, parts, rows, cols):
+    scen_dev, bin_dev = density.shape
+    lines = bin_dev // LANES
+    base = jnp.reshape(offset, (1,)).astype(jnp.int32)
+    vmem = pl.BlockSpec(memory_space=pltpu.VMEM)
+    return pl.pallas_call(
+        functools.partial(prologue_kernel, nbin),
+        out_shape=jax.ShapeDtypeStruct((parts, 2 * scen_dev * rows + 8, cols), jnp.float32),
+        in_specs=[pl.BlockSpec(memory_space=pltpu.SMEM), vmem, vmem, vmem],
+        out_specs=vmem,
+    )(base, density.reshape(scen_dev, lines, LANES), cotangent.reshape(scen_dev, lines, LANES),
+      rate.reshape(lines, LANES))
+
+
 def exchange(value):
     return lax.all_to_all(value, "mass", 0, 0, tiled=True)
 
@@ -233,12 +289,8 @@
     offset = place * bin_dev
     mass = ((offset + counting(bin_dev)).astype(jnp.float32) + 0.5) / nbin
     weighted = mass[None, :] * density
-    partial = jnp.concatenate([jnp.sum(weighted, axis=1), jnp.sum(cotangent * weighted, axis=1)])
     flux = rate[None, :] * weighted
-    tile = jnp.zeros((8, cols), jnp.float32).at[0, :arrays].set(partial).at[1, :scen_dev].set(flux[:, -1])
-    stacked = jnp.concatenate([weighted, cotangent], axis=0).reshape(arrays, rows, parts, cols)
-    outgoing = stacked.transpose(2, 0, 1, 3).reshape(parts, arrays * rows, cols)
-    outgoing = jnp.concatenate([outgoing, jnp.broadcast_to(tile, (parts, 8, cols))], axis=1)
+    outgoing = prologue(density, cotangent, rate, offset, nbin, parts, rows, cols)
     incoming_rows = exchange(outgoing)
     moments = jnp.sum(incoming_rows[:, arrays * rows, :arrays], axis=0)
     first, cross = moments[:scen_dev], moments[scen_dev:]

time: 106 us -> 114 us (1.075)
  the two profiles are of different devices: /device:TPU:0 before, /device:TPU:27 now
where the time goes in v8:
time: 114 us
  waiting for transfers between devices  52.4 us (46%)
  starting transfers between devices  22.6 us (20%)
  Pallas kernels  13.4 us (12%)
  other arithmetic  10.2 us (9%)
  local copies, waits for them, and re-layouts  9.89 us (9%)
  between operations  2.82 us (2%)
  matrix products  2.13 us (2%)
    all_to_all x4, waiting for transfers between devices, exchange(): return lax.all_to_all(value, 'mass', 0, 0, tiled=True)  33.8 us
    all_to_all x4, starting transfers between devices, exchange(): return lax.all_to_all(value, 'mass', 0, 0, tiled=True)  19.9 us
    ppermute x2, waiting for transfers between devices, shards(): rate_gradient = rate_gradient + lax.ppermute(rate_gradient, 'scen', pairs)  18.6 us
    pallas_call x1, Pallas kernels, column_stage(): pl.pallas_call(column_kernel, out_shape=jax.ShapeDtypeStruct(received.sha...  10.9 us
    unnamed x20, local copies, waits for them, and re-layouts  5.48 us
    mul x1, other arithmetic, shards(): local_grad = jnp.sum(weighted * (following - cotangent), axis=0)  2.53 us
    ppermute x1, starting transfers between devices, from_behind(): lax.ppermute(value, axis, [(source, source + steps) for source in range(f...  2.44 us
    pallas_call x1, Pallas kernels, prologue(): pl.pallas_call(functools.partial(prologue_kernel, nbin), out_shape=jax.Sh...  2.42 us
  transfers between devices with their start and end apart: 7, of which 6 were waited for; matrix products, arithmetic and copies ran while one was open for 10% of the time, Pallas kernels for 0%

profile of v8, /device:TPU:27, one launch (start us, length us, event | category | flops | bytes accessed | tf_op | source)
XLA Modules:
  0.0 113.5 jit_solution(2211168228912541706)
XLA Ops:
  0.6 2.4 %shard_map.139 = f32[8,40,512]{2,1,0:T(8,128)} custom-call(s32[1]{0:T(128)} %bitcast.1.base_ref, f32[1,512,128]{2,1,0:T(8,128)} %bitcast.69, f32[1,512,128]{2,1,0:T(8,128)} %bitcast.67, f32[512,128]{1,0:T(8,128)} %bitcast.64), custom_call_target="tpu_custom_call" | custom-call | tf_op jit(solution)/shard_map/pallas_call | solution.py:261
  3.1 4.6 %all-to-all-start = ((f32[8,40,512]{2,1,0:T(8,128)}), f32[8,40,512]{2,1,0:T(8,128)S(1)}, u32[]{:S(2)}, u32[]{:S(2)}) async-start(f32[8,40,512]{2,1,0:T(8,128)} %shard_map.139), calls=%async_computation | async-start | bytes 1310720 | tf_op jit(solution)/shard_map/all_to_all | solution.py:271
  7.6 0.7 copy-done.8
  8.8 0.6 copy-done.6
  9.4 0.7 add_negate_fusion
  10.7 0.6 add_convert_fusion.flag_ref
  11.3 5.9 %all-to-all-done = f32[8,40,512]{2,1,0:T(8,128)S(1)} async-done(((f32[8,40,512]{2,1,0:T(8,128)}), f32[8,40,512]{2,1,0:T(8,128)S(1)}, u32[]{:S(2)}, u32[]{:S(2)}) %all-to-all-start) | async-done | bytes 655392 | tf_op jit(solution)/shard_map/all_to_all | solution.py:271
  17.3 1.0 copy-done.5
  18.3 1.1 convolution_bitcast_fusion
  19.6 1.0 maximum_bitcast_fusion
  20.7 5.0 %all-to-all-start.1 = ((f32[8,2,1,32,512]{4,3,2,1,0:T(8,128)}), f32[8,2,1,32,512]{4,3,2,1,0:T(8,128)S(1)}, u32[]{:S(2)}, u32[]{:S(2)}) async-start(f32[8,2,1,32,512]{4,3,2,1,0:T(8,128)} %maximum_bitcast_fusion), calls=%async_computation.1 | async-start | bytes 2097152 | tf_op jit(solution)/shard_map/all_to_all | solution.py:271
  26.4 1.1 pad_maximum_fusion.back_ref
  27.5 12.1 %all-to-all-done.1.x_ref = f32[8,2,1,32,512]{4,3,2,1,0:T(8,128)S(1)} async-done(((f32[8,2,1,32,512]{4,3,2,1,0:T(8,128)}), f32[8,2,1,32,512]{4,3,2,1,0:T(8,128)S(1)}, u32[]{:S(2)}, u32[]{:S(2)}) %all-to-all-start.1) | async-done | bytes 1048608 | tf_op jit(solution)/shard_map/all_to_all | solution.py:271
  39.5 1.0 copy-done
  40.5 10.9 %shard_map.140 = f32[8,2,1,32,512]{4,3,2,1,0:T(8,128)} custom-call(f32[8,2,1,32,512]{4,3,2,1,0:T(8,128)} %copy-done, f32[2,32,1,128]{3,2,1,0:T(1,128)} %constant.148.phi_ref, f32[2,32,1,128]{3,2,1,0:T(1,128)} %constant.149.tw1_ref, f32[2,4,1,128]{3,2,1,0:T(1,128)} %constant.150.tw2_ref, f32[2,32,32,128]{3,2,1,0:T(8,128)} %pad_maximum_fusion.back_ref, ...), custom_call_target="tpu_custom_call" | custom-call | tf_op jit(solution)/shard_map/pallas_call | solution.py:207
  51.5 5.2 %all-to-all-start.2 = ((f32[8,2,1,32,512]{4,3,2,1,0:T(8,128)}), f32[8,2,1,32,512]{4,3,2,1,0:T(8,128)S(1)}, u32[]{:S(2)}, u32[]{:S(2)}) async-start(f32[8,2,1,32,512]{4,3,2,1,0:T(8,128)} %shard_map.140), calls=%async_computation.2 | async-start | bytes 2097152 | tf_op jit(solution)/shard_map/all_to_all | solution.py:271
  57.2 2.4 %collective-permute-start = (f32[1,1]{1,0:T(1,128)}, f32[1,1]{1,0:T(1,128)}, u32[]{:S(2)}, u32[]{:S(2)}) collective-permute-start(f32[1,1]{1,0:T(1,128)} %slice.49), channel_id=1, source_target_pairs={{4,0},{8,4},{12,8},{16,12},{20,16},{24,20},{28,24},{5,1},{9,5},{13... | collective-permute-start | bytes 20 | tf_op jit(solution)/shard_map/ppermute | solution.py:22
  59.6 0.6 slice.48
  60.3 10.3 %all-to-all-done.2 = f32[8,2,1,32,512]{4,3,2,1,0:T(8,128)S(1)} async-done(((f32[8,2,1,32,512]{4,3,2,1,0:T(8,128)}), f32[8,2,1,32,512]{4,3,2,1,0:T(8,128)S(1)}, u32[]{:S(2)}, u32[]{:S(2)}) %all-to-all-start.2) | async-done | bytes 1048608 | tf_op jit(solution)/shard_map/all_to_all | solution.py:271
  70.6 0.9 copy-done.4
  71.6 1.1 fusion.23
  72.6 0.9 copy.44
  73.5 5.1 %all-to-all-start.3 = ((f32[8,2,16,512]{3,2,1,0:T(8,128)}), f32[8,2,16,512]{3,2,1,0:T(8,128)S(1)}, u32[]{:S(2)}, u32[]{:S(2)}) async-start(f32[8,2,16,512]{3,2,1,0:T(8,128)} %bitcast.58), calls=%async_computation.3 | async-start | bytes 1048576 | tf_op jit(solution)/shard_map/all_to_all | solution.py:271
  78.7 0.7 maximum_multiply_fusion
  79.4 0.6 fusion.22
  81.3 5.5 %all-to-all-done.3 = f32[8,2,16,512]{3,2,1,0:T(8,128)S(1)} async-done(((f32[8,2,16,512]{3,2,1,0:T(8,128)}), f32[8,2,16,512]{3,2,1,0:T(8,128)S(1)}, u32[]{:S(2)}, u32[]{:S(2)}) %all-to-all-start.3) | async-done | bytes 524320 | tf_op jit(solution)/shard_map/all_to_all | solution.py:271
  87.4 0.7 copy-done.3
  88.1 2.5 %fusion = (f32[1,65536]{1,0:T(1,128)S(1)}, f32[1,65536]{1,0:T(1,128)S(1)}, f32[1,65536]{1,0:T(1,128)}) fusion(f32[1,65536]{1,0:T(1,128)S(1)} %copy-done.2, f32[1,1]{1,0:T(1,128)} %collective-permute-done, f32[1,65535]{1,0:T(1,128)S(1)} %slice.48, f32[1,65536]{1,0:T(1,128)S(1)} %copy-done.3, s32[]{:T(128)} %mul.382, f32[1,65536]{1,0:T(1,128)S(1)} %bitcast.65, ...), kind=kLoop, calls=%fused_computation.16 | loop fusion | flops 1048576 | bytes 2359308 | tf_op jit(solution)/shard_map/mul | solution.py:347
  92.4 5.7 %collective-permute-done.1 = f32[65536]{0:T(1024)S(1)} collective-permute-done((f32[65536]{0:T(1024)S(1)}, f32[65536]{0:T(1024)S(1)}, u32[]{:S(2)}, u32[]{:S(2)}) %collective-permute-start.1) | collective-permute-done | bytes 262176 | tf_op jit(solution)/shard_map/ppermute | solution.py:354
  98.2 1.6 %maximum_add_fusion = f32[1,65536]{1,0:T(1,128)} fusion(f32[1,65535]{1,0:T(1,128)S(1)} %bitcast.81, f32[1,1]{1,0:T(1,128)} %bitcast.31, f32[1,65536]{1,0:T(1,128)S(1)} %bitcast.77, f32[]{:T(128)} %bitcast.27, f32[1,65536]{1,0:T(1,128)S(1)} %copy-done.3, s32[]{:T(128)} %mul.382, f32[1,65536]{1,0:T(1,128)S(1)} %bitcast.66), kind=kLoop, calls=%fused_computation.13 | loop fusion | flops 720896 | bytes 1310728 | tf_op jit(solution)/shard_map/add | solution.py:337
  99.8 13.0 %collective-permute-done.2 = f32[65536]{0:T(1024)S(1)} collective-permute-done((f32[65536]{0:T(1024)S(1)}, f32[65536]{0:T(1024)S(1)}, u32[]{:S(2)}, u32[]{:S(2)}) %collective-permute-start.2) | collective-permute-done | bytes 262176 | tf_op jit(solution)/shard_map/ppermute | solution.py:354
  112.8 0.7 add.177
  (44 shorter events, 4.5 us)
Async XLA Ops:
  3.1 14.2 %all-to-all-start = ((f32[8,40,512]{2,1,0:T(8,128)}), f32[8,40,512]{2,1,0:T(8,128)S(1)}, u32[]{:S(2)}, u32[]{:S(2)}) async-start(f32[8,40,512]{2,1,0:T(8,128)} %shard_map.139), calls=%async_computation | async-start | bytes 1310720 | tf_op jit(solution)/shard_map/all_to_all | solution.py:271
  7.6 0.7 copy-start.8
  8.4 0.9 copy-start.6
  8.5 1.0 copy-start.7
  17.3 1.0 copy-start.5
  20.7 18.8 %all-to-all-start.1 = ((f32[8,2,1,32,512]{4,3,2,1,0:T(8,128)}), f32[8,2,1,32,512]{4,3,2,1,0:T(8,128)S(1)}, u32[]{:S(2)}, u32[]{:S(2)}) async-start(f32[8,2,1,32,512]{4,3,2,1,0:T(8,128)} %maximum_bitcast_fusion), calls=%async_computation.1 | async-start | bytes 2097152 | tf_op jit(solution)/shard_map/all_to_all | solution.py:271
  39.5 1.0 copy-start
  51.5 5.2 %copy-start.2 = (f32[1,65536]{1,0:T(1,128)S(1)}, f32[1,65536]{1,0:T(1,128)}, u32[]{:S(2)}) copy-start(f32[1,65536]{1,0:T(1,128)} %param.13) | copy-start | bytes 786436
  51.5 19.0 %all-to-all-start.2 = ((f32[8,2,1,32,512]{4,3,2,1,0:T(8,128)}), f32[8,2,1,32,512]{4,3,2,1,0:T(8,128)S(1)}, u32[]{:S(2)}, u32[]{:S(2)}) async-start(f32[8,2,1,32,512]{4,3,2,1,0:T(8,128)} %shard_map.140), calls=%async_computation.2 | async-start | bytes 2097152 | tf_op jit(solution)/shard_map/all_to_all | solution.py:271
  57.2 21.5 %collective-permute-start = (f32[1,1]{1,0:T(1,128)}, f32[1,1]{1,0:T(1,128)}, u32[]{:S(2)}, u32[]{:S(2)}) collective-permute-start(f32[1,1]{1,0:T(1,128)} %slice.49), channel_id=1, source_target_pairs={{4,0},{8,4},{12,8},{16,12},{20,16},{24,20},{28,24},{5,1},{9,5},{13... | collective-permute-start | bytes 20 | tf_op jit(solution)/shard_map/ppermute | solution.py:22
  70.5 1.0 copy-start.4
  73.5 5.1 %copy-start.1 = (f32[65536]{0:T(1024)S(1)}, f32[65536]{0:T(1024)}, u32[]{:S(2)}) copy-start(f32[65536]{0:T(1024)} %param.14) | copy-start | bytes 786436
  73.5 13.4 %all-to-all-start.3 = ((f32[8,2,16,512]{3,2,1,0:T(8,128)}), f32[8,2,16,512]{3,2,1,0:T(8,128)S(1)}, u32[]{:S(2)}, u32[]{:S(2)}) async-start(f32[8,2,16,512]{3,2,1,0:T(8,128)} %bitcast.58), calls=%async_computation.3 | async-start | bytes 1048576 | tf_op jit(solution)/shard_map/all_to_all | solution.py:271
  87.1 1.0 copy-start.3
  90.6 7.4 %collective-permute-start.1 = (f32[65536]{0:T(1024)S(1)}, f32[65536]{0:T(1024)S(1)}, u32[]{:S(2)}, u32[]{:S(2)}) collective-permute-start(f32[65536]{0:T(1024)S(1)} %bitcast.78), channel_id=1, source_target_pairs={{0,1},{1,0},{2,3},{3,2},{4,5},{5,4},{6,7},{7,6},{8,9},{9,8},{10,11... | collective-permute-start | bytes 786440 | tf_op jit(solution)/shard_map/ppermute | solution.py:354
  98.1 14.7 %collective-permute-start.2 = (f32[65536]{0:T(1024)S(1)}, f32[65536]{0:T(1024)S(1)}, u32[]{:S(2)}, u32[]{:S(2)}) collective-permute-start(f32[65536]{0:T(1024)S(1)} %add.176), channel_id=1, source_target_pairs={{0,2},{1,3},{2,0},{3,1},{4,6},{5,7},{6,4},{7,5},{8,10},{9,11},{10,... | collective-permute-start | bytes 786440 | tf_op jit(solution)/shard_map/ppermute | solution.py:354

commit v9 on v8

--- a/solution.py
+++ b/solution.py
@@ -323,7 +323,21 @@
     tw_cos, tw_sin = tw_cos.reshape(full_rows, cols), tw_sin.reshape(full_rows, cols)
     twisted = jnp.stack(complex_mul((freq[0], freq[1]), (tw_cos, -tw_sin)))
     twisted = twisted.reshape(2, scen_dev, parts, block, cols).transpose(2, 0, 1, 3, 4)
-    untwisted = column_stage(exchange(twisted), own_rows, place, nfft)
+    arriving = from_behind(cotangent[:, :1], "mass", -1)
+    following = jnp.concatenate([cotangent[:, 1:], arriving], axis=1)
+    local_grad = jnp.sum(weighted * (following - cotangent), axis=0)
+    rate_gradient = local_grad
+    groups = lax.axis_size("scen")
+    if groups & (groups - 1) == 0:
+        step = 1
+        while step < groups:
+            pairs = [(source, source ^ step) for source in range(groups)]
+            rate_gradient = rate_gradient + lax.ppermute(rate_gradient, "scen", pairs)
+            step *= 2
+    else:
+        rate_gradient = lax.psum(local_grad, "scen")
+    received, rate_gradient = lax.optimization_barrier((exchange(twisted), rate_gradient))
+    untwisted = column_stage(received, own_rows, place, nfft)
     returned = exchange(untwisted).transpose(1, 2, 0, 3, 4).reshape(2, scen_dev, full_rows, cols)
     inv_cos, inv_sin = row_cos.T, row_sin.T
     inverse_rows = jnp.stack([jnp.stack([inv_cos, -inv_sin], axis=1), jnp.stack([inv_sin, inv_cos], axis=1)])
@@ -335,8 +349,6 @@
     corr = gathered[scen_dev:]
     inflow = jnp.concatenate([incoming, flux[:, :-1]], axis=1)
     tendency = 0.5 * beta * birth - beta * first[:, None] * weighted - flux + inflow
-    arriving = from_behind(cotangent[:, :1], "mass", -1)
-    following = jnp.concatenate([cotangent[:, 1:], arriving], axis=1)
     adjoint = mass[None, :] * (
         beta * corr
         - beta * first[:, None] * cotangent
@@ -344,17 +356,6 @@
         - rate[None, :] * cotangent
         + rate[None, :] * following
     )
-    local_grad = jnp.sum(weighted * (following - cotangent), axis=0)
-    rate_gradient = local_grad
-    groups = lax.axis_size("scen")
-    if groups & (groups - 1) == 0:
-        step = 1
-        while step < groups:
-            pairs = [(source, source ^ step) for source in range(groups)]
-            rate_gradient = rate_gradient + lax.ppermute(rate_gradient, "scen", pairs)
-            step *= 2
-    else:
-        rate_gradient = lax.psum(local_grad, "scen")
     return (tendency, adjoint, rate_gradient)
 
 

time: 114 us -> 106 us (0.930)
  the two profiles are of different devices: /device:TPU:27 before, /device:TPU:0 now
where the time goes in v9:
time: 106 us
  waiting for transfers between devices  44.3 us (42%)
  starting transfers between devices  23.3 us (22%)
  Pallas kernels  13.4 us (13%)
  local copies, waits for them, and re-layouts  10.1 us (10%)
  other arithmetic  9.56 us (9%)
  between operations  2.86 us (3%)
  matrix products  2.13 us (2%)
    all_to_all x4, waiting for transfers between devices, exchange(): return lax.all_to_all(value, 'mass', 0, 0, tiled=True)  28.3 us
    all_to_all x4, starting transfers between devices, exchange(): return lax.all_to_all(value, 'mass', 0, 0, tiled=True)  17.8 us
    ppermute x2, waiting for transfers between devices, shards(): rate_gradient = rate_gradient + lax.ppermute(rate_gradient, 'scen', pairs)  16 us
    pallas_call x1, Pallas kernels, column_stage(): pl.pallas_call(column_kernel, out_shape=jax.ShapeDtypeStruct(received.sha...  11 us
    unnamed x20, local copies, waits for them, and re-layouts  5.06 us
    ppermute x2, starting transfers between devices, shards(): rate_gradient = rate_gradient + lax.ppermute(rate_gradient, 'scen', pairs)  4.24 us
    pallas_call x1, Pallas kernels, prologue(): pl.pallas_call(functools.partial(prologue_kernel, nbin), out_shape=jax.Sh...  2.42 us
    mul x1, other arithmetic, shards(): mass[None, :]  2.15 us
  transfers between devices with their start and end apart: 7, of which 5 were waited for; matrix products, arithmetic and copies ran while one was open for 10% of the time, Pallas kernels for 2%

profile of v9, /device:TPU:0, one launch (start us, length us, event | category | flops | bytes accessed | tf_op | source)
XLA Modules:
  0.0 105.7 jit_solution(13923733049556751780)
XLA Ops:
  0.6 1.2 %slice.42 = f32[1,1]{1,0:T(1,128)} slice(f32[1,65536]{1,0:T(1,128)} %param.13), slice={[0:1], [0:1]} | slice | bytes 8 | tf_op jit(solution)/shard_map/slice | solution.py:326
  1.8 1.3 %collective-permute-start = (f32[1,1]{1,0:T(1,128)}, f32[1,1]{1,0:T(1,128)}, u32[]{:S(2)}, u32[]{:S(2)}) collective-permute-start(f32[1,1]{1,0:T(1,128)} %slice.42), channel_id=1, source_target_pairs={{4,0},{8,4},{12,8},{16,12},{20,16},{24,20},{28,24},{5,1},{9,5},{13... | collective-permute-start | bytes 20 | tf_op jit(solution)/shard_map/ppermute | solution.py:22
  3.1 2.4 %shard_map.139 = f32[8,40,512]{2,1,0:T(8,128)} custom-call(s32[1]{0:T(128)} %bitcast.1.base_ref, f32[1,512,128]{2,1,0:T(8,128)} %bitcast.69, f32[1,512,128]{2,1,0:T(8,128)} %bitcast.64, f32[512,128]{1,0:T(8,128)} %bitcast.65), custom_call_target="tpu_custom_call" | custom-call | tf_op jit(solution)/shard_map/pallas_call | solution.py:261
  5.5 6.4 %all-to-all-start = ((f32[8,40,512]{2,1,0:T(8,128)}), f32[8,40,512]{2,1,0:T(8,128)S(1)}, u32[]{:S(2)}, u32[]{:S(2)}) async-start(f32[8,40,512]{2,1,0:T(8,128)} %shard_map.139), calls=%async_computation | async-start | bytes 1310720 | tf_op jit(solution)/shard_map/all_to_all | solution.py:271
  11.9 0.7 copy-done.8
  13.0 0.6 copy-done.6
  13.7 0.7 add_negate_fusion
  14.6 0.6 slice.41
  15.9 7.2 %all-to-all-done = f32[8,40,512]{2,1,0:T(8,128)S(1)} async-done(((f32[8,40,512]{2,1,0:T(8,128)}), f32[8,40,512]{2,1,0:T(8,128)S(1)}, u32[]{:S(2)}, u32[]{:S(2)}) %all-to-all-start) | async-done | bytes 655392 | tf_op jit(solution)/shard_map/all_to_all | solution.py:271
  23.2 1.0 copy-done.5
  24.1 1.1 convolution_bitcast_fusion
  25.5 1.1 %maximum_bitcast_fusion = f32[8,2,1,32,512]{4,3,2,1,0:T(8,128)} fusion(f32[1,1,8,32,512]{4,3,1,0,2:T(8,128)S(1)} %bitcast.74, f32[1,1,8,32,512]{4,3,1,0,2:T(8,128)S(1)} %bitcast.73), kind=kLoop, calls=%fused_computation.1 | loop fusion | flops 262144 | bytes 2097152 | tf_op jit(solution)/shard_map/transpose | solution.py:325
  26.5 3.9 %all-to-all-start.1 = ((f32[8,2,1,32,512]{4,3,2,1,0:T(8,128)}), f32[8,2,1,32,512]{4,3,2,1,0:T(8,128)S(1)}, u32[]{:S(2)}, u32[]{:S(2)}) async-start(f32[8,2,1,32,512]{4,3,2,1,0:T(8,128)} %maximum_bitcast_fusion), calls=%async_computation.1 | async-start | bytes 2097152 | tf_op jit(solution)/shard_map/all_to_all | solution.py:271
  30.4 1.4 %fusion = (f32[1,65536]{1,0:T(1,128)S(1)}, f32[1,65536]{1,0:T(1,128)S(1)}) fusion(f32[1,65536]{1,0:T(1,128)S(1)} %copy-done.1, f32[1,1]{1,0:T(1,128)} %collective-permute-done, f32[1,65535]{1,0:T(1,128)S(1)} %slice.41, f32[1,65536]{1,0:T(1,128)S(1)} %copy-done.3, s32[]{:T(128)} %mul.382, f32[1,65536]{1,0:T(1,128)S(1)} %bitcast.66), kind=kLoop, calls=%fused_computation.14 | loop fusion | flops 589824 | bytes 1572868 | tf_op jit(solution)/shard_map/mul | solution.py:328
  31.8 1.6 %collective-permute-start.1 = (f32[65536]{0:T(1024)S(1)}, f32[65536]{0:T(1024)S(1)}, u32[]{:S(2)}, u32[]{:S(2)}) collective-permute-start(f32[65536]{0:T(1024)S(1)} %bitcast.75), channel_id=1, source_target_pairs={{0,1},{1,0},{2,3},{3,2},{4,5},{5,4},{6,7},{7,6},{8,9},{9,8},{10,11... | collective-permute-start | bytes 786440 | tf_op jit(solution)/shard_map/ppermute | solution.py:335
  33.9 6.4 %collective-permute-done.1 = f32[65536]{0:T(1024)S(1)} collective-permute-done((f32[65536]{0:T(1024)S(1)}, f32[65536]{0:T(1024)S(1)}, u32[]{:S(2)}, u32[]{:S(2)}) %collective-permute-start.1) | collective-permute-done | bytes 262176 | tf_op jit(solution)/shard_map/ppermute | solution.py:335
  40.3 2.7 %collective-permute-start.2 = (f32[65536]{0:T(1024)S(1)}, f32[65536]{0:T(1024)S(1)}, u32[]{:S(2)}, u32[]{:S(2)}) collective-permute-start(f32[65536]{0:T(1024)S(1)} %add.166), channel_id=1, source_target_pairs={{0,2},{1,3},{2,0},{3,1},{4,6},{5,7},{6,4},{7,5},{8,10},{9,11},{10,... | collective-permute-start | bytes 786440 | tf_op jit(solution)/shard_map/ppermute | solution.py:335
  43.1 0.6 add_convert_fusion.flag_ref
  43.7 1.1 %pad_maximum_fusion.back_ref = f32[2,32,32,128]{3,2,1,0:T(8,128)} fusion(f32[1,32,32,128]{3,2,1,0:T(8,128)S(1)} %get-tuple-element.18, f32[1,32,32,128]{3,2,1,0:T(8,128)S(1)} %get-tuple-element.17), kind=kLoop, calls=%fused_computation.2 | loop fusion | flops 262144 | bytes 2097152 | tf_op jit(solution)/shard_map/stack | solution.py:201
  44.8 9.7 %collective-permute-done.2 = f32[65536]{0:T(1024)S(1)} collective-permute-done((f32[65536]{0:T(1024)S(1)}, f32[65536]{0:T(1024)S(1)}, u32[]{:S(2)}, u32[]{:S(2)}) %collective-permute-start.2) | collective-permute-done | bytes 262176 | tf_op jit(solution)/shard_map/ppermute | solution.py:335
  54.5 0.7 add.167
  55.2 1.0 copy-done
  56.2 11.0 %shard_map.140 = f32[8,2,1,32,512]{4,3,2,1,0:T(8,128)} custom-call(f32[8,2,1,32,512]{4,3,2,1,0:T(8,128)} %copy-done, f32[2,32,1,128]{3,2,1,0:T(1,128)} %constant.148.phi_ref, f32[2,32,1,128]{3,2,1,0:T(1,128)} %constant.149.tw1_ref, f32[2,4,1,128]{3,2,1,0:T(1,128)} %constant.150.tw2_ref, f32[2,32,32,128]{3,2,1,0:T(8,128)} %pad_maximum_fusion.back_ref, ...), custom_call_target="tpu_custom_call" | custom-call | tf_op jit(solution)/shard_map/pallas_call | solution.py:207
  67.2 3.8 %all-to-all-start.2 = ((f32[8,2,1,32,512]{4,3,2,1,0:T(8,128)}), f32[8,2,1,32,512]{4,3,2,1,0:T(8,128)S(1)}, u32[]{:S(2)}, u32[]{:S(2)}) async-start(f32[8,2,1,32,512]{4,3,2,1,0:T(8,128)} %shard_map.140), calls=%async_computation.2 | async-start | bytes 2097152 | tf_op jit(solution)/shard_map/all_to_all | solution.py:271
  71.0 15.4 %all-to-all-done.2 = f32[8,2,1,32,512]{4,3,2,1,0:T(8,128)S(1)} async-done(((f32[8,2,1,32,512]{4,3,2,1,0:T(8,128)}), f32[8,2,1,32,512]{4,3,2,1,0:T(8,128)S(1)}, u32[]{:S(2)}, u32[]{:S(2)}) %all-to-all-start.2) | async-done | bytes 1048608 | tf_op jit(solution)/shard_map/all_to_all | solution.py:271
  86.5 0.9 copy-done.4
  87.4 1.1 %fusion.23 = f32[512,2,128,1]{0,2,3,1:T(8,128)S(1)} fusion(f32[2,256,512,1]{2,1,0,3:T(8,128)S(1)} %bitcast.63, f32[2,128,2,256]{3,1,2,0:T(8,128)S(1)} %copy-done.4), kind=kOutput, calls=%fused_computation.68 | convolution fusion | flops 805306368 | bytes 2097152 | tf_op jit(solution)/shard_map/orik,iskw->osrw/dot_general | solution.py:344
  88.5 0.9 copy.44
  89.4 3.7 %all-to-all-start.3 = ((f32[8,2,16,512]{3,2,1,0:T(8,128)}), f32[8,2,16,512]{3,2,1,0:T(8,128)S(1)}, u32[]{:S(2)}, u32[]{:S(2)}) async-start(f32[8,2,16,512]{3,2,1,0:T(8,128)} %bitcast.58), calls=%async_computation.3 | async-start | bytes 1048576 | tf_op jit(solution)/shard_map/all_to_all | solution.py:271
  93.1 0.6 maximum_multiply_fusion
  96.8 5.7 %all-to-all-done.3 = f32[8,2,16,512]{3,2,1,0:T(8,128)S(1)} async-done(((f32[8,2,16,512]{3,2,1,0:T(8,128)}), f32[8,2,16,512]{3,2,1,0:T(8,128)S(1)}, u32[]{:S(2)}, u32[]{:S(2)}) %all-to-all-start.3) | async-done | bytes 524320 | tf_op jit(solution)/shard_map/all_to_all | solution.py:271
  103.5 2.2 %add_multiply_fusion = (f32[1,65536]{1,0:T(1,128)}, f32[1,65536]{1,0:T(1,128)}) fusion(f32[1,65536]{1,0:T(1,128)S(1)} %bitcast.82, f32[1,65536]{1,0:T(1,128)S(1)} %bitcast.67, f32[1,65536]{1,0:T(1,128)S(1)} %copy-done.1, f32[1,65536]{1,0:T(1,128)S(1)} %bitcast.79, f32[]{:T(128)} %bitcast.33, f32[]{:T(128)} %bitcast.28, s32[]{:T(128)} %mul.382, ...), kind=kLoop, calls=%fused_computation.19 | loop fusion | flops 1179648 | bytes 2359308 | tf_op jit(solution)/shard_map/mul | solution.py:352
  (44 shorter events, 4.5 us)
Async XLA Ops:
  1.8 28.6 %collective-permute-start = (f32[1,1]{1,0:T(1,128)}, f32[1,1]{1,0:T(1,128)}, u32[]{:S(2)}, u32[]{:S(2)}) collective-permute-start(f32[1,1]{1,0:T(1,128)} %slice.42), channel_id=1, source_target_pairs={{4,0},{8,4},{12,8},{16,12},{20,16},{24,20},{28,24},{5,1},{9,5},{13... | collective-permute-start | bytes 20 | tf_op jit(solution)/shard_map/ppermute | solution.py:22
  5.5 17.5 %all-to-all-start = ((f32[8,40,512]{2,1,0:T(8,128)}), f32[8,40,512]{2,1,0:T(8,128)S(1)}, u32[]{:S(2)}, u32[]{:S(2)}) async-start(f32[8,40,512]{2,1,0:T(8,128)} %shard_map.139), calls=%async_computation | async-start | bytes 1310720 | tf_op jit(solution)/shard_map/all_to_all | solution.py:271
  11.9 0.7 copy-start.8
  12.7 0.9 copy-start.6
  12.7 1.0 copy-start.7
  13.7 0.9 copy-start.1
  23.1 1.0 copy-start.5
  26.5 3.9 %copy-start.2 = (f32[65536]{0:T(1024)S(1)}, f32[65536]{0:T(1024)}, u32[]{:S(2)}) copy-start(f32[65536]{0:T(1024)} %param.14) | copy-start | bytes 786436
  26.5 3.9 %copy-start.3 = (f32[1,65536]{1,0:T(1,128)S(1)}, f32[1,65536]{1,0:T(1,128)}, u32[]{:S(2)}) copy-start(f32[1,65536]{1,0:T(1,128)} %param.12) | copy-start | bytes 786436
  26.5 28.7 %all-to-all-start.1 = ((f32[8,2,1,32,512]{4,3,2,1,0:T(8,128)}), f32[8,2,1,32,512]{4,3,2,1,0:T(8,128)S(1)}, u32[]{:S(2)}, u32[]{:S(2)}) async-start(f32[8,2,1,32,512]{4,3,2,1,0:T(8,128)} %maximum_bitcast_fusion), calls=%async_computation.1 | async-start | bytes 2097152 | tf_op jit(solution)/shard_map/all_to_all | solution.py:271
  31.8 8.4 %collective-permute-start.1 = (f32[65536]{0:T(1024)S(1)}, f32[65536]{0:T(1024)S(1)}, u32[]{:S(2)}, u32[]{:S(2)}) collective-permute-start(f32[65536]{0:T(1024)S(1)} %bitcast.75), channel_id=1, source_target_pairs={{0,1},{1,0},{2,3},{3,2},{4,5},{5,4},{6,7},{7,6},{8,9},{9,8},{10,11... | collective-permute-start | bytes 786440 | tf_op jit(solution)/shard_map/ppermute | solution.py:335
  40.3 14.2 %collective-permute-start.2 = (f32[65536]{0:T(1024)S(1)}, f32[65536]{0:T(1024)S(1)}, u32[]{:S(2)}, u32[]{:S(2)}) collective-permute-start(f32[65536]{0:T(1024)S(1)} %add.166), channel_id=1, source_target_pairs={{0,2},{1,3},{2,0},{3,1},{4,6},{5,7},{6,4},{7,5},{8,10},{9,11},{10,... | collective-permute-start | bytes 786440 | tf_op jit(solution)/shard_map/ppermute | solution.py:335
  55.2 1.0 copy-start
  67.2 19.2 %all-to-all-start.2 = ((f32[8,2,1,32,512]{4,3,2,1,0:T(8,128)}), f32[8,2,1,32,512]{4,3,2,1,0:T(8,128)S(1)}, u32[]{:S(2)}, u32[]{:S(2)}) async-start(f32[8,2,1,32,512]{4,3,2,1,0:T(8,128)} %shard_map.140), calls=%async_computation.2 | async-start | bytes 2097152 | tf_op jit(solution)/shard_map/all_to_all | solution.py:271
  86.4 1.0 copy-start.4
  89.4 13.2 %all-to-all-start.3 = ((f32[8,2,16,512]{3,2,1,0:T(8,128)}), f32[8,2,16,512]{3,2,1,0:T(8,128)S(1)}, u32[]{:S(2)}, u32[]{:S(2)}) async-start(f32[8,2,16,512]{3,2,1,0:T(8,128)} %bitcast.58), calls=%async_computation.3 | async-start | bytes 1048576 | tf_op jit(solution)/shard_map/all_to_all | solution.py:271

commit v10 on v9

--- a/solution.py
+++ b/solution.py
@@ -328,7 +328,18 @@
     local_grad = jnp.sum(weighted * (following - cotangent), axis=0)
     rate_gradient = local_grad
     groups = lax.axis_size("scen")
-    if groups & (groups - 1) == 0:
+    if groups & (groups - 1) == 0 and groups <= 4:
+        member = lax.axis_index("scen")
+        held = [local_grad] + [
+            lax.ppermute(local_grad, "scen", [(source, source ^ k) for source in range(groups)])
+            for k in range(1, groups)
+        ]
+        held = jnp.stack(held)
+        ordered = jnp.take(held, jnp.bitwise_xor(member, counting(groups)), axis=0)
+        rate_gradient = ordered[0]
+        for k in range(1, groups):
+            rate_gradient = rate_gradient + ordered[k]
+    elif groups & (groups - 1) == 0:
         step = 1
         while step < groups:
             pairs = [(source, source ^ step) for source in range(groups)]
@@ -336,8 +347,8 @@
             step *= 2
     else:
         rate_gradient = lax.psum(local_grad, "scen")
-    received, rate_gradient = lax.optimization_barrier((exchange(twisted), rate_gradient))
-    untwisted = column_stage(received, own_rows, place, nfft)
+    untwisted = column_stage(exchange(twisted), own_rows, place, nfft)
+    untwisted, rate_gradient = lax.optimization_barrier((untwisted, rate_gradient))
     returned = exchange(untwisted).transpose(1, 2, 0, 3, 4).reshape(2, scen_dev, full_rows, cols)
     inv_cos, inv_sin = row_cos.T, row_sin.T
     inverse_rows = jnp.stack([jnp.stack([inv_cos, -inv_sin], axis=1), jnp.stack([inv_sin, inv_cos], axis=1)])

time: 106 us -> 124 us (1.17)
  waiting for transfers between devices: 44.3 us -> 52.2 us
  local copies, waits for them, and re-layouts: 10.1 us -> 15 us
  other arithmetic: 9.56 us -> 14.2 us
    all_to_all x4, waiting for transfers between devices: 28.3 us -> 33.6 us  [exchange(): return lax.all_to_all(value, 'mass', 0, 0, tiled=True)]
    ppermute x2 -> x3, waiting for transfers between devices: 16 us -> 18.6 us  [shards(): lax.ppermute(local_grad, 'scen', [(source, source ^ k) for source in rang...]
    another operation x0 -> x1, other arithmetic: none -> 2.18 us  [shards(): held = jnp.stack(held)]
    unnamed x20 -> x24, local copies, waits for them, and re-layouts: 5.06 us -> 5.46 us
    ppermute x2 -> x3, starting transfers between devices: 4.24 us -> 4.39 us  [shards(): lax.ppermute(local_grad, 'scen', [(source, source ^ k) for source in rang...]
  transfers between devices with their start and end apart: 7 -> 8, of which waited for: 5 -> 5; matrix products, arithmetic and copies ran while one was open for 10% -> 13% of each run, Pallas kernels for 2% -> 2%
where the time goes in v10:
time: 124 us; the launch traced here: 123 us
  waiting for transfers between devices  52.2 us (42%)
  starting transfers between devices  23.5 us (19%)
  local copies, waits for them, and re-layouts  15 us (12%)
  other arithmetic  14.2 us (11%)
  Pallas kernels  13.4 us (11%)
  between operations  2.91 us (2%)
  matrix products  2.13 us (2%)
    all_to_all x4, waiting for transfers between devices, exchange(): return lax.all_to_all(value, 'mass', 0, 0, tiled=True)  33.6 us
    ppermute x3, waiting for transfers between devices, shards(): lax.ppermute(local_grad, 'scen', [(source, source ^ k) for source in rang...  18.6 us
    all_to_all x4, starting transfers between devices, exchange(): return lax.all_to_all(value, 'mass', 0, 0, tiled=True)  17.9 us
    pallas_call x1, Pallas kernels, column_stage(): pl.pallas_call(column_kernel, out_shape=jax.ShapeDtypeStruct(received.sha...  11 us
    unnamed x24, local copies, waits for them, and re-layouts  5.46 us
    ppermute x3, starting transfers between devices, shards(): lax.ppermute(local_grad, 'scen', [(source, source ^ k) for source in rang...  4.39 us
  transfers between devices with their start and end apart: 8, of which 5 were waited for; matrix products, arithmetic and copies ran while one was open for 13% of the time, Pallas kernels for 2%

profile of v10, /device:TPU:0, one launch (start us, length us, event | category | flops | bytes accessed | tf_op | source)
XLA Modules:
  0.0 123.4 jit_solution(5826528634151918187)
XLA Ops:
  0.6 1.2 slice.54
  1.8 1.3 %collective-permute-start = (f32[1,1]{1,0:T(1,128)}, f32[1,1]{1,0:T(1,128)}, u32[]{:S(2)}, u32[]{:S(2)}) collective-permute-start(f32[1,1]{1,0:T(1,128)} %slice.54), channel_id=1, source_target_pairs={{4,0},{8,4},{12,8},{16,12},{20,16},{24,20},{28,24},{5,1},{9,5},{13... | collective-permute-start | bytes 20 | tf_op jit(solution)/shard_map/ppermute | solution.py:22
  3.1 2.4 %shard_map.139 = f32[8,40,512]{2,1,0:T(8,128)} custom-call(s32[1]{0:T(128)} %bitcast.1.base_ref, f32[1,512,128]{2,1,0:T(8,128)} %bitcast.75, f32[1,512,128]{2,1,0:T(8,128)} %bitcast.70, f32[512,128]{1,0:T(8,128)} %bitcast.71), custom_call_target="tpu_custom_call" | custom-call | tf_op jit(solution)/shard_map/pallas_call | solution.py:261
  5.5 6.5 %all-to-all-start = ((f32[8,40,512]{2,1,0:T(8,128)}), f32[8,40,512]{2,1,0:T(8,128)}, u32[]{:S(2)}, u32[]{:S(2)}) async-start(f32[8,40,512]{2,1,0:T(8,128)} %shard_map.139), calls=%async_computation | async-start | bytes 1310720 | tf_op jit(solution)/shard_map/all_to_all | solution.py:271
  16.4 2.1 %fusion = (f32[1,65536]{1,0:T(1,128)}, f32[1,65536]{1,0:T(1,128)S(1)}) fusion(f32[1,65536]{1,0:T(1,128)S(1)} %copy-done.1, f32[1,1]{1,0:T(1,128)} %collective-permute-done, f32[1,65535]{1,0:T(1,128)S(1)} %slice.53, f32[1,65536]{1,0:T(1,128)S(1)} %copy-done.3, s32[]{:T(128)} %mul.382, f32[1,65536]{1,0:T(1,128)S(1)} %bitcast.72), kind=kLoop, calls=%fused_computation.20 | loop fusion | flops 589824 | bytes 1572868 | tf_op jit(solution)/shard_map/mul | solution.py:328
  18.6 3.6 %collective-permute-start.3 = (f32[65536]{0:T(1024)}, f32[65536]{0:T(1024)}, u32[]{:S(2)}, u32[]{:S(2)}) collective-permute-start(f32[65536]{0:T(1024)} %bitcast.17), channel_id=1, source_target_pairs={{0,3},{1,2},{2,1},{3,0},{4,7},{5,6},{6,5},{7,4},{8,11},{9,10},{10,... | collective-permute-start | bytes 786440 | tf_op jit(solution)/shard_map/ppermute | solution.py:334
  22.2 0.8 collective-permute-start.1
  23.0 1.0 neg.24
  24.0 1.0 sub.79
  25.8 1.1 pad_maximum_fusion.back_ref
  26.9 3.1 %collective-permute-done.3 = f32[65536]{0:T(1024)} collective-permute-done((f32[65536]{0:T(1024)}, f32[65536]{0:T(1024)}, u32[]{:S(2)}, u32[]{:S(2)}) %collective-permute-start.3) | collective-permute-done | bytes 262176 | tf_op jit(solution)/shard_map/ppermute | solution.py:334
  29.9 15.5 %collective-permute-done.2 = f32[65536]{0:T(1024)} collective-permute-done((f32[65536]{0:T(1024)}, f32[65536]{0:T(1024)}, u32[]{:S(2)}, u32[]{:S(2)}) %collective-permute-start.2) | collective-permute-done | bytes 262176 | tf_op jit(solution)/shard_map/ppermute | solution.py:334
  45.5 2.2 %pad_maximum_fusion.1 = f32[4,65536]{1,0:T(4,128)S(1)} fusion(f32[1,65536]{1,0:T(1,128)} %bitcast.20, f32[1,65536]{1,0:T(1,128)} %bitcast.19, f32[1,65536]{1,0:T(1,128)} %bitcast.18, f32[1,65536]{1,0:T(1,128)} %get-tuple-element.15), kind=kLoop, calls=%fused_computation.4 | loop fusion | flops 786432 | bytes 2097152 | tf_op jit(solution)/shard_map/stack | solution.py:337
  47.7 1.1 gather_fusion
  49.1 1.1 slice.68
  50.2 1.0 copy-done.7
  51.2 1.1 convolution_bitcast_fusion
  52.7 1.1 maximum_bitcast_fusion
  53.7 4.1 %all-to-all-start.1 = ((f32[8,2,1,32,512]{4,3,2,1,0:T(8,128)}), f32[8,2,1,32,512]{4,3,2,1,0:T(8,128)S(1)}, u32[]{:S(2)}, u32[]{:S(2)}) async-start(f32[8,2,1,32,512]{4,3,2,1,0:T(8,128)} %maximum_bitcast_fusion), calls=%async_computation.1 | async-start | bytes 2097152 | tf_op jit(solution)/shard_map/all_to_all | solution.py:271
  57.8 1.3 %slice_add_fusion = f32[1,65536]{1,0:T(1,128)} fusion(f32[4,65536]{1,0:T(4,128)S(1)} %broadcast_select_fusion), kind=kLoop, calls=%fused_computation.16 | loop fusion | flops 196608 | bytes 1310720 | tf_op jit(solution)/shard_map/add | solution.py:341
  59.1 14.1 %all-to-all-done.1.x_ref = f32[8,2,1,32,512]{4,3,2,1,0:T(8,128)S(1)} async-done(((f32[8,2,1,32,512]{4,3,2,1,0:T(8,128)}), f32[8,2,1,32,512]{4,3,2,1,0:T(8,128)S(1)}, u32[]{:S(2)}, u32[]{:S(2)}) %all-to-all-start.1) | async-done | bytes 1048608 | tf_op jit(solution)/shard_map/all_to_all | solution.py:271
  73.2 1.0 copy-done
  74.2 11.0 %shard_map.140 = f32[8,2,1,32,512]{4,3,2,1,0:T(8,128)} custom-call(f32[8,2,1,32,512]{4,3,2,1,0:T(8,128)} %copy-done, f32[2,32,1,128]{3,2,1,0:T(1,128)} %constant.166.phi_ref, f32[2,32,1,128]{3,2,1,0:T(1,128)} %constant.167.tw1_ref, f32[2,4,1,128]{3,2,1,0:T(1,128)} %constant.168.tw2_ref, f32[2,32,32,128]{3,2,1,0:T(8,128)} %pad_maximum_fusion.back_ref, ...), custom_call_target="tpu_custom_call" | custom-call | tf_op jit(solution)/shard_map/pallas_call | solution.py:207
  85.2 3.6 %all-to-all-start.2 = ((f32[8,2,1,32,512]{4,3,2,1,0:T(8,128)}), f32[8,2,1,32,512]{4,3,2,1,0:T(8,128)S(1)}, u32[]{:S(2)}, u32[]{:S(2)}) async-start(f32[8,2,1,32,512]{4,3,2,1,0:T(8,128)} %shard_map.140), calls=%async_computation.2 | async-start | bytes 2097152 | tf_op jit(solution)/shard_map/all_to_all | solution.py:271
  88.8 15.3 %all-to-all-done.2 = f32[8,2,1,32,512]{4,3,2,1,0:T(8,128)S(1)} async-done(((f32[8,2,1,32,512]{4,3,2,1,0:T(8,128)}), f32[8,2,1,32,512]{4,3,2,1,0:T(8,128)S(1)}, u32[]{:S(2)}, u32[]{:S(2)}) %all-to-all-start.2) | async-done | bytes 1048608 | tf_op jit(solution)/shard_map/all_to_all | solution.py:271
  104.2 0.9 copy-done.6
  105.1 1.1 fusion.24
  106.2 0.9 copy.41
  107.1 3.7 %all-to-all-start.3 = ((f32[8,2,16,512]{3,2,1,0:T(8,128)}), f32[8,2,16,512]{3,2,1,0:T(8,128)S(1)}, u32[]{:S(2)}, u32[]{:S(2)}) async-start(f32[8,2,16,512]{3,2,1,0:T(8,128)} %bitcast.64), calls=%async_computation.3 | async-start | bytes 1048576 | tf_op jit(solution)/shard_map/all_to_all | solution.py:271
  111.5 0.8 slice_reduce_fusion
  116.1 4.2 %all-to-all-done.3 = f32[8,2,16,512]{3,2,1,0:T(8,128)S(1)} async-done(((f32[8,2,16,512]{3,2,1,0:T(8,128)}), f32[8,2,16,512]{3,2,1,0:T(8,128)S(1)}, u32[]{:S(2)}, u32[]{:S(2)}) %all-to-all-start.3) | async-done | bytes 524320 | tf_op jit(solution)/shard_map/all_to_all | solution.py:271
  121.2 2.2 %add_multiply_fusion = (f32[1,65536]{1,0:T(1,128)}, f32[1,65536]{1,0:T(1,128)}) fusion(f32[1,65536]{1,0:T(1,128)S(1)} %bitcast.86, f32[1,65536]{1,0:T(1,128)S(1)} %bitcast.73, f32[1,65536]{1,0:T(1,128)S(1)} %copy-done.1, f32[1,65536]{1,0:T(1,128)S(1)} %bitcast.83, f32[]{:T(128)} %bitcast.38, f32[]{:T(128)} %bitcast.33, s32[]{:T(128)} %mul.382, ...), kind=kLoop, calls=%fused_computation.25 | loop fusion | flops 1179648 | bytes 2359308 | tf_op jit(solution)/shard_map/mul | solution.py:363
  (55 shorter events, 9.3 us)
Async XLA Ops:
  1.8 14.0 %collective-permute-start = (f32[1,1]{1,0:T(1,128)}, f32[1,1]{1,0:T(1,128)}, u32[]{:S(2)}, u32[]{:S(2)}) collective-permute-start(f32[1,1]{1,0:T(1,128)} %slice.54), channel_id=1, source_target_pairs={{4,0},{8,4},{12,8},{16,12},{20,16},{24,20},{28,24},{5,1},{9,5},{13... | collective-permute-start | bytes 20 | tf_op jit(solution)/shard_map/ppermute | solution.py:22
  5.5 6.5 %copy-start.1 = (f32[1,65536]{1,0:T(1,128)S(1)}, f32[1,65536]{1,0:T(1,128)}, u32[]{:S(2)}) copy-start(f32[1,65536]{1,0:T(1,128)} %param.13) | copy-start | bytes 786436
  5.5 43.5 %all-to-all-start = ((f32[8,40,512]{2,1,0:T(8,128)}), f32[8,40,512]{2,1,0:T(8,128)}, u32[]{:S(2)}, u32[]{:S(2)}) async-start(f32[8,40,512]{2,1,0:T(8,128)} %shard_map.139), calls=%async_computation | async-start | bytes 1310720 | tf_op jit(solution)/shard_map/all_to_all | solution.py:271
  12.9 0.7 copy-start.10
  13.7 0.9 copy-start.8
  13.8 1.0 copy-start.9
  15.4 1.0 copy-start.2
  15.4 1.0 copy-start.3
  18.6 11.4 %collective-permute-start.3 = (f32[65536]{0:T(1024)}, f32[65536]{0:T(1024)}, u32[]{:S(2)}, u32[]{:S(2)}) collective-permute-start(f32[65536]{0:T(1024)} %bitcast.17), channel_id=1, source_target_pairs={{0,3},{1,2},{2,1},{3,0},{4,7},{5,6},{6,5},{7,4},{8,11},{9,10},{10,... | collective-permute-start | bytes 786440 | tf_op jit(solution)/shard_map/ppermute | solution.py:334
  22.2 23.3 %collective-permute-start.2 = (f32[65536]{0:T(1024)}, f32[65536]{0:T(1024)}, u32[]{:S(2)}, u32[]{:S(2)}) collective-permute-start(f32[65536]{0:T(1024)} %bitcast.17), channel_id=1, source_target_pairs={{0,2},{1,3},{2,0},{3,1},{4,6},{5,7},{6,4},{7,5},{8,10},{9,11},{10,... | collective-permute-start | bytes 786440 | tf_op jit(solution)/shard_map/ppermute | solution.py:334
  22.2 23.3 %collective-permute-start.1 = (f32[65536]{0:T(1024)}, f32[65536]{0:T(1024)}, u32[]{:S(2)}, u32[]{:S(2)}) collective-permute-start(f32[65536]{0:T(1024)} %bitcast.17), channel_id=1, source_target_pairs={{0,1},{1,0},{2,3},{3,2},{4,5},{5,4},{6,7},{7,6},{8,9},{9,8},{10,11... | collective-permute-start | bytes 786440 | tf_op jit(solution)/shard_map/ppermute | solution.py:334
  50.1 1.0 copy-start.7
  51.2 1.1 copy-start.4
  51.2 1.2 copy-start.5
  53.7 19.5 %all-to-all-start.1 = ((f32[8,2,1,32,512]{4,3,2,1,0:T(8,128)}), f32[8,2,1,32,512]{4,3,2,1,0:T(8,128)S(1)}, u32[]{:S(2)}, u32[]{:S(2)}) async-start(f32[8,2,1,32,512]{4,3,2,1,0:T(8,128)} %maximum_bitcast_fusion), calls=%async_computation.1 | async-start | bytes 2097152 | tf_op jit(solution)/shard_map/all_to_all | solution.py:271
  73.2 1.0 copy-start
  85.2 18.9 %all-to-all-start.2 = ((f32[8,2,1,32,512]{4,3,2,1,0:T(8,128)}), f32[8,2,1,32,512]{4,3,2,1,0:T(8,128)S(1)}, u32[]{:S(2)}, u32[]{:S(2)}) async-start(f32[8,2,1,32,512]{4,3,2,1,0:T(8,128)} %shard_map.140), calls=%async_computation.2 | async-start | bytes 2097152 | tf_op jit(solution)/shard_map/all_to_all | solution.py:271
  104.1 1.0 copy-start.6
  107.1 13.2 %all-to-all-start.3 = ((f32[8,2,16,512]{3,2,1,0:T(8,128)}), f32[8,2,16,512]{3,2,1,0:T(8,128)S(1)}, u32[]{:S(2)}, u32[]{:S(2)}) async-start(f32[8,2,16,512]{3,2,1,0:T(8,128)} %bitcast.64), calls=%async_computation.3 | async-start | bytes 1048576 | tf_op jit(solution)/shard_map/all_to_all | solution.py:271

commit v11 on v9

--- a/solution.py
+++ b/solution.py
@@ -326,6 +326,7 @@
     arriving = from_behind(cotangent[:, :1], "mass", -1)
     following = jnp.concatenate([cotangent[:, 1:], arriving], axis=1)
     local_grad = jnp.sum(weighted * (following - cotangent), axis=0)
+    received, local_grad = lax.optimization_barrier((exchange(twisted), local_grad))
     rate_gradient = local_grad
     groups = lax.axis_size("scen")
     if groups & (groups - 1) == 0:
@@ -336,7 +337,6 @@
             step *= 2
     else:
         rate_gradient = lax.psum(local_grad, "scen")
-    received, rate_gradient = lax.optimization_barrier((exchange(twisted), rate_gradient))
     untwisted = column_stage(received, own_rows, place, nfft)
     returned = exchange(untwisted).transpose(1, 2, 0, 3, 4).reshape(2, scen_dev, full_rows, cols)
     inv_cos, inv_sin = row_cos.T, row_sin.T

time: 106 us -> 96.5 us (0.910)
  waiting for transfers between devices: 44.3 us -> 32.9 us
  other arithmetic: 9.56 us -> 11.5 us
    ppermute x2, waiting for transfers between devices: 16 us -> 7.08 us  [shards(): rate_gradient = rate_gradient + lax.ppermute(rate_gradient, 'scen', pairs)]
    all_to_all x4, waiting for transfers between devices: 28.3 us -> 25.8 us  [exchange(): return lax.all_to_all(value, 'mass', 0, 0, tiled=True)]
    add x2, other arithmetic: 0.76 us -> 2.66 us  [shards(): rate_gradient = rate_gradient + lax.ppermute(rate_gradient, 'scen', pairs)]
  transfers between devices with their start and end apart: 7 -> 7, of which waited for: 5 -> 5; matrix products, arithmetic and copies ran while one was open for 10% -> 16% of each run, Pallas kernels for 2% -> 3%
where the time goes in v11:
time: 96.5 us; the launch traced here: 95.8 us
  waiting for transfers between devices  32.9 us (34%)
  starting transfers between devices  23.2 us (24%)
  Pallas kernels  13.4 us (14%)
  other arithmetic  11.5 us (12%)
  local copies, waits for them, and re-layouts  9.87 us (10%)
  between operations  2.89 us (3%)
  matrix products  2.13 us (2%)
    all_to_all x4, waiting for transfers between devices, exchange(): return lax.all_to_all(value, 'mass', 0, 0, tiled=True)  25.8 us
    all_to_all x4, starting transfers between devices, exchange(): return lax.all_to_all(value, 'mass', 0, 0, tiled=True)  17.7 us
    pallas_call x1, Pallas kernels, column_stage(): pl.pallas_call(column_kernel, out_shape=jax.ShapeDtypeStruct(received.sha...  11 us
    ppermute x2, waiting for transfers between devices, shards(): rate_gradient = rate_gradient + lax.ppermute(rate_gradient, 'scen', pairs)  7.08 us
    unnamed x20, local copies, waits for them, and re-layouts  4.8 us
    ppermute x2, starting transfers between devices, shards(): rate_gradient = rate_gradient + lax.ppermute(rate_gradient, 'scen', pairs)  4.3 us
    add x2, other arithmetic, shards(): rate_gradient = rate_gradient + lax.ppermute(rate_gradient, 'scen', pairs)  2.66 us
    pallas_call x1, Pallas kernels, prologue(): pl.pallas_call(functools.partial(prologue_kernel, nbin), out_shape=jax.Sh...  2.4 us
  transfers between devices with their start and end apart: 7, of which 5 were waited for; matrix products, arithmetic and copies ran while one was open for 16% of the time, Pallas kernels for 3%

profile of v11, /device:TPU:0, one launch (start us, length us, event | category | flops | bytes accessed | tf_op | source)
XLA Modules:
  0.0 95.8 jit_solution(11799605331863545957)
XLA Ops:
  0.6 1.2 %slice.42 = f32[1,1]{1,0:T(1,128)} slice(f32[1,65536]{1,0:T(1,128)} %param.13), slice={[0:1], [0:1]} | slice | bytes 8 | tf_op jit(solution)/shard_map/slice | solution.py:326
  1.8 1.3 %collective-permute-start = (f32[1,1]{1,0:T(1,128)}, f32[1,1]{1,0:T(1,128)}, u32[]{:S(2)}, u32[]{:S(2)}) collective-permute-start(f32[1,1]{1,0:T(1,128)} %slice.42), channel_id=1, source_target_pairs={{4,0},{8,4},{12,8},{16,12},{20,16},{24,20},{28,24},{5,1},{9,5},{13... | collective-permute-start | bytes 20 | tf_op jit(solution)/shard_map/ppermute | solution.py:22
  3.1 2.4 %shard_map.139 = f32[8,40,512]{2,1,0:T(8,128)} custom-call(s32[1]{0:T(128)} %bitcast.1.base_ref, f32[1,512,128]{2,1,0:T(8,128)} %bitcast.69, f32[1,512,128]{2,1,0:T(8,128)} %bitcast.64, f32[512,128]{1,0:T(8,128)} %bitcast.65), custom_call_target="tpu_custom_call" | custom-call | tf_op jit(solution)/shard_map/pallas_call | solution.py:261
  5.5 6.5 %all-to-all-start = ((f32[8,40,512]{2,1,0:T(8,128)}), f32[8,40,512]{2,1,0:T(8,128)S(1)}, u32[]{:S(2)}, u32[]{:S(2)}) async-start(f32[8,40,512]{2,1,0:T(8,128)} %shard_map.139), calls=%async_computation | async-start | bytes 1310720 | tf_op jit(solution)/shard_map/all_to_all | solution.py:271
  12.0 0.6 slice.41
  12.7 0.7 copy-done.8
  14.5 0.7 add_negate_fusion
  15.8 0.6 add_convert_fusion.flag_ref
  17.0 1.1 %pad_maximum_fusion.back_ref = f32[2,32,32,128]{3,2,1,0:T(8,128)} fusion(f32[1,32,32,128]{3,2,1,0:T(8,128)S(1)} %get-tuple-element.18, f32[1,32,32,128]{3,2,1,0:T(8,128)S(1)} %get-tuple-element.17), kind=kLoop, calls=%fused_computation.2 | loop fusion | flops 262144 | bytes 2097152 | tf_op jit(solution)/shard_map/stack | solution.py:201
  18.1 5.1 %all-to-all-done = f32[8,40,512]{2,1,0:T(8,128)S(1)} async-done(((f32[8,40,512]{2,1,0:T(8,128)}), f32[8,40,512]{2,1,0:T(8,128)S(1)}, u32[]{:S(2)}, u32[]{:S(2)}) %all-to-all-start) | async-done | bytes 655392 | tf_op jit(solution)/shard_map/all_to_all | solution.py:271
  23.3 1.0 %copy-done.5 = f32[2,256,2,128]{3,1,2,0:T(8,128)S(1)} copy-done((f32[2,256,2,128]{3,1,2,0:T(8,128)S(1)}, f32[2,256,2,128]{3,1,2,0:T(8,128)}, u32[]{:S(2)}) %copy-start.5) | copy-done | bytes 524312
  24.3 1.1 %convolution_bitcast_fusion = f32[2,1,256,512]{3,2,0,1:T(8,128)S(1)} fusion(f32[2,128,512,1]{2,1,0,3:T(8,128)S(1)} %bitcast.71, f32[2,256,2,128]{3,1,2,0:T(8,128)S(1)} %copy-done.5), kind=kOutput, calls=%fused_computation | convolution fusion | flops 805306368 | bytes 2097152 | tf_op jit(solution)/shard_map/okir,isrw->oskw/dot_general | solution.py:316
  25.6 1.1 %maximum_bitcast_fusion = f32[8,2,1,32,512]{4,3,2,1,0:T(8,128)} fusion(f32[1,1,8,32,512]{4,3,1,0,2:T(8,128)S(1)} %bitcast.74, f32[1,1,8,32,512]{4,3,1,0,2:T(8,128)S(1)} %bitcast.73), kind=kLoop, calls=%fused_computation.1 | loop fusion | flops 262144 | bytes 2097152 | tf_op jit(solution)/shard_map/transpose | solution.py:325
  26.7 3.9 %all-to-all-start.1 = ((f32[8,2,1,32,512]{4,3,2,1,0:T(8,128)}), f32[8,2,1,32,512]{4,3,2,1,0:T(8,128)S(1)}, u32[]{:S(2)}, u32[]{:S(2)}) async-start(f32[8,2,1,32,512]{4,3,2,1,0:T(8,128)} %maximum_bitcast_fusion), calls=%async_computation.1 | async-start | bytes 2097152 | tf_op jit(solution)/shard_map/all_to_all | solution.py:271
  30.6 1.4 %fusion = (f32[1,65536]{1,0:T(1,128)S(1)}, f32[1,65536]{1,0:T(1,128)S(1)}) fusion(f32[1,65536]{1,0:T(1,128)S(1)} %copy-done.1, f32[1,1]{1,0:T(1,128)} %collective-permute-done, f32[1,65535]{1,0:T(1,128)S(1)} %slice.41, f32[1,65536]{1,0:T(1,128)S(1)} %copy-done.3, s32[]{:T(128)} %mul.382, f32[1,65536]{1,0:T(1,128)S(1)} %bitcast.66), kind=kLoop, calls=%fused_computation.14 | loop fusion | flops 589824 | bytes 1572868 | tf_op jit(solution)/shard_map/mul | solution.py:328
  32.0 13.7 %all-to-all-done.1.x_ref = f32[8,2,1,32,512]{4,3,2,1,0:T(8,128)S(1)} async-done(((f32[8,2,1,32,512]{4,3,2,1,0:T(8,128)}), f32[8,2,1,32,512]{4,3,2,1,0:T(8,128)S(1)}, u32[]{:S(2)}, u32[]{:S(2)}) %all-to-all-start.1) | async-done | bytes 1048608 | tf_op jit(solution)/shard_map/all_to_all | solution.py:271
  45.7 1.0 %copy-done = f32[8,2,1,32,512]{4,3,2,1,0:T(8,128)} copy-done((f32[8,2,1,32,512]{4,3,2,1,0:T(8,128)}, f32[8,2,1,32,512]{4,3,2,1,0:T(8,128)S(1)}, u32[]{:S(2)}) %copy-start) | copy-done | bytes 1048600
  46.7 11.0 %shard_map.140 = f32[8,2,1,32,512]{4,3,2,1,0:T(8,128)} custom-call(f32[8,2,1,32,512]{4,3,2,1,0:T(8,128)} %copy-done, f32[2,32,1,128]{3,2,1,0:T(1,128)} %constant.148.phi_ref, f32[2,32,1,128]{3,2,1,0:T(1,128)} %constant.149.tw1_ref, f32[2,4,1,128]{3,2,1,0:T(1,128)} %constant.150.tw2_ref, f32[2,32,32,128]{3,2,1,0:T(8,128)} %pad_maximum_fusion.back_ref, ...), custom_call_target="tpu_custom_call" | custom-call | tf_op jit(solution)/shard_map/pallas_call | solution.py:207
  57.6 3.6 %all-to-all-start.2 = ((f32[8,2,1,32,512]{4,3,2,1,0:T(8,128)}), f32[8,2,1,32,512]{4,3,2,1,0:T(8,128)S(1)}, u32[]{:S(2)}, u32[]{:S(2)}) async-start(f32[8,2,1,32,512]{4,3,2,1,0:T(8,128)} %shard_map.140), calls=%async_computation.2 | async-start | bytes 2097152 | tf_op jit(solution)/shard_map/all_to_all | solution.py:271
  61.2 1.6 %collective-permute-start.1 = (f32[65536]{0:T(1024)S(1)}, f32[65536]{0:T(1024)}, u32[]{:S(2)}, u32[]{:S(2)}) collective-permute-start(f32[65536]{0:T(1024)S(1)} %bitcast.75), channel_id=1, source_target_pairs={{0,1},{1,0},{2,3},{3,2},{4,5},{5,4},{6,7},{7,6},{8,9},{9,8},{10,11... | collective-permute-start | bytes 786440 | tf_op jit(solution)/shard_map/ppermute | solution.py:336
  62.8 7.1 %collective-permute-done.1 = f32[65536]{0:T(1024)} collective-permute-done((f32[65536]{0:T(1024)S(1)}, f32[65536]{0:T(1024)}, u32[]{:S(2)}, u32[]{:S(2)}) %collective-permute-start.1) | collective-permute-done | bytes 262176 | tf_op jit(solution)/shard_map/ppermute | solution.py:336
  69.9 1.0 %add.176 = f32[65536]{0:T(1024)S(1)} add(f32[65536]{0:T(1024)S(1)} %bitcast.76, f32[65536]{0:T(1024)} %collective-permute-done.1) | non-fusion elementwise | flops 65536 | bytes 786432 | tf_op jit(solution)/shard_map/add | solution.py:336
  70.9 2.7 %collective-permute-start.2 = (f32[65536]{0:T(1024)S(1)}, f32[65536]{0:T(1024)}, u32[]{:S(2)}, u32[]{:S(2)}) collective-permute-start(f32[65536]{0:T(1024)S(1)} %add.176), channel_id=1, source_target_pairs={{0,2},{1,3},{2,0},{3,1},{4,6},{5,7},{6,4},{7,5},{8,10},{9,11},{10,... | collective-permute-start | bytes 786440 | tf_op jit(solution)/shard_map/ppermute | solution.py:336
  73.6 3.0 %all-to-all-done.2 = f32[8,2,1,32,512]{4,3,2,1,0:T(8,128)S(1)} async-done(((f32[8,2,1,32,512]{4,3,2,1,0:T(8,128)}), f32[8,2,1,32,512]{4,3,2,1,0:T(8,128)S(1)}, u32[]{:S(2)}, u32[]{:S(2)}) %all-to-all-start.2) | async-done | bytes 1048608 | tf_op jit(solution)/shard_map/all_to_all | solution.py:271
  76.6 0.9 copy-done.4
  77.6 1.1 %fusion.23 = f32[512,2,128,1]{0,2,3,1:T(8,128)S(1)} fusion(f32[2,256,512,1]{2,1,0,3:T(8,128)S(1)} %bitcast.63, f32[2,128,2,256]{3,1,2,0:T(8,128)S(1)} %copy-done.4), kind=kOutput, calls=%fused_computation.68 | convolution fusion | flops 805306368 | bytes 2097152 | tf_op jit(solution)/shard_map/orik,iskw->osrw/dot_general | solution.py:344
  78.7 0.9 copy.44
  79.5 3.7 %all-to-all-start.3 = ((f32[8,2,16,512]{3,2,1,0:T(8,128)}), f32[8,2,16,512]{3,2,1,0:T(8,128)S(1)}, u32[]{:S(2)}, u32[]{:S(2)}) async-start(f32[8,2,16,512]{3,2,1,0:T(8,128)} %bitcast.58), calls=%async_computation.3 | async-start | bytes 1048576 | tf_op jit(solution)/shard_map/all_to_all | solution.py:271
  83.2 0.6 maximum_multiply_fusion
  87.0 1.7 %add.177 = f32[65536]{0:T(1024)} add(f32[65536]{0:T(1024)S(1)} %add.176, f32[65536]{0:T(1024)} %collective-permute-done.2) | non-fusion elementwise | flops 65536 | bytes 786432 | tf_op jit(solution)/shard_map/add | solution.py:336
  88.7 4.0 %all-to-all-done.3 = f32[8,2,16,512]{3,2,1,0:T(8,128)S(1)} async-done(((f32[8,2,16,512]{3,2,1,0:T(8,128)}), f32[8,2,16,512]{3,2,1,0:T(8,128)S(1)}, u32[]{:S(2)}, u32[]{:S(2)}) %all-to-all-start.3) | async-done | bytes 524320 | tf_op jit(solution)/shard_map/all_to_all | solution.py:271
  93.7 2.2 %add_multiply_fusion = (f32[1,65536]{1,0:T(1,128)}, f32[1,65536]{1,0:T(1,128)}) fusion(f32[1,65536]{1,0:T(1,128)S(1)} %bitcast.82, f32[1,65536]{1,0:T(1,128)S(1)} %bitcast.67, f32[1,65536]{1,0:T(1,128)S(1)} %copy-done.1, f32[1,65536]{1,0:T(1,128)S(1)} %bitcast.79, f32[]{:T(128)} %bitcast.33, f32[]{:T(128)} %bitcast.28, s32[]{:T(128)} %mul.382, ...), kind=kLoop, calls=%fused_computation.19 | loop fusion | flops 1179648 | bytes 2359308 | tf_op jit(solution)/shard_map/mul | solution.py:352
  (44 shorter events, 4.8 us)
Async XLA Ops:
  1.8 28.7 %collective-permute-start = (f32[1,1]{1,0:T(1,128)}, f32[1,1]{1,0:T(1,128)}, u32[]{:S(2)}, u32[]{:S(2)}) collective-permute-start(f32[1,1]{1,0:T(1,128)} %slice.42), channel_id=1, source_target_pairs={{4,0},{8,4},{12,8},{16,12},{20,16},{24,20},{28,24},{5,1},{9,5},{13... | collective-permute-start | bytes 20 | tf_op jit(solution)/shard_map/ppermute | solution.py:22
  5.5 6.5 %copy-start.1 = (f32[1,65536]{1,0:T(1,128)S(1)}, f32[1,65536]{1,0:T(1,128)}, u32[]{:S(2)}) copy-start(f32[1,65536]{1,0:T(1,128)} %param.13) | copy-start | bytes 786436
  5.5 17.7 %all-to-all-start = ((f32[8,40,512]{2,1,0:T(8,128)}), f32[8,40,512]{2,1,0:T(8,128)S(1)}, u32[]{:S(2)}, u32[]{:S(2)}) async-start(f32[8,40,512]{2,1,0:T(8,128)} %shard_map.139), calls=%async_computation | async-start | bytes 1310720 | tf_op jit(solution)/shard_map/all_to_all | solution.py:271
  12.7 0.7 copy-start.8
  13.5 0.9 copy-start.6
  13.5 1.0 %copy-start.7 = (f32[256,128]{1,0:T(8,128)S(1)}, f32[256,128]{1,0:T(8,128)}, u32[]{:S(2)}) copy-start(f32[256,128]{1,0:T(8,128)} %constant.131.clone) | copy-start | bytes 393220
  23.2 1.0 %copy-start.5 = (f32[2,256,2,128]{3,1,2,0:T(8,128)S(1)}, f32[2,256,2,128]{3,1,2,0:T(8,128)}, u32[]{:S(2)}) copy-start(f32[2,256,2,128]{3,1,2,0:T(8,128)} %constant.147) | copy-start | bytes 1572868
  26.6 3.9 %copy-start.2 = (f32[65536]{0:T(1024)S(1)}, f32[65536]{0:T(1024)}, u32[]{:S(2)}) copy-start(f32[65536]{0:T(1024)} %param.14) | copy-start | bytes 786436
  26.7 3.9 %copy-start.3 = (f32[1,65536]{1,0:T(1,128)S(1)}, f32[1,65536]{1,0:T(1,128)}, u32[]{:S(2)}) copy-start(f32[1,65536]{1,0:T(1,128)} %param.12) | copy-start | bytes 786436
  26.7 19.0 %all-to-all-start.1 = ((f32[8,2,1,32,512]{4,3,2,1,0:T(8,128)}), f32[8,2,1,32,512]{4,3,2,1,0:T(8,128)S(1)}, u32[]{:S(2)}, u32[]{:S(2)}) async-start(f32[8,2,1,32,512]{4,3,2,1,0:T(8,128)} %maximum_bitcast_fusion), calls=%async_computation.1 | async-start | bytes 2097152 | tf_op jit(solution)/shard_map/all_to_all | solution.py:271
  45.7 1.0 %copy-start = (f32[8,2,1,32,512]{4,3,2,1,0:T(8,128)}, f32[8,2,1,32,512]{4,3,2,1,0:T(8,128)S(1)}, u32[]{:S(2)}) copy-start(f32[8,2,1,32,512]{4,3,2,1,0:T(8,128)S(1)} %all-to-all-done.1.x_ref) | copy-start | bytes 3145732
  57.6 18.9 %all-to-all-start.2 = ((f32[8,2,1,32,512]{4,3,2,1,0:T(8,128)}), f32[8,2,1,32,512]{4,3,2,1,0:T(8,128)S(1)}, u32[]{:S(2)}, u32[]{:S(2)}) async-start(f32[8,2,1,32,512]{4,3,2,1,0:T(8,128)} %shard_map.140), calls=%async_computation.2 | async-start | bytes 2097152 | tf_op jit(solution)/shard_map/all_to_all | solution.py:271
  61.2 8.7 %collective-permute-start.1 = (f32[65536]{0:T(1024)S(1)}, f32[65536]{0:T(1024)}, u32[]{:S(2)}, u32[]{:S(2)}) collective-permute-start(f32[65536]{0:T(1024)S(1)} %bitcast.75), channel_id=1, source_target_pairs={{0,1},{1,0},{2,3},{3,2},{4,5},{5,4},{6,7},{7,6},{8,9},{9,8},{10,11... | collective-permute-start | bytes 786440 | tf_op jit(solution)/shard_map/ppermute | solution.py:336
  70.9 16.1 %collective-permute-start.2 = (f32[65536]{0:T(1024)S(1)}, f32[65536]{0:T(1024)}, u32[]{:S(2)}, u32[]{:S(2)}) collective-permute-start(f32[65536]{0:T(1024)S(1)} %add.176), channel_id=1, source_target_pairs={{0,2},{1,3},{2,0},{3,1},{4,6},{5,7},{6,4},{7,5},{8,10},{9,11},{10,... | collective-permute-start | bytes 786440 | tf_op jit(solution)/shard_map/ppermute | solution.py:336
  76.5 1.0 %copy-start.4 = (f32[2,128,2,256]{3,1,2,0:T(8,128)S(1)}, f32[2,128,2,256]{3,1,2,0:T(8,128)}, u32[]{:S(2)}) copy-start(f32[2,128,2,256]{3,1,2,0:T(8,128)} %constant.161) | copy-start | bytes 1572868
  79.5 13.2 %all-to-all-start.3 = ((f32[8,2,16,512]{3,2,1,0:T(8,128)}), f32[8,2,16,512]{3,2,1,0:T(8,128)S(1)}, u32[]{:S(2)}, u32[]{:S(2)}) async-start(f32[8,2,16,512]{3,2,1,0:T(8,128)} %bitcast.58), calls=%async_computation.3 | async-start | bytes 1048576 | tf_op jit(solution)/shard_map/all_to_all | solution.py:271

commit v12 on v11

--- a/solution.py
+++ b/solution.py
@@ -231,13 +231,15 @@
         sums.append((jnp.sum(weighted), sc))
         sums.append((jnp.sum(c_ref[sc] * weighted), scen_dev + sc))
         flux_last.append(r_ref[lines - 1:lines, LANES - 1:LANES] * weighted[lines - 1:lines, LANES - 1:LANES])
+        flux_last.append(c_ref[sc, 0:1, 0:1])
     t_row = lax.broadcasted_iota(jnp.int32, (8, cols), 0)
     t_lane = lax.broadcasted_iota(jnp.int32, (8, cols), 1)
     tile = jnp.zeros((8, cols), jnp.float32)
     for value, slot in sums:
         tile = jnp.where((t_row == 0) & (t_lane == slot), value, tile)
     for sc in range(scen_dev):
-        tile = jnp.where((t_row == 1) & (t_lane == sc), flux_last[sc], tile)
+        tile = jnp.where((t_row == 1) & (t_lane == sc), flux_last[2 * sc], tile)
+        tile = jnp.where((t_row == 1) & (t_lane == scen_dev + sc), flux_last[2 * sc + 1], tile)
     s_line = lax.broadcasted_iota(jnp.int32, (rows, LANES), 0)
     s_lane = lax.broadcasted_iota(jnp.int32, (rows, LANES), 1)
     for j in range(parts):
@@ -294,9 +296,11 @@
     incoming_rows = exchange(outgoing)
     moments = jnp.sum(incoming_rows[:, arrays * rows, :arrays], axis=0)
     first, cross = moments[:scen_dev], moments[scen_dev:]
-    neighbours = incoming_rows[:, arrays * rows + 1, :scen_dev]
+    neighbours = incoming_rows[:, arrays * rows + 1, :arrays]
     behind = lax.dynamic_index_in_dim(neighbours, (place + parts - 1) % parts, keepdims=False)
-    incoming = jnp.where(place > 0, behind, 0.0)[:, None]
+    ahead = lax.dynamic_index_in_dim(neighbours, (place + 1) % parts, keepdims=False)
+    incoming = jnp.where(place > 0, behind[:scen_dev], 0.0)[:, None]
+    arriving = jnp.where(place < parts - 1, ahead[scen_dev:], 0.0)[:, None]
     spread = incoming_rows[:, : arrays * rows].reshape(parts, arrays, rows, cols)
     spread = spread.transpose(1, 0, 2, 3).reshape(arrays, half_rows, cols)
     half = block // 2
@@ -323,7 +327,6 @@
     tw_cos, tw_sin = tw_cos.reshape(full_rows, cols), tw_sin.reshape(full_rows, cols)
     twisted = jnp.stack(complex_mul((freq[0], freq[1]), (tw_cos, -tw_sin)))
     twisted = twisted.reshape(2, scen_dev, parts, block, cols).transpose(2, 0, 1, 3, 4)
-    arriving = from_behind(cotangent[:, :1], "mass", -1)
     following = jnp.concatenate([cotangent[:, 1:], arriving], axis=1)
     local_grad = jnp.sum(weighted * (following - cotangent), axis=0)
     received, local_grad = lax.optimization_barrier((exchange(twisted), local_grad))

time: 96.5 us -> 92.8 us (0.962)
  waiting for transfers between devices: 32.9 us -> 36.5 us
  other arithmetic: 11.5 us -> 8.4 us
  starting transfers between devices: 23.2 us -> 20.7 us
  local copies, waits for them, and re-layouts: 9.87 us -> 8.13 us
    all_to_all x4, waiting for transfers between devices: 25.8 us -> 29.5 us  [exchange(): return lax.all_to_all(value, 'mass', 0, 0, tiled=True)]
    add x2, other arithmetic: 2.66 us -> 0.76 us  [shards(): rate_gradient = rate_gradient + lax.ppermute(rate_gradient, 'scen', pairs)]
    ppermute x1 -> x0, starting transfers between devices: 1.28 us -> none  [from_behind(): lax.ppermute(value, axis, [(source, source + steps) for source in range(f...]
    all_to_all x4, starting transfers between devices: 17.7 us -> 16.4 us  [exchange(): return lax.all_to_all(value, 'mass', 0, 0, tiled=True)]
  transfers between devices with their start and end apart: 7 -> 6, of which waited for: 5 -> 5; matrix products, arithmetic and copies ran while one was open for 16% -> 10% of each run, Pallas kernels for 3% -> 0%
where the time goes in v12:
time: 92.8 us; the launch traced here: 92.1 us
  waiting for transfers between devices  36.5 us (39%)
  starting transfers between devices  20.7 us (22%)
  Pallas kernels  13.4 us (14%)
  other arithmetic  8.4 us (9%)
  local copies, waits for them, and re-layouts  8.13 us (9%)
  between operations  2.91 us (3%)
  matrix products  2.13 us (2%)
    all_to_all x4, waiting for transfers between devices, exchange(): return lax.all_to_all(value, 'mass', 0, 0, tiled=True)  29.5 us
    all_to_all x4, starting transfers between devices, exchange(): return lax.all_to_all(value, 'mass', 0, 0, tiled=True)  16.4 us
    pallas_call x1, Pallas kernels, column_stage(): pl.pallas_call(column_kernel, out_shape=jax.ShapeDtypeStruct(received.sha...  10.9 us
    ppermute x2, waiting for transfers between devices, shards(): rate_gradient = rate_gradient + lax.ppermute(rate_gradient, 'scen', pairs)  6.98 us
    ppermute x2, starting transfers between devices, shards(): rate_gradient = rate_gradient + lax.ppermute(rate_gradient, 'scen', pairs)  4.29 us
    unnamed x20, local copies, waits for them, and re-layouts  4.17 us
    pallas_call x1, Pallas kernels, prologue(): pl.pallas_call(functools.partial(prologue_kernel, nbin), out_shape=jax.Sh...  2.42 us
    mul x1, other arithmetic, shards(): mass[None, :]  2.15 us
  transfers between devices with their start and end apart: 6, of which 5 were waited for; matrix products, arithmetic and copies ran while one was open for 10% of the time, Pallas kernels for 0%

profile of v12, /device:TPU:0, one launch (start us, length us, event | category | flops | bytes accessed | tf_op | source)
XLA Modules:
  0.0 92.1 jit_solution(2387612985897143843)
XLA Ops:
  0.6 2.4 %shard_map.139 = f32[8,40,512]{2,1,0:T(8,128)} custom-call(s32[1]{0:T(128)} %bitcast.1.base_ref, f32[1,512,128]{2,1,0:T(8,128)} %bitcast.72, f32[1,512,128]{2,1,0:T(8,128)} %bitcast.67, f32[512,128]{1,0:T(8,128)} %bitcast.68), custom_call_target="tpu_custom_call" | custom-call | tf_op jit(solution)/shard_map/pallas_call | solution.py:263
  3.1 5.3 %all-to-all-start = ((f32[8,40,512]{2,1,0:T(8,128)}), f32[8,40,512]{2,1,0:T(8,128)S(1)}, u32[]{:S(2)}, u32[]{:S(2)}) async-start(f32[8,40,512]{2,1,0:T(8,128)} %shard_map.139), calls=%async_computation | async-start | bytes 1310720 | tf_op jit(solution)/shard_map/all_to_all | solution.py:273
  8.4 0.6 slice.50
  9.0 0.7 copy-done.8
  10.1 0.6 copy-done.6
  10.8 0.7 add_negate_fusion
  12.1 0.6 add_convert_fusion.flag_ref
  13.0 0.3 multiply_subtract_fusion
  13.4 1.1 %pad_maximum_fusion.back_ref = f32[2,32,32,128]{3,2,1,0:T(8,128)} fusion(f32[1,32,32,128]{3,2,1,0:T(8,128)S(1)} %get-tuple-element.20, f32[1,32,32,128]{3,2,1,0:T(8,128)S(1)} %get-tuple-element.19), kind=kLoop, calls=%fused_computation.2 | loop fusion | flops 262144 | bytes 2097152 | tf_op jit(solution)/shard_map/stack | solution.py:201
  14.4 5.1 %all-to-all-done = f32[8,40,512]{2,1,0:T(8,128)S(1)} async-done(((f32[8,40,512]{2,1,0:T(8,128)}), f32[8,40,512]{2,1,0:T(8,128)S(1)}, u32[]{:S(2)}, u32[]{:S(2)}) %all-to-all-start) | async-done | bytes 655392 | tf_op jit(solution)/shard_map/all_to_all | solution.py:273
  19.7 0.6 slice.52
  20.2 0.4 copy-done.5
  20.6 1.1 %convolution_bitcast_fusion = f32[2,1,256,512]{3,2,0,1:T(8,128)S(1)} fusion(f32[2,128,512,1]{2,1,0,3:T(8,128)S(1)} %bitcast.74, f32[2,256,2,128]{3,1,2,0:T(8,128)S(1)} %copy-done.5), kind=kOutput, calls=%fused_computation | convolution fusion | flops 805306368 | bytes 2097152 | tf_op jit(solution)/shard_map/okir,isrw->oskw/dot_general | solution.py:320
  21.9 1.1 %maximum_bitcast_fusion = f32[8,2,1,32,512]{4,3,2,1,0:T(8,128)} fusion(f32[1,1,8,32,512]{4,3,1,0,2:T(8,128)S(1)} %bitcast.77, f32[1,1,8,32,512]{4,3,1,0,2:T(8,128)S(1)} %bitcast.76), kind=kLoop, calls=%fused_computation.1 | loop fusion | flops 262144 | bytes 2097152 | tf_op jit(solution)/shard_map/transpose | solution.py:329
  23.0 3.9 %all-to-all-start.1 = ((f32[8,2,1,32,512]{4,3,2,1,0:T(8,128)}), f32[8,2,1,32,512]{4,3,2,1,0:T(8,128)S(1)}, u32[]{:S(2)}, u32[]{:S(2)}) async-start(f32[8,2,1,32,512]{4,3,2,1,0:T(8,128)} %maximum_bitcast_fusion), calls=%async_computation.1 | async-start | bytes 2097152 | tf_op jit(solution)/shard_map/all_to_all | solution.py:273
  27.5 0.8 fusion
  28.4 13.7 %all-to-all-done.1.x_ref = f32[8,2,1,32,512]{4,3,2,1,0:T(8,128)S(1)} async-done(((f32[8,2,1,32,512]{4,3,2,1,0:T(8,128)}), f32[8,2,1,32,512]{4,3,2,1,0:T(8,128)S(1)}, u32[]{:S(2)}, u32[]{:S(2)}) %all-to-all-start.1) | async-done | bytes 1048608 | tf_op jit(solution)/shard_map/all_to_all | solution.py:273
  42.0 1.0 %copy-done = f32[8,2,1,32,512]{4,3,2,1,0:T(8,128)} copy-done((f32[8,2,1,32,512]{4,3,2,1,0:T(8,128)}, f32[8,2,1,32,512]{4,3,2,1,0:T(8,128)S(1)}, u32[]{:S(2)}) %copy-start) | copy-done | bytes 1048600
  43.0 10.9 %shard_map.140 = f32[8,2,1,32,512]{4,3,2,1,0:T(8,128)} custom-call(f32[8,2,1,32,512]{4,3,2,1,0:T(8,128)} %copy-done, f32[2,32,1,128]{3,2,1,0:T(1,128)} %constant.157.phi_ref, f32[2,32,1,128]{3,2,1,0:T(1,128)} %constant.158.tw1_ref, f32[2,4,1,128]{3,2,1,0:T(1,128)} %constant.159.tw2_ref, f32[2,32,32,128]{3,2,1,0:T(8,128)} %pad_maximum_fusion.back_ref, ...), custom_call_target="tpu_custom_call" | custom-call | tf_op jit(solution)/shard_map/pallas_call | solution.py:207
  54.0 3.6 %all-to-all-start.2 = ((f32[8,2,1,32,512]{4,3,2,1,0:T(8,128)}), f32[8,2,1,32,512]{4,3,2,1,0:T(8,128)S(1)}, u32[]{:S(2)}, u32[]{:S(2)}) async-start(f32[8,2,1,32,512]{4,3,2,1,0:T(8,128)} %shard_map.140), calls=%async_computation.2 | async-start | bytes 2097152 | tf_op jit(solution)/shard_map/all_to_all | solution.py:273
  57.5 1.6 %collective-permute-start = (f32[65536]{0:T(1024)S(1)}, f32[65536]{0:T(1024)S(1)}, u32[]{:S(2)}, u32[]{:S(2)}) collective-permute-start(f32[65536]{0:T(1024)S(1)} %bitcast.78), channel_id=1, source_target_pairs={{0,1},{1,0},{2,3},{3,2},{4,5},{5,4},{6,7},{7,6},{8,9},{9,8},{10,11... | collective-permute-start | bytes 786440 | tf_op jit(solution)/shard_map/ppermute | solution.py:339
  59.2 7.0 %collective-permute-done = f32[65536]{0:T(1024)S(1)} collective-permute-done((f32[65536]{0:T(1024)S(1)}, f32[65536]{0:T(1024)S(1)}, u32[]{:S(2)}, u32[]{:S(2)}) %collective-permute-start) | collective-permute-done | bytes 262176 | tf_op jit(solution)/shard_map/ppermute | solution.py:339
  66.2 2.7 %collective-permute-start.1 = (f32[65536]{0:T(1024)S(1)}, f32[65536]{0:T(1024)S(1)}, u32[]{:S(2)}, u32[]{:S(2)}) collective-permute-start(f32[65536]{0:T(1024)S(1)} %add.188), channel_id=1, source_target_pairs={{0,2},{1,3},{2,0},{3,1},{4,6},{5,7},{6,4},{7,5},{8,10},{9,11},{10,... | collective-permute-start | bytes 786440 | tf_op jit(solution)/shard_map/ppermute | solution.py:339
  68.8 4.0 %all-to-all-done.2 = f32[8,2,1,32,512]{4,3,2,1,0:T(8,128)S(1)} async-done(((f32[8,2,1,32,512]{4,3,2,1,0:T(8,128)}), f32[8,2,1,32,512]{4,3,2,1,0:T(8,128)S(1)}, u32[]{:S(2)}, u32[]{:S(2)}) %all-to-all-start.2) | async-done | bytes 1048608 | tf_op jit(solution)/shard_map/all_to_all | solution.py:273
  73.0 0.9 %copy-done.4 = f32[2,128,2,256]{3,1,2,0:T(8,128)S(1)} copy-done((f32[2,128,2,256]{3,1,2,0:T(8,128)S(1)}, f32[2,128,2,256]{3,1,2,0:T(8,128)}, u32[]{:S(2)}) %copy-start.4) | copy-done | bytes 524312
  73.9 1.1 %fusion.23 = f32[512,2,128,1]{0,2,3,1:T(8,128)S(1)} fusion(f32[2,256,512,1]{2,1,0,3:T(8,128)S(1)} %bitcast.66, f32[2,128,2,256]{3,1,2,0:T(8,128)S(1)} %copy-done.4), kind=kOutput, calls=%fused_computation.69 | convolution fusion | flops 805306368 | bytes 2097152 | tf_op jit(solution)/shard_map/orik,iskw->osrw/dot_general | solution.py:347
  75.0 0.9 copy.44
  75.8 3.7 %all-to-all-start.3 = ((f32[8,2,16,512]{3,2,1,0:T(8,128)}), f32[8,2,16,512]{3,2,1,0:T(8,128)S(1)}, u32[]{:S(2)}, u32[]{:S(2)}) async-start(f32[8,2,16,512]{3,2,1,0:T(8,128)} %bitcast.60), calls=%async_computation.3 | async-start | bytes 1048576 | tf_op jit(solution)/shard_map/all_to_all | solution.py:273
  79.6 0.6 fusion.22
  81.6 0.7 add.189
  82.3 6.7 %all-to-all-done.3 = f32[8,2,16,512]{3,2,1,0:T(8,128)S(1)} async-done(((f32[8,2,16,512]{3,2,1,0:T(8,128)}), f32[8,2,16,512]{3,2,1,0:T(8,128)S(1)}, u32[]{:S(2)}, u32[]{:S(2)}) %all-to-all-start.3) | async-done | bytes 524320 | tf_op jit(solution)/shard_map/all_to_all | solution.py:273
  90.0 2.2 %add_multiply_fusion = (f32[1,65536]{1,0:T(1,128)}, f32[1,65536]{1,0:T(1,128)}) fusion(f32[1,65536]{1,0:T(1,128)S(1)} %bitcast.85, f32[1,65536]{1,0:T(1,128)S(1)} %bitcast.70, f32[1,65536]{1,0:T(1,128)S(1)} %copy-done.1, f32[1,65536]{1,0:T(1,128)S(1)} %bitcast.82, f32[]{:T(128)} %bitcast.36, f32[]{:T(128)} %bitcast.31, s32[]{:T(128)} %mul.382, ...), kind=kLoop, calls=%fused_computation.19 | loop fusion | flops 1179648 | bytes 2359308 | tf_op jit(solution)/shard_map/mul | solution.py:355
  (41 shorter events, 2.9 us)
Async XLA Ops:
  3.1 5.3 %copy-start.1 = (f32[1,65536]{1,0:T(1,128)S(1)}, f32[1,65536]{1,0:T(1,128)}, u32[]{:S(2)}) copy-start(f32[1,65536]{1,0:T(1,128)} %param.13) | copy-start | bytes 786436
  3.1 16.5 %all-to-all-start = ((f32[8,40,512]{2,1,0:T(8,128)}), f32[8,40,512]{2,1,0:T(8,128)S(1)}, u32[]{:S(2)}, u32[]{:S(2)}) async-start(f32[8,40,512]{2,1,0:T(8,128)} %shard_map.139), calls=%async_computation | async-start | bytes 1310720 | tf_op jit(solution)/shard_map/all_to_all | solution.py:273
  9.0 0.7 copy-start.8
  9.8 0.9 copy-start.6
  9.8 1.0 %copy-start.7 = (f32[256,128]{1,0:T(8,128)S(1)}, f32[256,128]{1,0:T(8,128)}, u32[]{:S(2)}) copy-start(f32[256,128]{1,0:T(8,128)} %constant.140.clone) | copy-start | bytes 393220
  19.6 1.0 %copy-start.5 = (f32[2,256,2,128]{3,1,2,0:T(8,128)S(1)}, f32[2,256,2,128]{3,1,2,0:T(8,128)}, u32[]{:S(2)}) copy-start(f32[2,256,2,128]{3,1,2,0:T(8,128)} %constant.156) | copy-start | bytes 1572868
  23.0 4.5 %copy-start.2 = (f32[65536]{0:T(1024)S(1)}, f32[65536]{0:T(1024)}, u32[]{:S(2)}) copy-start(f32[65536]{0:T(1024)} %param.14) | copy-start | bytes 786436
  23.0 4.5 %copy-start.3 = (f32[1,65536]{1,0:T(1,128)S(1)}, f32[1,65536]{1,0:T(1,128)}, u32[]{:S(2)}) copy-start(f32[1,65536]{1,0:T(1,128)} %param.12) | copy-start | bytes 786436
  23.0 19.0 %all-to-all-start.1 = ((f32[8,2,1,32,512]{4,3,2,1,0:T(8,128)}), f32[8,2,1,32,512]{4,3,2,1,0:T(8,128)S(1)}, u32[]{:S(2)}, u32[]{:S(2)}) async-start(f32[8,2,1,32,512]{4,3,2,1,0:T(8,128)} %maximum_bitcast_fusion), calls=%async_computation.1 | async-start | bytes 2097152 | tf_op jit(solution)/shard_map/all_to_all | solution.py:273
  42.0 1.0 %copy-start = (f32[8,2,1,32,512]{4,3,2,1,0:T(8,128)}, f32[8,2,1,32,512]{4,3,2,1,0:T(8,128)S(1)}, u32[]{:S(2)}) copy-start(f32[8,2,1,32,512]{4,3,2,1,0:T(8,128)S(1)} %all-to-all-done.1.x_ref) | copy-start | bytes 3145732
  54.0 18.9 %all-to-all-start.2 = ((f32[8,2,1,32,512]{4,3,2,1,0:T(8,128)}), f32[8,2,1,32,512]{4,3,2,1,0:T(8,128)S(1)}, u32[]{:S(2)}, u32[]{:S(2)}) async-start(f32[8,2,1,32,512]{4,3,2,1,0:T(8,128)} %shard_map.140), calls=%async_computation.2 | async-start | bytes 2097152 | tf_op jit(solution)/shard_map/all_to_all | solution.py:273
  57.5 8.6 %collective-permute-start = (f32[65536]{0:T(1024)S(1)}, f32[65536]{0:T(1024)S(1)}, u32[]{:S(2)}, u32[]{:S(2)}) collective-permute-start(f32[65536]{0:T(1024)S(1)} %bitcast.78), channel_id=1, source_target_pairs={{0,1},{1,0},{2,3},{3,2},{4,5},{5,4},{6,7},{7,6},{8,9},{9,8},{10,11... | collective-permute-start | bytes 786440 | tf_op jit(solution)/shard_map/ppermute | solution.py:339
  66.2 15.4 %collective-permute-start.1 = (f32[65536]{0:T(1024)S(1)}, f32[65536]{0:T(1024)S(1)}, u32[]{:S(2)}, u32[]{:S(2)}) collective-permute-start(f32[65536]{0:T(1024)S(1)} %add.188), channel_id=1, source_target_pairs={{0,2},{1,3},{2,0},{3,1},{4,6},{5,7},{6,4},{7,5},{8,10},{9,11},{10,... | collective-permute-start | bytes 786440 | tf_op jit(solution)/shard_map/ppermute | solution.py:339
  72.9 1.0 %copy-start.4 = (f32[2,128,2,256]{3,1,2,0:T(8,128)S(1)}, f32[2,128,2,256]{3,1,2,0:T(8,128)}, u32[]{:S(2)}) copy-start(f32[2,128,2,256]{3,1,2,0:T(8,128)} %constant.170) | copy-start | bytes 1572868
  75.8 13.2 %all-to-all-start.3 = ((f32[8,2,16,512]{3,2,1,0:T(8,128)}), f32[8,2,16,512]{3,2,1,0:T(8,128)S(1)}, u32[]{:S(2)}, u32[]{:S(2)}) async-start(f32[8,2,16,512]{3,2,1,0:T(8,128)} %bitcast.60), calls=%async_computation.3 | async-start | bytes 1048576 | tf_op jit(solution)/shard_map/all_to_all | solution.py:273

commit v13 on v12

--- a/solution.py
+++ b/solution.py
@@ -101,7 +101,7 @@
     parts, _, scen_dev, block, cols = x_ref.shape
     tiles = cols // LANES
     half = block // 2
-    high = lax.Precision.HIGHEST
+    high = lax.Precision.HIGH
     keep = flag_ref[0] > 0.5
     plain = flag_ref[1] > 0.5
     dft_cos = dft_ref[0]
@@ -317,7 +317,7 @@
     row_cos, row_sin = jnp.asarray(np.cos(row_angle), jnp.float32), jnp.asarray(np.sin(row_angle), jnp.float32)
     forward_rows = jnp.stack([jnp.stack([row_cos, row_sin], axis=1), jnp.stack([-row_sin, row_cos], axis=1)])
     packed = spread.reshape(2, scen_dev, half_rows, cols)
-    freq = jnp.einsum("okir,isrw->oskw", forward_rows, packed, precision=high)
+    freq = jnp.einsum("okir,isrw->oskw", forward_rows, packed, precision=lax.Precision.HIGH)
     tiles = cols // LANES
     coarse_cos, coarse_sin = phases(order, place * cols + counting(tiles) * LANES, nfft)
     fine_angle = 2.0 * np.pi * ((order_np[:, None] * np.arange(LANES)[None, :]) % nfft) / nfft
@@ -344,7 +344,7 @@
     returned = exchange(untwisted).transpose(1, 2, 0, 3, 4).reshape(2, scen_dev, full_rows, cols)
     inv_cos, inv_sin = row_cos.T, row_sin.T
     inverse_rows = jnp.stack([jnp.stack([inv_cos, -inv_sin], axis=1), jnp.stack([inv_sin, inv_cos], axis=1)])
-    real_part = jnp.einsum("orik,iskw->osrw", inverse_rows, returned, precision=high)
+    real_part = jnp.einsum("orik,iskw->osrw", inverse_rows, returned, precision=lax.Precision.HIGH)
     real_part = real_part.reshape(arrays, half_rows, cols)
     real_part = real_part.reshape(arrays, parts, rows, cols).transpose(1, 0, 2, 3)
     gathered = exchange(real_part).transpose(1, 2, 0, 3).reshape(arrays, bin_dev) / nfft

time: 92.8 us -> 88.3 us (0.952)
  Pallas kernels: 13.4 us -> 9.87 us
  matrix products: 2.13 us -> 1.2 us
    pallas_call x1, Pallas kernels: 10.9 us -> 7.45 us  [column_stage(): pl.pallas_call(column_kernel, out_shape=jax.ShapeDtypeStruct(received.sha...]
    dot_general x2, matrix products: 2.13 us -> 1.2 us  [the longest x1 0.6 us: shards(): jnp.einsum('orik,iskw->osrw', inverse_rows, returned, precision=lax.Preci...]
where the time goes in v13:
time: 88.3 us; the launch traced here: 87.7 us
  waiting for transfers between devices  36.7 us (42%)
  starting transfers between devices  20.5 us (23%)
  Pallas kernels  9.87 us (11%)
  other arithmetic  8.4 us (10%)
  local copies, waits for them, and re-layouts  8.13 us (9%)
  between operations  2.91 us (3%)
  matrix products  1.2 us (1%)
    all_to_all x4, waiting for transfers between devices, exchange(): return lax.all_to_all(value, 'mass', 0, 0, tiled=True)  29.7 us
    all_to_all x4, starting transfers between devices, exchange(): return lax.all_to_all(value, 'mass', 0, 0, tiled=True)  16.2 us
    pallas_call x1, Pallas kernels, column_stage(): pl.pallas_call(column_kernel, out_shape=jax.ShapeDtypeStruct(received.sha...  7.45 us
    ppermute x2, waiting for transfers between devices, shards(): rate_gradient = rate_gradient + lax.ppermute(rate_gradient, 'scen', pairs)  6.98 us
    ppermute x2, starting transfers between devices, shards(): rate_gradient = rate_gradient + lax.ppermute(rate_gradient, 'scen', pairs)  4.3 us
    unnamed x20, local copies, waits for them, and re-layouts  4.17 us
    pallas_call x1, Pallas kernels, prologue(): pl.pallas_call(functools.partial(prologue_kernel, nbin), out_shape=jax.Sh...  2.42 us
    mul x1, other arithmetic, shards(): mass[None, :]  2.15 us
  transfers between devices with their start and end apart: 6, of which 5 were waited for; matrix products, arithmetic and copies ran while one was open for 10% of the time, Pallas kernels for 0%

profile of v13, /device:TPU:0, one launch (start us, length us, event | category | flops | bytes accessed | tf_op | source)
XLA Modules:
  0.0 87.7 jit_solution(12811402091640987050)
XLA Ops:
  0.6 2.4 %shard_map.139 = f32[8,40,512]{2,1,0:T(8,128)} custom-call(s32[1]{0:T(128)} %bitcast.1.base_ref, f32[1,512,128]{2,1,0:T(8,128)} %bitcast.72, f32[1,512,128]{2,1,0:T(8,128)} %bitcast.67, f32[512,128]{1,0:T(8,128)} %bitcast.68), custom_call_target="tpu_custom_call" | custom-call | tf_op jit(solution)/shard_map/pallas_call | solution.py:263
  3.1 5.3 %all-to-all-start = ((f32[8,40,512]{2,1,0:T(8,128)}), f32[8,40,512]{2,1,0:T(8,128)S(1)}, u32[]{:S(2)}, u32[]{:S(2)}) async-start(f32[8,40,512]{2,1,0:T(8,128)} %shard_map.139), calls=%async_computation | async-start | bytes 1310720 | tf_op jit(solution)/shard_map/all_to_all | solution.py:273
  8.4 0.6 slice.50
  9.0 0.7 copy-done.8
  10.1 0.6 copy-done.6
  10.8 0.7 add_negate_fusion
  12.1 0.6 add_convert_fusion.flag_ref
  13.0 0.3 multiply_subtract_fusion
  13.4 1.1 %pad_maximum_fusion.back_ref = f32[2,32,32,128]{3,2,1,0:T(8,128)} fusion(f32[1,32,32,128]{3,2,1,0:T(8,128)S(1)} %get-tuple-element.20, f32[1,32,32,128]{3,2,1,0:T(8,128)S(1)} %get-tuple-element.19), kind=kLoop, calls=%fused_computation.2 | loop fusion | flops 262144 | bytes 2097152 | tf_op jit(solution)/shard_map/stack | solution.py:201
  14.4 5.1 %all-to-all-done = f32[8,40,512]{2,1,0:T(8,128)S(1)} async-done(((f32[8,40,512]{2,1,0:T(8,128)}), f32[8,40,512]{2,1,0:T(8,128)S(1)}, u32[]{:S(2)}, u32[]{:S(2)}) %all-to-all-start) | async-done | bytes 655392 | tf_op jit(solution)/shard_map/all_to_all | solution.py:273
  19.7 0.6 slice.52
  20.2 0.4 copy-done.5
  20.6 0.6 convolution_bitcast_fusion
  21.5 1.1 %maximum_bitcast_fusion = f32[8,2,1,32,512]{4,3,2,1,0:T(8,128)} fusion(f32[1,1,8,32,512]{4,3,1,0,2:T(8,128)S(1)} %bitcast.77, f32[1,1,8,32,512]{4,3,1,0,2:T(8,128)S(1)} %bitcast.76), kind=kLoop, calls=%fused_computation.1 | loop fusion | flops 262144 | bytes 2097152 | tf_op jit(solution)/shard_map/transpose | solution.py:329
  22.5 3.7 %all-to-all-start.1 = ((f32[8,2,1,32,512]{4,3,2,1,0:T(8,128)}), f32[8,2,1,32,512]{4,3,2,1,0:T(8,128)S(1)}, u32[]{:S(2)}, u32[]{:S(2)}) async-start(f32[8,2,1,32,512]{4,3,2,1,0:T(8,128)} %maximum_bitcast_fusion), calls=%async_computation.1 | async-start | bytes 2097152 | tf_op jit(solution)/shard_map/all_to_all | solution.py:273
  26.9 0.8 fusion
  27.7 13.8 %all-to-all-done.1.x_ref = f32[8,2,1,32,512]{4,3,2,1,0:T(8,128)S(1)} async-done(((f32[8,2,1,32,512]{4,3,2,1,0:T(8,128)}), f32[8,2,1,32,512]{4,3,2,1,0:T(8,128)S(1)}, u32[]{:S(2)}, u32[]{:S(2)}) %all-to-all-start.1) | async-done | bytes 1048608 | tf_op jit(solution)/shard_map/all_to_all | solution.py:273
  41.6 1.0 %copy-done = f32[8,2,1,32,512]{4,3,2,1,0:T(8,128)} copy-done((f32[8,2,1,32,512]{4,3,2,1,0:T(8,128)}, f32[8,2,1,32,512]{4,3,2,1,0:T(8,128)S(1)}, u32[]{:S(2)}) %copy-start) | copy-done | bytes 1048600
  42.5 7.5 %shard_map.140 = f32[8,2,1,32,512]{4,3,2,1,0:T(8,128)} custom-call(f32[8,2,1,32,512]{4,3,2,1,0:T(8,128)} %copy-done, f32[2,32,1,128]{3,2,1,0:T(1,128)} %constant.157.phi_ref, f32[2,32,1,128]{3,2,1,0:T(1,128)} %constant.158.tw1_ref, f32[2,4,1,128]{3,2,1,0:T(1,128)} %constant.159.tw2_ref, f32[2,32,32,128]{3,2,1,0:T(8,128)} %pad_maximum_fusion.back_ref, ...), custom_call_target="tpu_custom_call" | custom-call | tf_op jit(solution)/shard_map/pallas_call | solution.py:207
  50.0 3.6 %all-to-all-start.2 = ((f32[8,2,1,32,512]{4,3,2,1,0:T(8,128)}), f32[8,2,1,32,512]{4,3,2,1,0:T(8,128)S(1)}, u32[]{:S(2)}, u32[]{:S(2)}) async-start(f32[8,2,1,32,512]{4,3,2,1,0:T(8,128)} %shard_map.140), calls=%async_computation.2 | async-start | bytes 2097152 | tf_op jit(solution)/shard_map/all_to_all | solution.py:273
  53.6 1.6 %collective-permute-start = (f32[65536]{0:T(1024)S(1)}, f32[65536]{0:T(1024)S(1)}, u32[]{:S(2)}, u32[]{:S(2)}) collective-permute-start(f32[65536]{0:T(1024)S(1)} %bitcast.78), channel_id=1, source_target_pairs={{0,1},{1,0},{2,3},{3,2},{4,5},{5,4},{6,7},{7,6},{8,9},{9,8},{10,11... | collective-permute-start | bytes 786440 | tf_op jit(solution)/shard_map/ppermute | solution.py:339
  55.2 7.0 %collective-permute-done = f32[65536]{0:T(1024)S(1)} collective-permute-done((f32[65536]{0:T(1024)S(1)}, f32[65536]{0:T(1024)S(1)}, u32[]{:S(2)}, u32[]{:S(2)}) %collective-permute-start) | collective-permute-done | bytes 262176 | tf_op jit(solution)/shard_map/ppermute | solution.py:339
  62.2 2.7 %collective-permute-start.1 = (f32[65536]{0:T(1024)S(1)}, f32[65536]{0:T(1024)S(1)}, u32[]{:S(2)}, u32[]{:S(2)}) collective-permute-start(f32[65536]{0:T(1024)S(1)} %add.188), channel_id=1, source_target_pairs={{0,2},{1,3},{2,0},{3,1},{4,6},{5,7},{6,4},{7,5},{8,10},{9,11},{10,... | collective-permute-start | bytes 786440 | tf_op jit(solution)/shard_map/ppermute | solution.py:339
  64.9 4.0 %all-to-all-done.2 = f32[8,2,1,32,512]{4,3,2,1,0:T(8,128)S(1)} async-done(((f32[8,2,1,32,512]{4,3,2,1,0:T(8,128)}), f32[8,2,1,32,512]{4,3,2,1,0:T(8,128)S(1)}, u32[]{:S(2)}, u32[]{:S(2)}) %all-to-all-start.2) | async-done | bytes 1048608 | tf_op jit(solution)/shard_map/all_to_all | solution.py:273
  69.0 0.9 %copy-done.4 = f32[2,128,2,256]{3,1,2,0:T(8,128)S(1)} copy-done((f32[2,128,2,256]{3,1,2,0:T(8,128)S(1)}, f32[2,128,2,256]{3,1,2,0:T(8,128)}, u32[]{:S(2)}) %copy-start.4) | copy-done | bytes 524312
  69.9 0.6 fusion.23
  70.6 0.9 copy.44
  71.4 3.7 %all-to-all-start.3 = ((f32[8,2,16,512]{3,2,1,0:T(8,128)}), f32[8,2,16,512]{3,2,1,0:T(8,128)S(1)}, u32[]{:S(2)}, u32[]{:S(2)}) async-start(f32[8,2,16,512]{3,2,1,0:T(8,128)} %bitcast.60), calls=%async_computation.3 | async-start | bytes 1048576 | tf_op jit(solution)/shard_map/all_to_all | solution.py:273
  75.2 0.6 fusion.22
  77.1 0.7 add.189
  77.8 6.8 %all-to-all-done.3 = f32[8,2,16,512]{3,2,1,0:T(8,128)S(1)} async-done(((f32[8,2,16,512]{3,2,1,0:T(8,128)}), f32[8,2,16,512]{3,2,1,0:T(8,128)S(1)}, u32[]{:S(2)}, u32[]{:S(2)}) %all-to-all-start.3) | async-done | bytes 524320 | tf_op jit(solution)/shard_map/all_to_all | solution.py:273
  85.6 2.2 %add_multiply_fusion = (f32[1,65536]{1,0:T(1,128)}, f32[1,65536]{1,0:T(1,128)}) fusion(f32[1,65536]{1,0:T(1,128)S(1)} %bitcast.85, f32[1,65536]{1,0:T(1,128)S(1)} %bitcast.70, f32[1,65536]{1,0:T(1,128)S(1)} %copy-done.1, f32[1,65536]{1,0:T(1,128)S(1)} %bitcast.82, f32[]{:T(128)} %bitcast.36, f32[]{:T(128)} %bitcast.31, s32[]{:T(128)} %mul.382, ...), kind=kLoop, calls=%fused_computation.19 | loop fusion | flops 1179648 | bytes 2359308 | tf_op jit(solution)/shard_map/mul | solution.py:355
  (41 shorter events, 2.9 us)
Async XLA Ops:
  3.1 5.3 %copy-start.1 = (f32[1,65536]{1,0:T(1,128)S(1)}, f32[1,65536]{1,0:T(1,128)}, u32[]{:S(2)}) copy-start(f32[1,65536]{1,0:T(1,128)} %param.13) | copy-start | bytes 786436
  3.1 16.5 %all-to-all-start = ((f32[8,40,512]{2,1,0:T(8,128)}), f32[8,40,512]{2,1,0:T(8,128)S(1)}, u32[]{:S(2)}, u32[]{:S(2)}) async-start(f32[8,40,512]{2,1,0:T(8,128)} %shard_map.139), calls=%async_computation | async-start | bytes 1310720 | tf_op jit(solution)/shard_map/all_to_all | solution.py:273
  9.0 0.7 copy-start.8
  9.8 0.9 %copy-start.6 = (f32[256,128]{1,0:T(8,128)S(1)}, f32[256,128]{1,0:T(8,128)}, u32[]{:S(2)}) copy-start(f32[256,128]{1,0:T(8,128)} %constant.141.clone) | copy-start | bytes 393220
  9.8 1.0 %copy-start.7 = (f32[256,128]{1,0:T(8,128)S(1)}, f32[256,128]{1,0:T(8,128)}, u32[]{:S(2)}) copy-start(f32[256,128]{1,0:T(8,128)} %constant.140.clone) | copy-start | bytes 393220
  19.6 1.0 %copy-start.5 = (f32[2,256,2,128]{3,1,2,0:T(8,128)S(1)}, f32[2,256,2,128]{3,1,2,0:T(8,128)}, u32[]{:S(2)}) copy-start(f32[2,256,2,128]{3,1,2,0:T(8,128)} %constant.156) | copy-start | bytes 1572868
  22.5 4.3 %copy-start.2 = (f32[65536]{0:T(1024)S(1)}, f32[65536]{0:T(1024)}, u32[]{:S(2)}) copy-start(f32[65536]{0:T(1024)} %param.14) | copy-start | bytes 786436
  22.5 4.4 %copy-start.3 = (f32[1,65536]{1,0:T(1,128)S(1)}, f32[1,65536]{1,0:T(1,128)}, u32[]{:S(2)}) copy-start(f32[1,65536]{1,0:T(1,128)} %param.12) | copy-start | bytes 786436
  22.5 19.0 %all-to-all-start.1 = ((f32[8,2,1,32,512]{4,3,2,1,0:T(8,128)}), f32[8,2,1,32,512]{4,3,2,1,0:T(8,128)S(1)}, u32[]{:S(2)}, u32[]{:S(2)}) async-start(f32[8,2,1,32,512]{4,3,2,1,0:T(8,128)} %maximum_bitcast_fusion), calls=%async_computation.1 | async-start | bytes 2097152 | tf_op jit(solution)/shard_map/all_to_all | solution.py:273
  41.6 1.0 %copy-start = (f32[8,2,1,32,512]{4,3,2,1,0:T(8,128)}, f32[8,2,1,32,512]{4,3,2,1,0:T(8,128)S(1)}, u32[]{:S(2)}) copy-start(f32[8,2,1,32,512]{4,3,2,1,0:T(8,128)S(1)} %all-to-all-done.1.x_ref) | copy-start | bytes 3145732
  50.0 18.9 %all-to-all-start.2 = ((f32[8,2,1,32,512]{4,3,2,1,0:T(8,128)}), f32[8,2,1,32,512]{4,3,2,1,0:T(8,128)S(1)}, u32[]{:S(2)}, u32[]{:S(2)}) async-start(f32[8,2,1,32,512]{4,3,2,1,0:T(8,128)} %shard_map.140), calls=%async_computation.2 | async-start | bytes 2097152 | tf_op jit(solution)/shard_map/all_to_all | solution.py:273
  53.6 8.6 %collective-permute-start = (f32[65536]{0:T(1024)S(1)}, f32[65536]{0:T(1024)S(1)}, u32[]{:S(2)}, u32[]{:S(2)}) collective-permute-start(f32[65536]{0:T(1024)S(1)} %bitcast.78), channel_id=1, source_target_pairs={{0,1},{1,0},{2,3},{3,2},{4,5},{5,4},{6,7},{7,6},{8,9},{9,8},{10,11... | collective-permute-start | bytes 786440 | tf_op jit(solution)/shard_map/ppermute | solution.py:339
  62.2 14.9 %collective-permute-start.1 = (f32[65536]{0:T(1024)S(1)}, f32[65536]{0:T(1024)S(1)}, u32[]{:S(2)}, u32[]{:S(2)}) collective-permute-start(f32[65536]{0:T(1024)S(1)} %add.188), channel_id=1, source_target_pairs={{0,2},{1,3},{2,0},{3,1},{4,6},{5,7},{6,4},{7,5},{8,10},{9,11},{10,... | collective-permute-start | bytes 786440 | tf_op jit(solution)/shard_map/ppermute | solution.py:339
  68.9 1.0 %copy-start.4 = (f32[2,128,2,256]{3,1,2,0:T(8,128)S(1)}, f32[2,128,2,256]{3,1,2,0:T(8,128)}, u32[]{:S(2)}) copy-start(f32[2,128,2,256]{3,1,2,0:T(8,128)} %constant.170) | copy-start | bytes 1572868
  71.4 13.2 %all-to-all-start.3 = ((f32[8,2,16,512]{3,2,1,0:T(8,128)}), f32[8,2,16,512]{3,2,1,0:T(8,128)S(1)}, u32[]{:S(2)}, u32[]{:S(2)}) async-start(f32[8,2,16,512]{3,2,1,0:T(8,128)} %bitcast.60), calls=%async_computation.3 | async-start | bytes 1048576 | tf_op jit(solution)/shard_map/all_to_all | solution.py:273

commit v14 on v13

--- a/solution.py
+++ b/solution.py
@@ -317,7 +317,8 @@
     row_cos, row_sin = jnp.asarray(np.cos(row_angle), jnp.float32), jnp.asarray(np.sin(row_angle), jnp.float32)
     forward_rows = jnp.stack([jnp.stack([row_cos, row_sin], axis=1), jnp.stack([-row_sin, row_cos], axis=1)])
     packed = spread.reshape(2, scen_dev, half_rows, cols)
-    freq = jnp.einsum("okir,isrw->oskw", forward_rows, packed, precision=lax.Precision.HIGH)
+    forward_rows = forward_rows.reshape(2, parts, block, 2, half_rows)
+    freq = jnp.einsum("ojkir,isrw->joskw", forward_rows, packed, precision=lax.Precision.HIGH)
     tiles = cols // LANES
     coarse_cos, coarse_sin = phases(order, place * cols + counting(tiles) * LANES, nfft)
     fine_angle = 2.0 * np.pi * ((order_np[:, None] * np.arange(LANES)[None, :]) % nfft) / nfft
@@ -325,8 +326,9 @@
     fine_sin = jnp.asarray(np.sin(fine_angle), jnp.float32)[:, None, :]
     tw_cos, tw_sin = complex_mul((coarse_cos[:, :, None], coarse_sin[:, :, None]), (fine_cos, fine_sin))
     tw_cos, tw_sin = tw_cos.reshape(full_rows, cols), tw_sin.reshape(full_rows, cols)
-    twisted = jnp.stack(complex_mul((freq[0], freq[1]), (tw_cos, -tw_sin)))
-    twisted = twisted.reshape(2, scen_dev, parts, block, cols).transpose(2, 0, 1, 3, 4)
+    tw_cos = tw_cos.reshape(parts, 1, block, cols)
+    tw_sin = tw_sin.reshape(parts, 1, block, cols)
+    twisted = jnp.stack(complex_mul((freq[:, 0], freq[:, 1]), (tw_cos, -tw_sin)), axis=1)
     following = jnp.concatenate([cotangent[:, 1:], arriving], axis=1)
     local_grad = jnp.sum(weighted * (following - cotangent), axis=0)
     received, local_grad = lax.optimization_barrier((exchange(twisted), local_grad))
@@ -344,9 +346,9 @@
     returned = exchange(untwisted).transpose(1, 2, 0, 3, 4).reshape(2, scen_dev, full_rows, cols)
     inv_cos, inv_sin = row_cos.T, row_sin.T
     inverse_rows = jnp.stack([jnp.stack([inv_cos, -inv_sin], axis=1), jnp.stack([inv_sin, inv_cos], axis=1)])
-    real_part = jnp.einsum("orik,iskw->osrw", inverse_rows, returned, precision=lax.Precision.HIGH)
-    real_part = real_part.reshape(arrays, half_rows, cols)
-    real_part = real_part.reshape(arrays, parts, rows, cols).transpose(1, 0, 2, 3)
+    inverse_rows = inverse_rows.reshape(2, parts, rows, 2, full_rows)
+    real_part = jnp.einsum("ojrik,iskw->josrw", inverse_rows, returned, precision=lax.Precision.HIGH)
+    real_part = real_part.reshape(parts, arrays, rows, cols)
     gathered = exchange(real_part).transpose(1, 2, 0, 3).reshape(arrays, bin_dev) / nfft
     birth = gathered[:scen_dev]
     corr = gathered[scen_dev:]

time: 88.3 us -> 88.3 us (level)
    another operation x0 -> x1, other arithmetic: none -> 1.05 us  [shards(): jnp.stack(complex_mul((freq[:, 0], freq[:, 1]), (tw_cos, -tw_sin)), axis=1)]
    transpose x1 -> x0, other arithmetic: 1.05 us -> none  [shards(): twisted.reshape(2, scen_dev, parts, block, cols).transpose(2, 0, 1, 3, 4)]
where the time goes in v14:
time: 88.3 us; the launch traced here: 87.7 us
  waiting for transfers between devices  36.7 us (42%)
  starting transfers between devices  20.5 us (23%)
  Pallas kernels  9.87 us (11%)
  other arithmetic  8.39 us (10%)
  local copies, waits for them, and re-layouts  8.13 us (9%)
  between operations  2.91 us (3%)
  matrix products  1.2 us (1%)
    all_to_all x4, waiting for transfers between devices, exchange(): return lax.all_to_all(value, 'mass', 0, 0, tiled=True)  29.7 us
    all_to_all x4, starting transfers between devices, exchange(): return lax.all_to_all(value, 'mass', 0, 0, tiled=True)  16.2 us
    pallas_call x1, Pallas kernels, column_stage(): pl.pallas_call(column_kernel, out_shape=jax.ShapeDtypeStruct(received.sha...  7.45 us
    ppermute x2, waiting for transfers between devices, shards(): rate_gradient = rate_gradient + lax.ppermute(rate_gradient, 'scen', pairs)  6.98 us
    ppermute x2, starting transfers between devices, shards(): rate_gradient = rate_gradient + lax.ppermute(rate_gradient, 'scen', pairs)  4.3 us
    unnamed x20, local copies, waits for them, and re-layouts  4.17 us
    pallas_call x1, Pallas kernels, prologue(): pl.pallas_call(functools.partial(prologue_kernel, nbin), out_shape=jax.Sh...  2.42 us
    mul x1, other arithmetic, shards(): mass[None, :]  2.15 us
  transfers between devices with their start and end apart: 6, of which 5 were waited for; matrix products, arithmetic and copies ran while one was open for 10% of the time, Pallas kernels for 0%

profile of v14, /device:TPU:0, one launch (start us, length us, event | category | flops | bytes accessed | tf_op | source)
XLA Modules:
  0.0 87.7 jit_solution(11558932590931964757)
XLA Ops:
  0.6 2.4 %shard_map.139 = f32[8,40,512]{2,1,0:T(8,128)} custom-call(s32[1]{0:T(128)} %bitcast.base_ref, f32[1,512,128]{2,1,0:T(8,128)} %bitcast.65, f32[1,512,128]{2,1,0:T(8,128)} %bitcast.60, f32[512,128]{1,0:T(8,128)} %bitcast.61), custom_call_target="tpu_custom_call" | custom-call | tf_op jit(solution)/shard_map/pallas_call | solution.py:263
  3.1 5.3 %all-to-all-start = ((f32[8,40,512]{2,1,0:T(8,128)}), f32[8,40,512]{2,1,0:T(8,128)S(1)}, u32[]{:S(2)}, u32[]{:S(2)}) async-start(f32[8,40,512]{2,1,0:T(8,128)} %shard_map.139), calls=%async_computation | async-start | bytes 1310720 | tf_op jit(solution)/shard_map/all_to_all | solution.py:273
  8.4 0.6 slice.50
  9.0 0.7 copy-done.7
  10.1 0.6 copy-done.5
  10.8 0.7 add_negate_fusion
  12.1 0.6 add_convert_fusion.flag_ref
  13.0 0.3 multiply_subtract_fusion
  13.4 1.1 %pad_maximum_fusion.1.back_ref = f32[2,32,32,128]{3,2,1,0:T(8,128)} fusion(f32[1,32,32,128]{3,2,1,0:T(8,128)S(1)} %get-tuple-element.20, f32[1,32,32,128]{3,2,1,0:T(8,128)S(1)} %get-tuple-element.19), kind=kLoop, calls=%fused_computation.3 | loop fusion | flops 262144 | bytes 2097152 | tf_op jit(solution)/shard_map/stack | solution.py:201
  14.4 5.1 %all-to-all-done = f32[8,40,512]{2,1,0:T(8,128)S(1)} async-done(((f32[8,40,512]{2,1,0:T(8,128)}), f32[8,40,512]{2,1,0:T(8,128)S(1)}, u32[]{:S(2)}, u32[]{:S(2)}) %all-to-all-start) | async-done | bytes 655392 | tf_op jit(solution)/shard_map/all_to_all | solution.py:273
  19.7 0.6 slice.52
  20.2 0.4 copy-done.4
  20.6 0.6 convolution_bitcast_fusion
  21.4 1.1 %pad_maximum_fusion = f32[8,2,1,32,512]{4,3,2,1,0:T(8,128)} fusion(f32[8,1,1,32,512]{4,3,2,1,0:T(8,128)S(1)} %get-tuple-element.8, f32[8,1,1,32,512]{4,3,2,1,0:T(8,128)S(1)} %get-tuple-element.7), kind=kLoop, calls=%fused_computation.2 | loop fusion | flops 262144 | bytes 2097152 | tf_op jit(solution)/shard_map/stack | solution.py:331
  22.5 3.7 %all-to-all-start.1 = ((f32[8,2,1,32,512]{4,3,2,1,0:T(8,128)}), f32[8,2,1,32,512]{4,3,2,1,0:T(8,128)S(1)}, u32[]{:S(2)}, u32[]{:S(2)}) async-start(f32[8,2,1,32,512]{4,3,2,1,0:T(8,128)} %pad_maximum_fusion), calls=%async_computation.1 | async-start | bytes 2097152 | tf_op jit(solution)/shard_map/all_to_all | solution.py:273
  26.9 0.8 fusion
  27.7 13.8 %all-to-all-done.1.x_ref = f32[8,2,1,32,512]{4,3,2,1,0:T(8,128)S(1)} async-done(((f32[8,2,1,32,512]{4,3,2,1,0:T(8,128)}), f32[8,2,1,32,512]{4,3,2,1,0:T(8,128)S(1)}, u32[]{:S(2)}, u32[]{:S(2)}) %all-to-all-start.1) | async-done | bytes 1048608 | tf_op jit(solution)/shard_map/all_to_all | solution.py:273
  41.5 1.0 %copy-done = f32[8,2,1,32,512]{4,3,2,1,0:T(8,128)} copy-done((f32[8,2,1,32,512]{4,3,2,1,0:T(8,128)}, f32[8,2,1,32,512]{4,3,2,1,0:T(8,128)S(1)}, u32[]{:S(2)}) %copy-start) | copy-done | bytes 1048600
  42.5 7.5 %shard_map.140 = f32[8,2,1,32,512]{4,3,2,1,0:T(8,128)} custom-call(f32[8,2,1,32,512]{4,3,2,1,0:T(8,128)} %copy-done, f32[2,32,1,128]{3,2,1,0:T(1,128)} %constant.155.phi_ref, f32[2,32,1,128]{3,2,1,0:T(1,128)} %constant.156.tw1_ref, f32[2,4,1,128]{3,2,1,0:T(1,128)} %constant.157.tw2_ref, f32[2,32,32,128]{3,2,1,0:T(8,128)} %pad_maximum_fusion.1.back_ref, ...), custom_call_target="tpu_custom_call" | custom-call | tf_op jit(solution)/shard_map/pallas_call | solution.py:207
  50.0 3.6 %all-to-all-start.2 = ((f32[8,2,1,32,512]{4,3,2,1,0:T(8,128)}), f32[8,2,1,32,512]{4,3,2,1,0:T(8,128)S(1)}, u32[]{:S(2)}, u32[]{:S(2)}) async-start(f32[8,2,1,32,512]{4,3,2,1,0:T(8,128)} %shard_map.140), calls=%async_computation.2 | async-start | bytes 2097152 | tf_op jit(solution)/shard_map/all_to_all | solution.py:273
  53.5 1.6 %collective-permute-start = (f32[65536]{0:T(1024)S(1)}, f32[65536]{0:T(1024)S(1)}, u32[]{:S(2)}, u32[]{:S(2)}) collective-permute-start(f32[65536]{0:T(1024)S(1)} %bitcast.69), channel_id=1, source_target_pairs={{0,1},{1,0},{2,3},{3,2},{4,5},{5,4},{6,7},{7,6},{8,9},{9,8},{10,11... | collective-permute-start | bytes 786440 | tf_op jit(solution)/shard_map/ppermute | solution.py:341
  55.2 7.0 %collective-permute-done = f32[65536]{0:T(1024)S(1)} collective-permute-done((f32[65536]{0:T(1024)S(1)}, f32[65536]{0:T(1024)S(1)}, u32[]{:S(2)}, u32[]{:S(2)}) %collective-permute-start) | collective-permute-done | bytes 262176 | tf_op jit(solution)/shard_map/ppermute | solution.py:341
  62.2 2.7 %collective-permute-start.1 = (f32[65536]{0:T(1024)S(1)}, f32[65536]{0:T(1024)S(1)}, u32[]{:S(2)}, u32[]{:S(2)}) collective-permute-start(f32[65536]{0:T(1024)S(1)} %add.188), channel_id=1, source_target_pairs={{0,2},{1,3},{2,0},{3,1},{4,6},{5,7},{6,4},{7,5},{8,10},{9,11},{10,... | collective-permute-start | bytes 786440 | tf_op jit(solution)/shard_map/ppermute | solution.py:341
  64.9 4.0 %all-to-all-done.2 = f32[8,2,1,32,512]{4,3,2,1,0:T(8,128)S(1)} async-done(((f32[8,2,1,32,512]{4,3,2,1,0:T(8,128)}), f32[8,2,1,32,512]{4,3,2,1,0:T(8,128)S(1)}, u32[]{:S(2)}, u32[]{:S(2)}) %all-to-all-start.2) | async-done | bytes 1048608 | tf_op jit(solution)/shard_map/all_to_all | solution.py:273
  69.0 0.9 %copy-done.8 = f32[2,8,16,2,256]{4,2,3,1,0:T(8,128)S(1)} copy-done((f32[2,8,16,2,256]{4,2,3,1,0:T(8,128)S(1)}, f32[2,8,16,2,256]{4,2,3,1,0:T(8,128)}, u32[]{:S(2)}) %copy-start.8) | copy-done | bytes 524312
  69.9 0.6 convolution_bitcast_fusion.1
  70.5 0.9 copy.33
  71.4 3.7 %all-to-all-start.3 = ((f32[8,2,16,512]{3,2,1,0:T(8,128)}), f32[8,2,16,512]{3,2,1,0:T(8,128)S(1)}, u32[]{:S(2)}, u32[]{:S(2)}) async-start(f32[8,2,16,512]{3,2,1,0:T(8,128)} %copy.33), calls=%async_computation.3 | async-start | bytes 1048576 | tf_op jit(solution)/shard_map/all_to_all | solution.py:273
  75.2 0.6 fusion.22
  77.1 0.7 add.189
  77.8 6.8 %all-to-all-done.3 = f32[8,2,16,512]{3,2,1,0:T(8,128)S(1)} async-done(((f32[8,2,16,512]{3,2,1,0:T(8,128)}), f32[8,2,16,512]{3,2,1,0:T(8,128)S(1)}, u32[]{:S(2)}, u32[]{:S(2)}) %all-to-all-start.3) | async-done | bytes 524320 | tf_op jit(solution)/shard_map/all_to_all | solution.py:273
  85.5 2.2 %add_multiply_fusion = (f32[1,65536]{1,0:T(1,128)}, f32[1,65536]{1,0:T(1,128)}) fusion(f32[1,65536]{1,0:T(1,128)S(1)} %bitcast.76, f32[1,65536]{1,0:T(1,128)S(1)} %bitcast.63, f32[1,65536]{1,0:T(1,128)S(1)} %copy-done.1, f32[1,65536]{1,0:T(1,128)S(1)} %bitcast.73, f32[]{:T(128)} %bitcast.31, f32[]{:T(128)} %bitcast.26, s32[]{:T(128)} %mul.382, ...), kind=kLoop, calls=%fused_computation.19 | loop fusion | flops 1179648 | bytes 2359308 | tf_op jit(solution)/shard_map/mul | solution.py:357
  (41 shorter events, 2.9 us)
Async XLA Ops:
  3.1 5.3 %copy-start.1 = (f32[1,65536]{1,0:T(1,128)S(1)}, f32[1,65536]{1,0:T(1,128)}, u32[]{:S(2)}) copy-start(f32[1,65536]{1,0:T(1,128)} %param.13) | copy-start | bytes 786436
  3.1 16.5 %all-to-all-start = ((f32[8,40,512]{2,1,0:T(8,128)}), f32[8,40,512]{2,1,0:T(8,128)S(1)}, u32[]{:S(2)}, u32[]{:S(2)}) async-start(f32[8,40,512]{2,1,0:T(8,128)} %shard_map.139), calls=%async_computation | async-start | bytes 1310720 | tf_op jit(solution)/shard_map/all_to_all | solution.py:273
  9.0 0.7 copy-start.7
  9.8 0.9 %copy-start.5 = (f32[256,128]{1,0:T(8,128)S(1)}, f32[256,128]{1,0:T(8,128)}, u32[]{:S(2)}) copy-start(f32[256,128]{1,0:T(8,128)} %constant.141.clone) | copy-start | bytes 393220
  9.8 1.0 %copy-start.6 = (f32[256,128]{1,0:T(8,128)S(1)}, f32[256,128]{1,0:T(8,128)}, u32[]{:S(2)}) copy-start(f32[256,128]{1,0:T(8,128)} %constant.140.clone) | copy-start | bytes 393220
  19.6 1.0 %copy-start.4 = (f32[2,8,32,2,128]{4,2,3,0,1:T(8,128)S(1)}, f32[2,8,32,2,128]{4,2,3,0,1:T(8,128)}, u32[]{:S(2)}) copy-start(f32[2,8,32,2,128]{4,2,3,0,1:T(8,128)} %constant.167) | copy-start | bytes 1572868
  22.5 4.3 %copy-start.2 = (f32[65536]{0:T(1024)S(1)}, f32[65536]{0:T(1024)}, u32[]{:S(2)}) copy-start(f32[65536]{0:T(1024)} %param.14) | copy-start | bytes 786436
  22.5 4.4 %copy-start.3 = (f32[1,65536]{1,0:T(1,128)S(1)}, f32[1,65536]{1,0:T(1,128)}, u32[]{:S(2)}) copy-start(f32[1,65536]{1,0:T(1,128)} %param.12) | copy-start | bytes 786436
  22.5 19.0 %all-to-all-start.1 = ((f32[8,2,1,32,512]{4,3,2,1,0:T(8,128)}), f32[8,2,1,32,512]{4,3,2,1,0:T(8,128)S(1)}, u32[]{:S(2)}, u32[]{:S(2)}) async-start(f32[8,2,1,32,512]{4,3,2,1,0:T(8,128)} %pad_maximum_fusion), calls=%async_computation.1 | async-start | bytes 2097152 | tf_op jit(solution)/shard_map/all_to_all | solution.py:273
  41.5 1.0 %copy-start = (f32[8,2,1,32,512]{4,3,2,1,0:T(8,128)}, f32[8,2,1,32,512]{4,3,2,1,0:T(8,128)S(1)}, u32[]{:S(2)}) copy-start(f32[8,2,1,32,512]{4,3,2,1,0:T(8,128)S(1)} %all-to-all-done.1.x_ref) | copy-start | bytes 3145732
  50.0 18.9 %all-to-all-start.2 = ((f32[8,2,1,32,512]{4,3,2,1,0:T(8,128)}), f32[8,2,1,32,512]{4,3,2,1,0:T(8,128)S(1)}, u32[]{:S(2)}, u32[]{:S(2)}) async-start(f32[8,2,1,32,512]{4,3,2,1,0:T(8,128)} %shard_map.140), calls=%async_computation.2 | async-start | bytes 2097152 | tf_op jit(solution)/shard_map/all_to_all | solution.py:273
  53.5 8.6 %collective-permute-start = (f32[65536]{0:T(1024)S(1)}, f32[65536]{0:T(1024)S(1)}, u32[]{:S(2)}, u32[]{:S(2)}) collective-permute-start(f32[65536]{0:T(1024)S(1)} %bitcast.69), channel_id=1, source_target_pairs={{0,1},{1,0},{2,3},{3,2},{4,5},{5,4},{6,7},{7,6},{8,9},{9,8},{10,11... | collective-permute-start | bytes 786440 | tf_op jit(solution)/shard_map/ppermute | solution.py:341
  62.2 14.9 %collective-permute-start.1 = (f32[65536]{0:T(1024)S(1)}, f32[65536]{0:T(1024)S(1)}, u32[]{:S(2)}, u32[]{:S(2)}) collective-permute-start(f32[65536]{0:T(1024)S(1)} %add.188), channel_id=1, source_target_pairs={{0,2},{1,3},{2,0},{3,1},{4,6},{5,7},{6,4},{7,5},{8,10},{9,11},{10,... | collective-permute-start | bytes 786440 | tf_op jit(solution)/shard_map/ppermute | solution.py:341
  68.9 1.0 %copy-start.8 = (f32[2,8,16,2,256]{4,2,3,1,0:T(8,128)S(1)}, f32[2,8,16,2,256]{4,2,3,1,0:T(8,128)}, u32[]{:S(2)}) copy-start(f32[2,8,16,2,256]{4,2,3,1,0:T(8,128)} %constant.166) | copy-start | bytes 1572868
  71.4 13.2 %all-to-all-start.3 = ((f32[8,2,16,512]{3,2,1,0:T(8,128)}), f32[8,2,16,512]{3,2,1,0:T(8,128)S(1)}, u32[]{:S(2)}, u32[]{:S(2)}) async-start(f32[8,2,16,512]{3,2,1,0:T(8,128)} %copy.33), calls=%async_computation.3 | async-start | bytes 1048576 | tf_op jit(solution)/shard_map/all_to_all | solution.py:273

commit v15 on v13

--- a/solution.py
+++ b/solution.py
@@ -351,14 +351,16 @@
     birth = gathered[:scen_dev]
     corr = gathered[scen_dev:]
     inflow = jnp.concatenate([incoming, flux[:, :-1]], axis=1)
-    tendency = 0.5 * beta * birth - beta * first[:, None] * weighted - flux + inflow
-    adjoint = mass[None, :] * (
-        beta * corr
-        - beta * first[:, None] * cotangent
+    rest_t = -beta * first[:, None] * weighted - flux + inflow
+    rest_a = (
+        -beta * first[:, None] * cotangent
         - beta * cross[:, None]
         - rate[None, :] * cotangent
         + rate[None, :] * following
     )
+    rest_t, rest_a = lax.optimization_barrier((rest_t, rest_a))
+    tendency = 0.5 * beta * birth + rest_t
+    adjoint = mass[None, :] * (beta * corr + rest_a)
     return (tendency, adjoint, rate_gradient)
 
 

time: 88.3 us -> 95.2 us (1.078)
  waiting for transfers between devices: 36.7 us -> 41.2 us
  other arithmetic: 8.4 us -> 10.5 us
    ppermute x2, waiting for transfers between devices: 6.98 us -> 12.5 us  [shards(): rate_gradient = rate_gradient + lax.ppermute(rate_gradient, 'scen', pairs)]
    add x0 -> x2, other arithmetic: none -> 3.39 us  [the longest x1 2.42 us: shards(): -beta * first[:, None] * cotangent - beta * cross[:, None]]
    mul x3, other arithmetic: 3.02 us -> 1.7 us  [the longest x2 1.22 us: shards(): adjoint = mass[None, :] * (beta * corr + rest_a)]
    all_to_all x4, waiting for transfers between devices: 29.7 us -> 28.7 us  [exchange(): return lax.all_to_all(value, 'mass', 0, 0, tiled=True)]
    unnamed x20 -> x22, local copies, waits for them, and re-layouts: 4.17 us -> 3.87 us
  transfers between devices with their start and end apart: 6 -> 6, of which waited for: 5 -> 4; matrix products, arithmetic and copies ran while one was open for 10% -> 11% of each run, Pallas kernels for 0% -> 0%
where the time goes in v15:
time: 95.2 us; the launch traced here: 94.6 us
  waiting for transfers between devices  41.2 us (43%)
  starting transfers between devices  20.2 us (21%)
  other arithmetic  10.5 us (11%)
  Pallas kernels  9.9 us (10%)
  local copies, waits for them, and re-layouts  8.7 us (9%)
  between operations  2.91 us (3%)
  matrix products  1.2 us (1%)
    all_to_all x4, waiting for transfers between devices, exchange(): return lax.all_to_all(value, 'mass', 0, 0, tiled=True)  28.7 us
    all_to_all x4, starting transfers between devices, exchange(): return lax.all_to_all(value, 'mass', 0, 0, tiled=True)  15.9 us
    ppermute x2, waiting for transfers between devices, shards(): rate_gradient = rate_gradient + lax.ppermute(rate_gradient, 'scen', pairs)  12.5 us
    pallas_call x1, Pallas kernels, column_stage(): pl.pallas_call(column_kernel, out_shape=jax.ShapeDtypeStruct(received.sha...  7.48 us
    ppermute x2, starting transfers between devices, shards(): rate_gradient = rate_gradient + lax.ppermute(rate_gradient, 'scen', pairs)  4.32 us
    unnamed x22, local copies, waits for them, and re-layouts  3.87 us
    pallas_call x1, Pallas kernels, prologue(): pl.pallas_call(functools.partial(prologue_kernel, nbin), out_shape=jax.Sh...  2.42 us
    add x1, other arithmetic, shards(): -beta * first[:, None] * cotangent - beta * cross[:, None]  2.42 us
  transfers between devices with their start and end apart: 6, of which 4 were waited for; matrix products, arithmetic and copies ran while one was open for 11% of the time, Pallas kernels for 0%

profile of v15, /device:TPU:0, one launch (start us, length us, event | category | flops | bytes accessed | tf_op | source)
XLA Modules:
  0.0 94.6 jit_solution(2709784810373178750)
XLA Ops:
  0.6 2.4 %shard_map.139 = f32[8,40,512]{2,1,0:T(8,128)} custom-call(s32[1]{0:T(128)} %bitcast.1.base_ref, f32[1,512,128]{2,1,0:T(8,128)} %bitcast.72, f32[1,512,128]{2,1,0:T(8,128)} %bitcast.70, f32[512,128]{1,0:T(8,128)} %bitcast.67), custom_call_target="tpu_custom_call" | custom-call | tf_op jit(solution)/shard_map/pallas_call | solution.py:263
  3.1 5.3 %all-to-all-start = ((f32[8,40,512]{2,1,0:T(8,128)}), f32[8,40,512]{2,1,0:T(8,128)S(1)}, u32[]{:S(2)}, u32[]{:S(2)}) async-start(f32[8,40,512]{2,1,0:T(8,128)} %shard_map.139), calls=%async_computation | async-start | bytes 1310720 | tf_op jit(solution)/shard_map/all_to_all | solution.py:273
  8.4 0.6 slice.50
  9.5 0.5 copy-done.1
  10.0 0.5 fusion.21
  10.9 0.7 add_negate_fusion
  11.6 1.0 %neg.24 = f32[1,1,256,512]{3,2,0,1:T(8,128)} reshape(f32[256,4,128]{2,1,0:T(4,128)S(1)} %get-tuple-element.17) | data formatting | bytes 1048576 | tf_op jit(solution)/shard_map/neg | solution.py:328
  13.0 0.6 add_convert_fusion.flag_ref
  14.3 1.1 %pad_maximum_fusion.back_ref = f32[2,32,32,128]{3,2,1,0:T(8,128)} fusion(f32[1,32,32,128]{3,2,1,0:T(8,128)S(1)} %get-tuple-element.23, f32[1,32,32,128]{3,2,1,0:T(8,128)S(1)} %get-tuple-element.22), kind=kLoop, calls=%fused_computation.2 | loop fusion | flops 262144 | bytes 2097152 | tf_op jit(solution)/shard_map/stack | solution.py:201
  15.4 4.2 %all-to-all-done = f32[8,40,512]{2,1,0:T(8,128)S(1)} async-done(((f32[8,40,512]{2,1,0:T(8,128)}), f32[8,40,512]{2,1,0:T(8,128)S(1)}, u32[]{:S(2)}, u32[]{:S(2)}) %all-to-all-start) | async-done | bytes 655392 | tf_op jit(solution)/shard_map/all_to_all | solution.py:273
  19.7 0.6 slice.52
  20.2 0.7 fusion.22
  20.9 0.6 convolution_bitcast_fusion
  21.5 0.4 copy-done.4
  22.2 1.1 %maximum_bitcast_fusion = f32[8,2,1,32,512]{4,3,2,1,0:T(8,128)} fusion(f32[1,1,8,32,512]{4,3,1,0,2:T(8,128)S(1)} %bitcast.77, f32[1,1,8,32,512]{4,3,1,0,2:T(8,128)S(1)} %bitcast.76), kind=kLoop, calls=%fused_computation.1 | loop fusion | flops 262144 | bytes 2097152 | tf_op jit(solution)/shard_map/transpose | solution.py:329
  23.3 3.6 %all-to-all-start.1 = ((f32[8,2,1,32,512]{4,3,2,1,0:T(8,128)}), f32[8,2,1,32,512]{4,3,2,1,0:T(8,128)S(1)}, u32[]{:S(2)}, u32[]{:S(2)}) async-start(f32[8,2,1,32,512]{4,3,2,1,0:T(8,128)} %maximum_bitcast_fusion), calls=%async_computation.1 | async-start | bytes 2097152 | tf_op jit(solution)/shard_map/all_to_all | solution.py:273
  28.9 2.4 %subtract_add_fusion = (f32[1,65536]{1,0:T(1,128)S(1)}, f32[1,65536]{1,0:T(1,128)S(1)}, f32[1,65536]{1,0:T(1,128)S(1)}) fusion(f32[1,65536]{1,0:T(1,128)S(1)} %bitcast.82, f32[1,65536]{1,0:T(1,128)S(1)} %bitcast.69, f32[1,65536]{1,0:T(1,128)S(1)} %copy-done.2, f32[]{:T(128)} %bitcast.36, f32[]{:T(128)} %bitcast.31, f32[1,1]{1,0:T(1,128)} %bitcast.19, ...), kind=kLoop, calls=%fused_computation.20 | loop fusion | flops 1179648 | bytes 2359308 | tf_op jit(solution)/shard_map/add | solution.py:356
  31.3 10.9 %all-to-all-done.1.x_ref = f32[8,2,1,32,512]{4,3,2,1,0:T(8,128)S(1)} async-done(((f32[8,2,1,32,512]{4,3,2,1,0:T(8,128)}), f32[8,2,1,32,512]{4,3,2,1,0:T(8,128)S(1)}, u32[]{:S(2)}, u32[]{:S(2)}) %all-to-all-start.1) | async-done | bytes 1048608 | tf_op jit(solution)/shard_map/all_to_all | solution.py:273
  42.2 1.0 %copy-done = f32[8,2,1,32,512]{4,3,2,1,0:T(8,128)} copy-done((f32[8,2,1,32,512]{4,3,2,1,0:T(8,128)}, f32[8,2,1,32,512]{4,3,2,1,0:T(8,128)S(1)}, u32[]{:S(2)}) %copy-start) | copy-done | bytes 1048600
  43.1 7.5 %shard_map.140 = f32[8,2,1,32,512]{4,3,2,1,0:T(8,128)} custom-call(f32[8,2,1,32,512]{4,3,2,1,0:T(8,128)} %copy-done, f32[2,32,1,128]{3,2,1,0:T(1,128)} %constant.159.phi_ref, f32[2,32,1,128]{3,2,1,0:T(1,128)} %constant.160.tw1_ref, f32[2,4,1,128]{3,2,1,0:T(1,128)} %constant.161.tw2_ref, f32[2,32,32,128]{3,2,1,0:T(8,128)} %pad_maximum_fusion.back_ref, ...), custom_call_target="tpu_custom_call" | custom-call | tf_op jit(solution)/shard_map/pallas_call | solution.py:207
  50.6 3.6 %all-to-all-start.2 = ((f32[8,2,1,32,512]{4,3,2,1,0:T(8,128)}), f32[8,2,1,32,512]{4,3,2,1,0:T(8,128)S(1)}, u32[]{:S(2)}, u32[]{:S(2)}) async-start(f32[8,2,1,32,512]{4,3,2,1,0:T(8,128)} %shard_map.140), calls=%async_computation.2 | async-start | bytes 2097152 | tf_op jit(solution)/shard_map/all_to_all | solution.py:273
  54.2 1.6 %collective-permute-start = (f32[65536]{0:T(1024)S(1)}, f32[65536]{0:T(1024)S(1)}, u32[]{:S(2)}, u32[]{:S(2)}) collective-permute-start(f32[65536]{0:T(1024)S(1)} %bitcast.78), channel_id=1, source_target_pairs={{0,1},{1,0},{2,3},{3,2},{4,5},{5,4},{6,7},{7,6},{8,9},{9,8},{10,11... | collective-permute-start | bytes 786440 | tf_op jit(solution)/shard_map/ppermute | solution.py:339
  55.8 13.7 %all-to-all-done.2 = f32[8,2,1,32,512]{4,3,2,1,0:T(8,128)S(1)} async-done(((f32[8,2,1,32,512]{4,3,2,1,0:T(8,128)}), f32[8,2,1,32,512]{4,3,2,1,0:T(8,128)S(1)}, u32[]{:S(2)}, u32[]{:S(2)}) %all-to-all-start.2) | async-done | bytes 1048608 | tf_op jit(solution)/shard_map/all_to_all | solution.py:273
  69.6 0.9 copy-done.5
  70.6 0.6 fusion.23
  71.2 0.9 copy.44
  72.0 3.5 %all-to-all-start.3 = ((f32[8,2,16,512]{3,2,1,0:T(8,128)}), f32[8,2,16,512]{3,2,1,0:T(8,128)S(1)}, u32[]{:S(2)}, u32[]{:S(2)}) async-start(f32[8,2,16,512]{3,2,1,0:T(8,128)} %bitcast.60), calls=%async_computation.3 | async-start | bytes 1048576 | tf_op jit(solution)/shard_map/all_to_all | solution.py:273
  75.6 2.7 %collective-permute-start.1 = (f32[65536]{0:T(1024)S(1)}, f32[65536]{0:T(1024)S(1)}, u32[]{:S(2)}, u32[]{:S(2)}) collective-permute-start(f32[65536]{0:T(1024)S(1)} %add.196), channel_id=1, source_target_pairs={{0,2},{1,3},{2,0},{3,1},{4,6},{5,7},{6,4},{7,5},{8,10},{9,11},{10,... | collective-permute-start | bytes 786440 | tf_op jit(solution)/shard_map/ppermute | solution.py:339
  78.3 12.5 %collective-permute-done.1 = f32[65536]{0:T(1024)S(1)} collective-permute-done((f32[65536]{0:T(1024)S(1)}, f32[65536]{0:T(1024)S(1)}, u32[]{:S(2)}, u32[]{:S(2)}) %collective-permute-start.1) | collective-permute-done | bytes 262176 | tf_op jit(solution)/shard_map/ppermute | solution.py:339
  90.8 0.7 add.197
  92.5 1.2 %add_multiply_fusion = f32[1,65536]{1,0:T(1,128)} fusion(f32[1,65536]{1,0:T(1,128)S(1)} %bitcast.85, f32[1,65536]{1,0:T(1,128)S(1)} %get-tuple-element.9, s32[]{:T(128)} %mul.382), kind=kLoop, calls=%fused_computation.19 | loop fusion | flops 393216 | bytes 786436 | tf_op jit(solution)/shard_map/mul | solution.py:363
  93.7 1.0 %add.194 = f32[1,65536]{1,0:T(1,128)} add(f32[1,65536]{1,0:T(1,128)S(1)} %bitcast.80, f32[1,65536]{1,0:T(1,128)S(1)} %get-tuple-element.8) | non-fusion elementwise | flops 65536 | bytes 786432 | tf_op jit(solution)/shard_map/add | solution.py:362
  (45 shorter events, 3.5 us)
Async XLA Ops:
  3.1 5.3 %copy-start.2 = (f32[1,65536]{1,0:T(1,128)S(1)}, f32[1,65536]{1,0:T(1,128)}, u32[]{:S(2)}) copy-start(f32[1,65536]{1,0:T(1,128)} %param.13) | copy-start | bytes 786436
  3.1 16.5 %all-to-all-start = ((f32[8,40,512]{2,1,0:T(8,128)}), f32[8,40,512]{2,1,0:T(8,128)S(1)}, u32[]{:S(2)}, u32[]{:S(2)}) async-start(f32[8,40,512]{2,1,0:T(8,128)} %shard_map.139), calls=%async_computation | async-start | bytes 1310720 | tf_op jit(solution)/shard_map/all_to_all | solution.py:273
  8.4 0.7 copy-start.9
  8.4 1.1 %copy-start.3 = (f32[1,65536]{1,0:T(1,128)S(1)}, f32[1,65536]{1,0:T(1,128)}, u32[]{:S(2)}) copy-start(f32[1,65536]{1,0:T(1,128)} %param.12) | copy-start | bytes 786436
  9.0 1.0 %copy-start.1 = (f32[65536]{0:T(1024)S(1)}, f32[65536]{0:T(1024)}, u32[]{:S(2)}) copy-start(f32[65536]{0:T(1024)} %param.14) | copy-start | bytes 786436
  10.0 0.9 copy-start.7
  10.0 1.0 %copy-start.8 = (f32[256,128]{1,0:T(8,128)S(1)}, f32[256,128]{1,0:T(8,128)}, u32[]{:S(2)}) copy-start(f32[256,128]{1,0:T(8,128)} %constant.142.clone) | copy-start | bytes 393220
  19.6 1.4 %copy-start.6 = (f32[2,256,2,128]{3,1,2,0:T(8,128)S(1)}, f32[2,256,2,128]{3,1,2,0:T(8,128)}, u32[]{:S(2)}) copy-start(f32[2,256,2,128]{3,1,2,0:T(8,128)} %constant.158) | copy-start | bytes 1572868
  20.9 1.0 %copy-start.4 = (f32[1,1,256,512]{3,2,0,1:T(8,128)S(1)}, f32[1,1,256,512]{3,2,0,1:T(8,128)}, u32[]{:S(2)}) copy-start(f32[1,1,256,512]{3,2,0,1:T(8,128)} %neg.24) | copy-start | bytes 1572868
  23.3 18.9 %all-to-all-start.1 = ((f32[8,2,1,32,512]{4,3,2,1,0:T(8,128)}), f32[8,2,1,32,512]{4,3,2,1,0:T(8,128)S(1)}, u32[]{:S(2)}, u32[]{:S(2)}) async-start(f32[8,2,1,32,512]{4,3,2,1,0:T(8,128)} %maximum_bitcast_fusion), calls=%async_computation.1 | async-start | bytes 2097152 | tf_op jit(solution)/shard_map/all_to_all | solution.py:273
  42.2 1.0 %copy-start = (f32[8,2,1,32,512]{4,3,2,1,0:T(8,128)}, f32[8,2,1,32,512]{4,3,2,1,0:T(8,128)S(1)}, u32[]{:S(2)}) copy-start(f32[8,2,1,32,512]{4,3,2,1,0:T(8,128)S(1)} %all-to-all-done.1.x_ref) | copy-start | bytes 3145732
  50.6 18.9 %all-to-all-start.2 = ((f32[8,2,1,32,512]{4,3,2,1,0:T(8,128)}), f32[8,2,1,32,512]{4,3,2,1,0:T(8,128)S(1)}, u32[]{:S(2)}, u32[]{:S(2)}) async-start(f32[8,2,1,32,512]{4,3,2,1,0:T(8,128)} %shard_map.140), calls=%async_computation.2 | async-start | bytes 2097152 | tf_op jit(solution)/shard_map/all_to_all | solution.py:273
  54.2 21.4 %collective-permute-start = (f32[65536]{0:T(1024)S(1)}, f32[65536]{0:T(1024)S(1)}, u32[]{:S(2)}, u32[]{:S(2)}) collective-permute-start(f32[65536]{0:T(1024)S(1)} %bitcast.78), channel_id=1, source_target_pairs={{0,1},{1,0},{2,3},{3,2},{4,5},{5,4},{6,7},{7,6},{8,9},{9,8},{10,11... | collective-permute-start | bytes 786440 | tf_op jit(solution)/shard_map/ppermute | solution.py:339
  69.5 1.0 %copy-start.5 = (f32[2,128,2,256]{3,1,2,0:T(8,128)S(1)}, f32[2,128,2,256]{3,1,2,0:T(8,128)}, u32[]{:S(2)}) copy-start(f32[2,128,2,256]{3,1,2,0:T(8,128)} %constant.172) | copy-start | bytes 1572868
  72.0 19.5 %all-to-all-start.3 = ((f32[8,2,16,512]{3,2,1,0:T(8,128)}), f32[8,2,16,512]{3,2,1,0:T(8,128)S(1)}, u32[]{:S(2)}, u32[]{:S(2)}) async-start(f32[8,2,16,512]{3,2,1,0:T(8,128)} %bitcast.60), calls=%async_computation.3 | async-start | bytes 1048576 | tf_op jit(solution)/shard_map/all_to_all | solution.py:273
  75.6 15.2 %collective-permute-start.1 = (f32[65536]{0:T(1024)S(1)}, f32[65536]{0:T(1024)S(1)}, u32[]{:S(2)}, u32[]{:S(2)}) collective-permute-start(f32[65536]{0:T(1024)S(1)} %add.196), channel_id=1, source_target_pairs={{0,2},{1,3},{2,0},{3,1},{4,6},{5,7},{6,4},{7,5},{8,10},{9,11},{10,... | collective-permute-start | bytes 786440 | tf_op jit(solution)/shard_map/ppermute | solution.py:339
